TPU v7x, 256 devices: a whole 4x4x8 slice. The times are simulated.
256 devices in a mesh: lat: 8 (over z), lev: 32 (over x, y, core).
Axes of the slice: x: 4, y: 4, z: 8, core: 2. Of those that a mesh axis runs over, the one named last changes fastest.
Arguments:
- spec_in: bfloat16 [32, 640, 1281], P('lev', 'lat'), may hold values from -6 to 6
- legendre: bfloat16 [640, 1280, 1281], P('lat', 'lev'), may hold values from -0.15625 to 0.15625
- gauss_weights: float32 [1280], P('lev'), may hold values from 0.1 to 1
- row_points: int32 [2, 1280], P(None, 'lev'), may hold values from 4 to 5120
Outputs:
- spec_out: bfloat16 [32, 640, 1281], P('lev', 'lat')
All inputs are finite; a program needn't handle non-finite values.
Results may differ from a plain program's by a relative error of at most 0.02.
Values may be sent and summed in bfloat16 or wider, within the bound.
No kernel may reach another device: no remote copies, remote signals or barrier semaphores. Data moves between devices by JAX's collectives and lax.ppermute only.
A program may use at most 128 MiB of HBM per device.

v0:
```python
import math

import jax
import jax.numpy as jnp
from jax import lax
from jax.sharding import PartitionSpec as P

NLON = 5120


SLOT_CODES = (0, 0, 1, 1)
PARITY_CODES = (0, 1, 0, 1)


def pair_masks(first_pair, pair_count, packed):
    pair_ids = first_pair + jnp.arange(pair_count, dtype=jnp.int32)
    positions = jnp.arange(packed, dtype=jnp.int32)
    boundary = packed - 1 - pair_ids
    in_second = (positions[None, :] >= boundary[:, None]).astype(jnp.int32)
    degree = positions[None, :] - in_second * boundary[:, None]
    parity = degree % 2
    slot_codes = jnp.array(SLOT_CODES, dtype=jnp.int32)
    parity_codes = jnp.array(PARITY_CODES, dtype=jnp.int32)
    return (in_second[:, :, None] == slot_codes) & (parity[:, :, None] == parity_codes)


def wave_tables(total_pairs, truncation):
    pair_ids = jnp.arange(total_pairs, dtype=jnp.int32)
    wavenumbers = jnp.stack([pair_ids, truncation - pair_ids], axis=1)
    longitudes = jnp.arange(NLON, dtype=jnp.int32)
    phases = wavenumbers[:, :, None] * longitudes[None, None, :] % NLON
    angles = phases.astype(jnp.float32) * (2.0 * math.pi / NLON)
    return (jnp.cos(angles).astype(jnp.bfloat16), jnp.sin(angles).astype(jnp.bfloat16), wavenumbers)


def fourier_work(spectrum, row_counts, cosines, sines, wavenumbers, truncation):
    kept_mask = (2 * wavenumbers[:, None, :] < row_counts[None, :, None]).astype(jnp.float32)
    masked = spectrum * kept_mask[..., None].astype(jnp.bfloat16)
    half_channels = spectrum.shape[-1] // 2
    levels = half_channels // 2
    real_part = masked[..., :half_channels]
    imag_part = masked[..., half_channels:]
    grid_values = jnp.einsum(
        "plsf,psk->lfk", real_part, cosines, preferred_element_type=jnp.float32
    )
    grid_values = (
        grid_values
        - jnp.einsum("plsf,psk->lfk", imag_part, sines, preferred_element_type=jnp.float32)
    ) * (1.0 / math.sqrt(truncation + 1))
    vortex = grid_values[:, :levels]
    divergence = grid_values[:, levels:]
    products = jnp.concatenate(
        [vortex * divergence, 0.5 * (vortex * vortex - divergence * divergence)], axis=1
    ).astype(jnp.bfloat16)
    scale_back = 4.0 / math.sqrt(NLON)
    real_out = (
        jnp.einsum("lfk,psk->plsf", products, cosines, preferred_element_type=jnp.float32)
        * scale_back
    )
    imag_out = (
        -jnp.einsum("lfk,psk->plsf", products, sines, preferred_element_type=jnp.float32)
        * scale_back
    )
    return (jnp.concatenate([real_out, imag_out], axis=-1) * kept_mask[..., None]).astype(
        jnp.bfloat16
    )


def local(spec_in, legendre, gauss_weights, row_points):
    pair_count, lat_count, packed = legendre.shape
    truncation = packed - 2
    groups = lax.axis_size("lat")
    local_channels = spec_in.shape[0]
    channels = local_channels * lax.axis_size("lev")
    tile_size = math.gcd(pair_count, 8)
    tile_count = pair_count // tile_size
    first_pair = lax.axis_index("lat") * pair_count
    selector = pair_masks(first_pair, pair_count, packed)
    select_half = selector.astype(jnp.bfloat16).reshape(tile_count, tile_size, packed, 4)
    select_full = selector.astype(jnp.float32).reshape(tile_count, tile_size, packed, 4)
    legendre_tiles = legendre.reshape(tile_count, tile_size, lat_count, packed)
    gathered = lax.all_gather(spec_in, "lev", axis=0, tiled=True)
    piece_width = gathered.shape[0]
    spectral = jnp.moveaxis(gathered.reshape(piece_width, tile_count, tile_size, packed), 1, 0)

    def inverse_tile(inputs):
        legendre_tile, spectral_tile, select_tile = inputs
        spread = spectral_tile[None] * jnp.moveaxis(select_tile, 2, 0)[:, None]
        return jnp.einsum(
            "pjq,xcpq->pjxc", legendre_tile, spread, preferred_element_type=jnp.float32
        )

    tile_sums = lax.map(inverse_tile, (legendre_tiles, spectral, select_half))
    legendre_sums = tile_sums.reshape(pair_count, lat_count, 4, piece_width)
    even_part = legendre_sums[:, :, 0::2]
    odd_part = legendre_sums[:, :, 1::2]
    fourier = jnp.concatenate([even_part + odd_part, even_part - odd_part], axis=1).astype(
        jnp.bfloat16
    )
    cosines, sines, wavenumbers = wave_tables(pair_count * groups, truncation)
    local_rows = row_points.reshape(1, 2 * lat_count)
    band_lats = 2 * lat_count // groups
    lat_rows = lax.all_to_all(fourier, "lat", split_axis=1, concat_axis=0, tiled=True)
    my_rows = lax.dynamic_slice_in_dim(local_rows[0], lax.axis_index("lat") * band_lats, band_lats)
    answered = fourier_work(lat_rows, my_rows, cosines, sines, wavenumbers, truncation)
    answered = answered.reshape(groups, pair_count, band_lats, 2, channels)
    returned = lax.all_to_all(answered, "lat", split_axis=0, concat_axis=0, tiled=True)
    back = jnp.moveaxis(returned, 0, 1).reshape(pair_count, 2 * lat_count, 2, channels)
    north_rows = back[:, :lat_count].astype(jnp.float32)
    south_rows = back[:, lat_count:].astype(jnp.float32)
    weights = gauss_weights[None, :, None, None]
    weighted = jnp.stack(
        [weights * (north_rows + south_rows), weights * (north_rows - south_rows)], axis=3
    )
    weighted = weighted.reshape(pair_count, lat_count, 4, channels).astype(jnp.bfloat16)
    part_tiles = weighted.reshape(
        tile_count, tile_size, lat_count, 4, local_channels * lax.axis_size("lev")
    )

    def direct_tile(inputs):
        legendre_tile, weighted_tile, select_tile = inputs
        full_sums = jnp.einsum(
            "pjq,pjxc->pqxc", legendre_tile, weighted_tile, preferred_element_type=jnp.float32
        )
        picked = jnp.sum(full_sums * select_tile[:, :, :, None], axis=2)
        return jnp.moveaxis(picked, 2, 0)

    picked_tiles = lax.map(direct_tile, (legendre_tiles, part_tiles, select_full))
    return lax.psum_scatter(
        jnp.moveaxis(picked_tiles, 0, 1)
        .reshape(local_channels * lax.axis_size("lev"), pair_count, packed)
        .astype(jnp.bfloat16),
        "lev",
        scatter_dimension=0,
        tiled=True,
    )


def solution(mesh):
    return jax.shard_map(
        local,
        mesh=mesh,
        in_specs=(P("lev", "lat", None), P("lat", "lev", None), P("lev"), P(None, "lev")),
        out_specs=P("lev", "lat", None),
        check_vma=False,
    )
```

profile of v0, /device:TPU:2, one launch (start us, length us, event | category | flops | bytes accessed | tf_op | source)
XLA Modules:
  0.0 796.2 jit_solution(10550959991378505809)
XLA Ops:
  7.7 2.7 fusion.74
  10.4 57.7 %all-gather.2.cloned.1.call-done = bf16[32,80,1281]{2,1,0:T(8,128)(2,1)} async-done(((bf16[1,80,1281]{2,1,0:T(8,128)(2,1)}), bf16[32,80,1281]{2,1,0:T(8,128)(2,1)}) %all-gather.2.cloned.1.call-update) | async-done | bytes 6558736 | tf_op jit(solution)/shard_map/all_gather | solution.py:82
  68.2 7.5 copy.45
  75.6 45.0 %while.20 = (s32[]{:T(128)}, f32[10,8,40,4,32]{2,4,3,1,0:T(8,128)}, bf16[10,8,40,1281]{3,2,1,0:T(8,128)(2,1)}, bf16[10,32,8,1281]{3,1,2,0:T(8,128)(2,1)}, bf16[10,8,1281,4]{2,3,1,0:T(4,128)(2,1)S(1)}, /*index=5*/s32[]{:T(128)}) while((s32[]{:T(128)}, f32[10,8,40,4,32]{2,4,3,1,0:T(8,128)}, bf16[10,8,40,1281]{3,2,1,0:T(8,128)(2,1)}, ...), condition=%wide.region_1.2_spmd, body=%wide.region_0.1_spmd.sunk | while | flops 106251264 | bytes 9575181 | solution.py:93
  75.6 1.2 dynamic-slice_bitcast_fusion.7
  77.2 2.1 fusion.110
  80.1 1.2 dynamic-slice_bitcast_fusion.7
  81.7 2.1 fusion.110
  84.6 1.2 dynamic-slice_bitcast_fusion.7
  86.2 2.1 fusion.110
  89.1 1.2 dynamic-slice_bitcast_fusion.7
  90.7 2.1 fusion.110
  93.6 1.2 dynamic-slice_bitcast_fusion.7
  95.2 2.1 fusion.110
  98.1 1.2 dynamic-slice_bitcast_fusion.7
  99.6 2.1 fusion.110
  102.6 1.2 dynamic-slice_bitcast_fusion.7
  104.2 2.1 fusion.110
  107.1 1.2 dynamic-slice_bitcast_fusion.7
  108.7 2.1 fusion.110
  111.6 1.2 dynamic-slice_bitcast_fusion.7
  113.2 2.1 fusion.110
  116.1 1.2 dynamic-slice_bitcast_fusion.7
  117.7 2.1 fusion.110
  120.6 3.4 add_convert_fusion
  124.7 3.5 copy.32
  128.2 7.0 all-to-all-start
  135.6 34.4 %all-to-all-done = bf16[80,80,2,32]{0,3,2,1:T(8,128)(2,1)S(1)} async-done(((bf16[80,80,2,32]{0,3,2,1:T(8,128)(2,1)}), bf16[80,80,2,32]{0,3,2,1:T(8,128)(2,1)S(1)}, u32[]{:S(2)}, u32[]{:S(2)}) %all-to-all-start) | async-done | bytes 819232 | tf_op jit(solution)/shard_map/all_to_all | solution.py:103
  170.0 1.0 copy.33
  171.0 1.0 all_to_all.19
  172.2 103.9 %fusion.27 = f32[10,16,5120]{2,1,0:T(8,128)S(1)} fusion(s32[640,2]{0,1:T(2,128)S(1)} %get-tuple-element.90, bf16[640,10,2,16]{0,3,2,1:T(8,128)(2,1)S(1)} %fusion.96), kind=kOutput, calls=%fused_computation.38 | convolution fusion | flops 2162688000 | bytes 3691520 | tf_op jit(solution)/shard_map/plsf,psk->lfk/dot_general | solution.py:48
  276.1 103.4 %fusion.30 = f32[10,16,5120]{2,1,0:T(8,128)S(1)} fusion(f32[10,16,5120]{2,1,0:T(8,128)S(1)} %fusion.27, s32[640,2]{0,1:T(2,128)S(1)} %get-tuple-element.90, bf16[640,10,2,16]{0,3,2,1:T(8,128)(2,1)S(1)} %fusion.98), kind=kOutput, calls=%fused_computation.39 | convolution fusion | flops 2164326400 | bytes 6968320 | tf_op jit(solution)/shard_map/plsf,psk->lfk/dot_general | solution.py:43
  380.0 1.3 maximum_bitcast_fusion.10
  381.3 103.4 %fusion.41 = f32[640,10,2,16]{0,3,1,2:T(8,128)S(1)} fusion(s32[640,2]{0,1:T(2,128)S(1)} %get-tuple-element.90, bf16[10,16,5120,1]{2,1,0,3:T(8,128)(2,1)S(1)} %maximum_bitcast_fusion.9), kind=kOutput, calls=%fused_computation.57 | convolution fusion | flops 2162892800 | bytes 2462720 | tf_op jit(solution)/shard_map/lfk,psk->plsf/dot_general | solution.py:57
  485.5 107.6 %fusion.50 = f32[640,10,2,16]{0,3,1,2:T(8,128)S(1)} fusion(s32[640,2]{0,1:T(2,128)S(1)} %get-tuple-element.90, bf16[10,16,5120,1]{2,1,0,3:T(8,128)(2,1)} %maximum_bitcast_fusion.10), kind=kOutput, calls=%fused_computation.60 | convolution fusion | flops 2163097600 | bytes 2462720 | tf_op jit(solution)/shard_map/lfk,psk->plsf/dot_general | solution.py:61
  594.0 1.6 fusion.33
  595.6 3.6 all-to-all-start.1
  599.2 34.7 %all-to-all-done.1 = bf16[8,80,10,2,32]{1,4,3,2,0:T(8,128)(2,1)S(1)} async-done(((bf16[8,80,10,2,32]{1,4,3,2,0:T(8,128)(2,1)}), bf16[8,80,10,2,32]{1,4,3,2,0:T(8,128)(2,1)S(1)}, u32[]{:S(2)}, u32[]{:S(2)}) %all-to-all-start.1) | async-done | bytes 819232 | tf_op jit(solution)/shard_map/all_to_all | solution.py:107
  634.3 1.4 pad_maximum_fusion.1
  635.7 5.9 copy.36
  641.6 46.5 %while.21 = (s32[]{:T(128)}, bf16[10,32,8,1281]{3,1,2,0:T(8,128)(2,1)}, bf16[10,8,40,1281]{3,2,1,0:T(8,128)(2,1)}, bf16[10,8,40,4,32]{2,4,3,1,0:T(8,128)(2,1)S(1)}, f32[10,8,1281,4]{2,3,1,0:T(4,128)}, /*index=5*/s32[]{:T(128)}) while((s32[]{:T(128)}, bf16[10,32,8,1281]{3,1,2,0:T(8,128)(2,1)}, bf16[10,8,40,1281]{3,2,1,0:T(8,128)(2,1)}, ...), condition=%wide.region_4.5_spmd, body=%wide.region_2.4_spmd.sunk | while | flops 107235072 | bytes 14686669 | solution.py:128
  641.7 2.1 fusion.113
  643.8 0.9 dynamic-slice_bitcast_fusion.8
  646.3 2.1 fusion.113
  648.4 0.9 dynamic-slice_bitcast_fusion.8
  651.0 2.1 fusion.113
  653.0 0.9 dynamic-slice_bitcast_fusion.8
  655.6 2.1 fusion.113
  657.7 0.9 dynamic-slice_bitcast_fusion.8
  660.3 2.1 fusion.113
  662.3 0.9 dynamic-slice_bitcast_fusion.8
  664.9 2.1 fusion.113
  667.0 0.9 dynamic-slice_bitcast_fusion.8
  669.6 2.1 fusion.113
  671.6 0.9 dynamic-slice_bitcast_fusion.8
  674.2 2.1 fusion.113
  676.3 0.9 dynamic-slice_bitcast_fusion.8
  677.9 1.0 bitcast_dynamic-update-slice_fusion.2
  678.9 2.1 fusion.113
  680.9 0.9 dynamic-slice_bitcast_fusion.8
  683.5 2.1 fusion.113
  685.6 0.9 dynamic-slice_bitcast_fusion.8
  688.1 8.4 %copy.44 = bf16[32,10,8,1281]{3,2,1,0:T(8,128)(2,1)} copy(bf16[32,10,8,1281]{3,0,2,1:T(8,128)(2,1)} %bitcast.110) | data formatting | bytes 13117440 | tf_op jit(solution)/shard_map/convert_element_type | solution.py:132
  696.6 92.5 %reduce-scatter.2.cloned.1.call-done = bf16[1,80,1281]{2,1,0:T(8,128)(2,1)} async-done(((bf16[32,80,1281]{2,1,0:T(8,128)(2,1)}), bf16[1,80,1281]{2,1,0:T(8,128)(2,1)}) %reduce-scatter.2.cloned.1.call-update) | async-done | bytes 204976 | tf_op jit(solution)/shard_map/reduce_scatter | solution.py:129
  (92 shorter events, 32.8 us)
Async XLA Ops:
  6.5 61.6 %all-gather.2.cloned.1.call-start = ((), (), s32[]{:S(2)}) async-start(), calls=%async_computation.3 | async-start | bytes 7434240 | tf_op jit(solution)/shard_map/all_gather | solution.py:82
  124.7 10.5 %copy-start.1 = (s32[2,40]{1,0:T(2,128)S(1)}, s32[2,40]{1,0:T(2,128)}, u32[]{:S(2)}) copy-start(s32[2,40]{1,0:T(2,128)} %param.13) | copy-start | bytes 964
  128.2 41.8 %all-to-all-start = ((bf16[80,80,2,32]{0,3,2,1:T(8,128)(2,1)}), bf16[80,80,2,32]{0,3,2,1:T(8,128)(2,1)S(1)}, u32[]{:S(2)}, u32[]{:S(2)}) async-start(bf16[80,80,2,32]{0,3,2,1:T(8,128)(2,1)} %copy.32), calls=%async_computation | async-start | bytes 2621440 | tf_op jit(solution)/shard_map/all_to_all | solution.py:103
  594.0 39.9 %copy-start = (f32[40]{0:T(128)S(1)}, f32[40]{0:T(128)}, u32[]{:S(2)}) copy-start(f32[40]{0:T(128)} %param.12) | copy-start | bytes 484
  595.6 38.3 %all-to-all-start.1 = ((bf16[8,80,10,2,32]{1,4,3,2,0:T(8,128)(2,1)}), bf16[8,80,10,2,32]{1,4,3,2,0:T(8,128)(2,1)S(1)}, u32[]{:S(2)}, u32[]{:S(2)}) async-start(bf16[8,80,10,2,32]{1,4,3,2,0:T(8,128)(2,1)} %fusion.33), calls=%async_computation.1 | async-start | bytes 2621440 | tf_op jit(solution)/shard_map/all_to_all | solution.py:107
  599.2 190.0 %reduce-scatter.2.cloned.1.call-start = ((), (), s32[]{:S(2)}) async-start(), calls=%async_computation.4 | async-start | bytes 7434240 | tf_op jit(solution)/shard_map/reduce_scatter | solution.py:129
Sparse Core Ops, SparseCore 0:
  10.0 58.1 all-gather.1
  696.7 92.3 reduce-scatter.1
where the time goes:
time: 804 us; the launch traced here: 796 us
  matrix products  460 us (57%)
  waiting for transfers between devices  220 us (27%)
  local copies, waits for them, and re-layouts  68.9 us (9%)
  other arithmetic  22.8 us (3%)
  between operations  13.9 us (2%)
  starting transfers between devices  10.6 us (1%)
    dot_general x1, matrix products, fourier_work(): jnp.einsum('lfk,psk->plsf', products, sines, preferred_element_type=jnp.f...  108 us
    dot_general x1, matrix products, fourier_work(): jnp.einsum('plsf,psk->lfk', imag_part, sines, preferred_element_type=jnp....  104 us
    dot_general x1, matrix products, fourier_work(): jnp.einsum('plsf,psk->lfk', real_part, cosines, preferred_element_type=jn...  103 us
    dot_general x1, matrix products, fourier_work(): jnp.einsum('lfk,psk->plsf', products, cosines, preferred_element_type=jnp...  103 us
    reduce_scatter x1, waiting for transfers between devices, local(): lax.psum_scatter(jnp.moveaxis(picked_tiles, 0, 1).reshape(local_channels...  92.5 us
    all_gather x1, waiting for transfers between devices, local(): gathered = lax.all_gather(spec_in, 'lev', axis=0, tiled=True)  57.7 us
    while x20, matrix products  41.2 us
    all_to_all x1, waiting for transfers between devices, local(): lax.all_to_all(answered, 'lat', split_axis=0, concat_axis=0, tiled=True)  34.7 us
  transfers between devices with their start and end apart: 4, of which 4 were waited for; matrix products, arithmetic and copies ran while one was open for 0% of the time, Pallas kernels for 0%

commit v1 on v0

--- a/solution.py
+++ b/solution.py
@@ -27,43 +27,61 @@
 def wave_tables(total_pairs, truncation):
     pair_ids = jnp.arange(total_pairs, dtype=jnp.int32)
     wavenumbers = jnp.stack([pair_ids, truncation - pair_ids], axis=1)
-    longitudes = jnp.arange(NLON, dtype=jnp.int32)
-    phases = wavenumbers[:, :, None] * longitudes[None, None, :] % NLON
-    angles = phases.astype(jnp.float32) * (2.0 * math.pi / NLON)
-    return (jnp.cos(angles).astype(jnp.bfloat16), jnp.sin(angles).astype(jnp.bfloat16), wavenumbers)
+    flat = wavenumbers.reshape(-1)
+    inner = 64
+    outer = NLON // inner
+    step = 2.0 * math.pi / NLON
+    coarse = (flat[:, None] * (inner * jnp.arange(outer, dtype=jnp.int32))[None, :]) % NLON
+    fine = (flat[:, None] * jnp.arange(inner, dtype=jnp.int32)[None, :]) % NLON
+    coarse_angle = coarse.astype(jnp.float32) * step
+    fine_angle = fine.astype(jnp.float32) * step
+    cos_a = jnp.cos(coarse_angle)[:, :, None]
+    sin_a = jnp.sin(coarse_angle)[:, :, None]
+    cos_b = jnp.cos(fine_angle)[:, None, :]
+    sin_b = jnp.sin(fine_angle)[:, None, :]
+    rows = flat.shape[0]
+    cosines = (cos_a * cos_b - sin_a * sin_b).reshape(rows, NLON).astype(jnp.bfloat16)
+    sines = (sin_a * cos_b + cos_a * sin_b).reshape(rows, NLON).astype(jnp.bfloat16)
+    table = lax.optimization_barrier(jnp.concatenate([cosines, sines], axis=0))
+    return table, wavenumbers
 
 
-def fourier_work(spectrum, row_counts, cosines, sines, wavenumbers, truncation):
-    kept_mask = (2 * wavenumbers[:, None, :] < row_counts[None, :, None]).astype(jnp.float32)
-    masked = spectrum * kept_mask[..., None].astype(jnp.bfloat16)
-    half_channels = spectrum.shape[-1] // 2
+def fourier_work(spectrum, row_counts, table, wavenumbers, truncation):
+    pairs, lats, slots, channels = spectrum.shape
+    kept_mask = (2 * wavenumbers[:, None, :] < row_counts[None, :, None]).astype(jnp.bfloat16)
+    masked = spectrum * kept_mask[..., None]
+    half_channels = channels // 2
     levels = half_channels // 2
-    real_part = masked[..., :half_channels]
-    imag_part = masked[..., half_channels:]
-    grid_values = jnp.einsum(
-        "plsf,psk->lfk", real_part, cosines, preferred_element_type=jnp.float32
+    rows = lats * half_channels
+    waves = pairs * slots
+    flat = jnp.transpose(masked, (1, 3, 0, 2)).reshape(lats, channels, waves)
+    real_part = flat[:, :half_channels].reshape(rows, waves)
+    imag_part = flat[:, half_channels:].reshape(rows, waves)
+    lhs = jnp.concatenate([real_part, -imag_part], axis=1)
+    grid_values = jnp.dot(lhs, table, preferred_element_type=jnp.float32) * (
+        1.0 / math.sqrt(truncation + 1)
     )
-    grid_values = (
-        grid_values
-        - jnp.einsum("plsf,psk->lfk", imag_part, sines, preferred_element_type=jnp.float32)
-    ) * (1.0 / math.sqrt(truncation + 1))
+    grid_values = grid_values.reshape(lats, half_channels, NLON)
     vortex = grid_values[:, :levels]
     divergence = grid_values[:, levels:]
     products = jnp.concatenate(
         [vortex * divergence, 0.5 * (vortex * vortex - divergence * divergence)], axis=1
     ).astype(jnp.bfloat16)
     scale_back = 4.0 / math.sqrt(NLON)
-    real_out = (
-        jnp.einsum("lfk,psk->plsf", products, cosines, preferred_element_type=jnp.float32)
-        * scale_back
+    back = lax.dot_general(
+        products.reshape(rows, NLON),
+        table,
+        (((1,), (1,)), ((), ())),
+        preferred_element_type=jnp.float32,
     )
-    imag_out = (
-        -jnp.einsum("lfk,psk->plsf", products, sines, preferred_element_type=jnp.float32)
-        * scale_back
+    real_out = back[:, :waves] * scale_back
+    imag_out = back[:, waves:] * (-scale_back)
+    out = jnp.concatenate(
+        [real_out.reshape(lats, half_channels, waves), imag_out.reshape(lats, half_channels, waves)],
+        axis=1,
     )
-    return (jnp.concatenate([real_out, imag_out], axis=-1) * kept_mask[..., None]).astype(
-        jnp.bfloat16
-    )
+    out = jnp.transpose(out.reshape(lats, channels, pairs, slots), (2, 0, 3, 1))
+    return (out * kept_mask[..., None].astype(jnp.float32)).astype(jnp.bfloat16)
 
 
 def local(spec_in, legendre, gauss_weights, row_points):
@@ -97,12 +115,12 @@
     fourier = jnp.concatenate([even_part + odd_part, even_part - odd_part], axis=1).astype(
         jnp.bfloat16
     )
-    cosines, sines, wavenumbers = wave_tables(pair_count * groups, truncation)
+    table, wavenumbers = wave_tables(pair_count * groups, truncation)
     local_rows = row_points.reshape(1, 2 * lat_count)
     band_lats = 2 * lat_count // groups
     lat_rows = lax.all_to_all(fourier, "lat", split_axis=1, concat_axis=0, tiled=True)
     my_rows = lax.dynamic_slice_in_dim(local_rows[0], lax.axis_index("lat") * band_lats, band_lats)
-    answered = fourier_work(lat_rows, my_rows, cosines, sines, wavenumbers, truncation)
+    answered = fourier_work(lat_rows, my_rows, table, wavenumbers, truncation)
     answered = answered.reshape(groups, pair_count, band_lats, 2, channels)
     returned = lax.all_to_all(answered, "lat", split_axis=0, concat_axis=0, tiled=True)
     back = jnp.moveaxis(returned, 0, 1).reshape(pair_count, 2 * lat_count, 2, channels)

time: 804 us -> 447 us (0.56)
  matrix products: 460 us -> 65.7 us
  local copies, waits for them, and re-layouts: 68.9 us -> 111 us
  other arithmetic: 22.8 us -> 55.8 us
  waiting for transfers between devices: 220 us -> 187 us
    dot_general x4 -> x2, matrix products: 418 us -> 24.5 us  [the longest x1 13.6 us: fourier_work(): jnp.dot(lhs, table, preferred_element_type=jnp.float32)]
    concatenate x4, local copies, waits for them, and re-layouts: 1.69 us -> 23.8 us  [fourier_work(): jnp.concatenate([real_out.reshape(lats, half_channels, waves), imag_out.r...]
    concatenate x0 -> x2, other arithmetic: none -> 18.3 us  [the longest x1 18.2 us: wave_tables(): table = lax.optimization_barrier(jnp.concatenate([cosines, sines], axis=0))]
    all_to_all x1, waiting for transfers between devices: 34.4 us -> 16.3 us  [local(): lax.all_to_all(fourier, 'lat', split_axis=1, concat_axis=0, tiled=True)]
    all_gather x1, waiting for transfers between devices: 57.7 us -> 42.6 us  [local(): gathered = lax.all_gather(spec_in, 'lev', axis=0, tiled=True)]
    convert_element_type x3, other arithmetic: 1.74 us -> 12.5 us  [the longest x1 12.3 us: wave_tables(): (cos_a * cos_b - sin_a * sin_b).reshape(rows, NLON).astype(jnp.bfloat16)]
  transfers between devices with their start and end apart: 4 -> 4, of which waited for: 4 -> 4; matrix products, arithmetic and copies ran while one was open for 0% -> 8% of each run, Pallas kernels for 0% -> 0%
where the time goes in v1:
time: 447 us; the launch traced here: 444 us
  waiting for transfers between devices  187 us (42%)
  local copies, waits for them, and re-layouts  111 us (25%)
  matrix products  65.7 us (15%)
  other arithmetic  55.8 us (12%)
  between operations  13.7 us (3%)
  starting transfers between devices  10.6 us (2%)
    reduce_scatter x1, waiting for transfers between devices, local(): lax.psum_scatter(jnp.moveaxis(picked_tiles, 0, 1).reshape(local_channels...  92.7 us
    all_gather x1, waiting for transfers between devices, local(): gathered = lax.all_gather(spec_in, 'lev', axis=0, tiled=True)  42.6 us
    while x20, matrix products  41.2 us
    all_to_all x1, waiting for transfers between devices, local(): lax.all_to_all(answered, 'lat', split_axis=0, concat_axis=0, tiled=True)  34.7 us
    concatenate x4, local copies, waits for them, and re-layouts, fourier_work(): jnp.concatenate([real_out.reshape(lats, half_channels, waves), imag_out.r...  23.8 us
    concatenate x1, other arithmetic, wave_tables(): table = lax.optimization_barrier(jnp.concatenate([cosines, sines], axis=0))  18.2 us
    all_to_all x1, waiting for transfers between devices, local(): lax.all_to_all(fourier, 'lat', split_axis=1, concat_axis=0, tiled=True)  16.3 us
    dot_general x1, matrix products, fourier_work(): jnp.dot(lhs, table, preferred_element_type=jnp.float32)  13.6 us
  transfers between devices with their start and end apart: 4, of which 4 were waited for; matrix products, arithmetic and copies ran while one was open for 8% of the time, Pallas kernels for 0%

profile of v1, /device:TPU:2, one launch (start us, length us, event | category | flops | bytes accessed | tf_op | source)
XLA Modules:
  0.0 444.5 jit_solution(14831004152289276899)
XLA Ops:
  8.1 1.3 fusion.33
  9.5 1.7 fusion.26
  11.2 2.1 fusion.37
  13.3 12.3 %subtract_convert_fusion = (bf16[1280,80,64]{0,2,1:T(8,128)(2,1)}, bf16[1280,80,64]{0,2,1:T(8,128)(2,1)}) fusion(f32[1280,64]{0,1:T(8,128)S(1)} %get-tuple-element.98, f32[1280,80]{0,1:T(8,128)S(1)} %get-tuple-element.96, f32[1280,64]{0,1:T(8,128)S(1)} %get-tuple-element.97, f32[1280,80]{0,1:T(8,128)S(1)} %get-tuple-element.95), kind=kLoop, calls=%fused_computation.18 | loop fusion | flops 52428800 | bytes 27688960 | tf_op jit(solution)/shard_map/convert_element_type | solution.py:43
  25.6 42.6 %all-gather.2.cloned.1.call-done = bf16[32,80,1281]{2,1,0:T(8,128)(2,1)} async-done(((bf16[1,80,1281]{2,1,0:T(8,128)(2,1)}), bf16[32,80,1281]{2,1,0:T(8,128)(2,1)}) %all-gather.2.cloned.1.call-update) | async-done | bytes 6558736 | tf_op jit(solution)/shard_map/all_gather | solution.py:100
  68.2 7.4 %copy.96 = bf16[32,10,8,1281]{3,0,2,1:T(8,128)(2,1)} copy(bf16[32,10,8,1281]{3,2,1,0:T(8,128)(2,1)} %bitcast.117) | data formatting | bytes 13117440 | tf_op jit(solution)/shard_map/reshape | solution.py:102
  75.6 44.9 %while.20 = (s32[]{:T(128)}, f32[10,8,40,4,32]{2,4,3,1,0:T(8,128)}, bf16[10,8,40,1281]{3,2,1,0:T(8,128)(2,1)}, bf16[10,32,8,1281]{3,1,2,0:T(8,128)(2,1)}, bf16[10,8,1281,4]{2,3,1,0:T(4,128)(2,1)S(1)}, /*index=5*/s32[]{:T(128)}) while((s32[]{:T(128)}, f32[10,8,40,4,32]{2,4,3,1,0:T(8,128)}, bf16[10,8,40,1281]{3,2,1,0:T(8,128)(2,1)}, ...), condition=%wide.region_1.2_spmd, body=%wide.region_0.1_spmd.sunk | while | flops 106251264 | bytes 9575181 | solution.py:111
  75.6 1.2 dynamic-slice_bitcast_fusion.7
  77.2 2.1 fusion.54
  80.1 1.2 dynamic-slice_bitcast_fusion.7
  81.7 2.1 fusion.54
  84.6 1.2 dynamic-slice_bitcast_fusion.7
  86.2 2.1 fusion.54
  89.1 1.2 dynamic-slice_bitcast_fusion.7
  90.7 2.1 fusion.54
  93.6 1.2 dynamic-slice_bitcast_fusion.7
  95.2 2.1 fusion.54
  98.1 1.2 dynamic-slice_bitcast_fusion.7
  99.7 2.1 fusion.54
  102.6 1.2 dynamic-slice_bitcast_fusion.7
  104.1 2.1 fusion.54
  107.1 1.2 dynamic-slice_bitcast_fusion.7
  108.6 2.1 fusion.54
  111.6 1.2 dynamic-slice_bitcast_fusion.7
  113.1 2.1 fusion.54
  116.0 1.2 dynamic-slice_bitcast_fusion.7
  117.6 2.1 fusion.54
  120.5 3.4 add_convert_fusion.1
  124.7 3.5 copy.79
  128.1 7.0 %all-to-all-start = ((bf16[80,80,2,32]{0,3,2,1:T(8,128)(2,1)}), bf16[80,80,2,32]{0,3,2,1:T(8,128)(2,1)S(1)}, u32[]{:S(2)}, u32[]{:S(2)}) async-start(bf16[80,80,2,32]{0,3,2,1:T(8,128)(2,1)} %copy.79), calls=%async_computation | async-start | bytes 2621440 | tf_op jit(solution)/shard_map/all_to_all | solution.py:121
  135.2 18.2 %pad_maximum_fusion = bf16[2560,5120]{0,1:T(8,128)(2,1)} fusion(bf16[1280,5120]{0,1:T(8,128)(2,1)} %bitcast.111, bf16[1280,5120]{0,1:T(8,128)(2,1)} %bitcast.110), kind=kLoop, calls=%fused_computation.16 | loop fusion | flops 52428800 | bytes 52428800 | tf_op jit(solution)/shard_map/concatenate | solution.py:45
  153.6 16.3 %all-to-all-done = bf16[80,80,2,32]{0,3,2,1:T(8,128)(2,1)S(1)} async-done(((bf16[80,80,2,32]{0,3,2,1:T(8,128)(2,1)}), bf16[80,80,2,32]{0,3,2,1:T(8,128)(2,1)S(1)}, u32[]{:S(2)}, u32[]{:S(2)}) %all-to-all-start) | async-done | bytes 819232 | tf_op jit(solution)/shard_map/all_to_all | solution.py:121
  170.9 1.0 all_to_all.19
  171.9 1.0 multiply_bitcast_fusion
  172.9 5.8 %copy.81 = bf16[10,32,640,2]{1,3,2,0:T(2,128)(2,1)S(1)} copy(bf16[10,32,640,2]{2,1,3,0:T(8,128)(2,1)} %multiply_bitcast_fusion) | data formatting | bytes 1638400 | tf_op jit(solution)/shard_map/transpose | solution.py:57
  178.7 3.9 fusion.39
  182.6 4.0 copy.92
  186.6 1.8 neg.6
  188.4 2.7 copy.82
  191.1 13.6 %convolution_multiply_fusion = f32[160,5120]{1,0:T(8,128)S(1)} fusion(bf16[2560,5120]{0,1:T(8,128)(2,1)} %pad_maximum_fusion, bf16[160,1280]{1,0:T(8,128)(2,1)} %bitcast.124, bf16[160,1280]{1,0:T(8,128)(2,1)} %bitcast.123), kind=kOutput, calls=%fused_computation.22 | convolution fusion | flops 4196761600 | bytes 30310400 | tf_op jit(solution)/shard_map/dot_general | solution.py:61
  205.2 10.8 %fusion.40 = f32[160,2560]{1,0:T(8,128)S(1)} fusion(bf16[160,5120]{1,0:T(8,128)(2,1)S(1)} %bitcast.122, bf16[2560,5120]{0,1:T(8,128)(2,1)} %pad_maximum_fusion), kind=kOutput, calls=%fused_computation.83 | convolution fusion | flops 4194304000 | bytes 29491200 | tf_op jit(solution)/shard_map/dot_general | solution.py:71
  216.6 5.9 %concatenate.30 = f32[10,16,640,2]{1,0,3,2:T(8,128)} reshape(f32[160,1280]{0,1:T(8,128)S(1)} %copy.85) | data formatting | bytes 1638400 | tf_op jit(solution)/shard_map/concatenate | solution.py:79
  222.5 6.0 %copy.87 = f32[10,16,640,2]{2,1,3,0:T(8,128)S(1)} copy(f32[10,16,640,2]{1,0,3,2:T(8,128)} %concatenate.30) | data formatting | bytes 1638400 | tf_op jit(solution)/shard_map/concatenate | solution.py:79
  228.9 5.9 %concatenate.31 = f32[10,16,640,2]{1,0,3,2:T(8,128)} reshape(f32[160,1280]{0,1:T(8,128)S(1)} %copy.86) | data formatting | bytes 1638400 | tf_op jit(solution)/shard_map/concatenate | solution.py:79
  234.8 6.0 %copy.88 = f32[10,16,640,2]{2,1,3,0:T(8,128)S(1)} copy(f32[10,16,640,2]{1,0,3,2:T(8,128)} %concatenate.31) | data formatting | bytes 1638400 | tf_op jit(solution)/shard_map/concatenate | solution.py:79
  241.0 1.6 reshape.309
  242.6 1.5 copy.89
  244.1 3.6 all-to-all-start.1
  247.8 34.7 %all-to-all-done.1 = bf16[8,80,10,2,32]{1,4,3,2,0:T(8,128)(2,1)S(1)} async-done(((bf16[8,80,10,2,32]{1,4,3,2,0:T(8,128)(2,1)}), bf16[8,80,10,2,32]{1,4,3,2,0:T(8,128)(2,1)S(1)}, u32[]{:S(2)}, u32[]{:S(2)}) %all-to-all-start.1) | async-done | bytes 819232 | tf_op jit(solution)/shard_map/all_to_all | solution.py:125
  282.8 1.5 pad_maximum_fusion.3
  284.3 5.7 %copy.90 = bf16[80,40,2,2,32]{1,4,3,2,0:T(8,128)(2,1)S(1)} copy(bf16[80,40,2,2,32]{0,4,2,1,3:T(8,128)(2,1)} %pad_maximum_fusion.3) | data formatting | bytes 1638400 | tf_op jit(solution)/shard_map/stack | solution.py:130
  290.0 46.5 %while.21 = (s32[]{:T(128)}, bf16[10,32,8,1281]{3,1,2,0:T(8,128)(2,1)}, bf16[10,8,40,1281]{3,2,1,0:T(8,128)(2,1)}, bf16[10,8,40,4,32]{2,4,3,1,0:T(8,128)(2,1)S(1)}, f32[10,8,1281,4]{2,3,1,0:T(4,128)}, /*index=5*/s32[]{:T(128)}) while((s32[]{:T(128)}, bf16[10,32,8,1281]{3,1,2,0:T(8,128)(2,1)}, bf16[10,8,40,1281]{3,2,1,0:T(8,128)(2,1)}, ...), condition=%wide.region_4.5_spmd, body=%wide.region_2.4_spmd.sunk | while | flops 107235072 | bytes 14686669 | solution.py:146
  290.0 2.1 fusion.57
  294.7 2.1 fusion.57
  299.4 2.1 fusion.57
  304.0 2.1 fusion.57
  308.6 2.1 fusion.57
  313.3 2.1 fusion.57
  317.9 2.1 fusion.57
  322.5 2.1 fusion.57
  327.2 2.1 fusion.57
  331.8 2.1 fusion.57
  336.5 8.4 %copy.95 = bf16[32,10,8,1281]{3,2,1,0:T(8,128)(2,1)} copy(bf16[32,10,8,1281]{3,0,2,1:T(8,128)(2,1)} %bitcast.75) | data formatting | bytes 13117440 | tf_op jit(solution)/shard_map/convert_element_type | solution.py:150
  344.9 92.7 %reduce-scatter.2.cloned.1.call-done = bf16[1,80,1281]{2,1,0:T(8,128)(2,1)} async-done(((bf16[32,80,1281]{2,1,0:T(8,128)(2,1)}), bf16[1,80,1281]{2,1,0:T(8,128)(2,1)}) %reduce-scatter.2.cloned.1.call-update) | async-done | bytes 204976 | tf_op jit(solution)/shard_map/reduce_scatter | solution.py:147
  (107 shorter events, 43.6 us)
Async XLA Ops:
  6.5 4.6 %copy-start.1 = (s32[4]{0:T(128)S(1)}, s32[4]{0:T(128)}, u32[]{:S(2)}) copy-start(s32[4]{0:T(128)} %constant.98.clone) | copy-start | bytes 52
  6.5 4.7 %copy-start.2 = (s32[4]{0:T(128)S(1)}, s32[4]{0:T(128)}, u32[]{:S(2)}) copy-start(s32[4]{0:T(128)} %constant.99.clone) | copy-start | bytes 52
  6.5 61.6 %all-gather.2.cloned.1.call-start = ((), (), s32[]{:S(2)}) async-start(), calls=%async_computation.3 | async-start | bytes 7434240 | tf_op jit(solution)/shard_map/all_gather | solution.py:100
  128.1 41.8 %all-to-all-start = ((bf16[80,80,2,32]{0,3,2,1:T(8,128)(2,1)}), bf16[80,80,2,32]{0,3,2,1:T(8,128)(2,1)S(1)}, u32[]{:S(2)}, u32[]{:S(2)}) async-start(bf16[80,80,2,32]{0,3,2,1:T(8,128)(2,1)} %copy.79), calls=%async_computation | async-start | bytes 2621440 | tf_op jit(solution)/shard_map/all_to_all | solution.py:121
  135.2 18.2 %copy-start.4 = (s32[2,40]{1,0:T(2,128)S(1)}, s32[2,40]{1,0:T(2,128)}, u32[]{:S(2)}) copy-start(s32[2,40]{1,0:T(2,128)} %param.13) | copy-start | bytes 964
  182.6 5.9 %copy-start = (bf16[10,16,1280]{1,2,0:T(8,128)(2,1)S(1)}, bf16[10,16,1280]{1,2,0:T(8,128)(2,1)}, u32[]{:S(2)}) copy-start(bf16[10,16,1280]{1,2,0:T(8,128)(2,1)} %get-tuple-element.85) | copy-start | bytes 1228804
  242.6 39.8 %copy-start.3 = (f32[40]{0:T(128)S(1)}, f32[40]{0:T(128)}, u32[]{:S(2)}) copy-start(f32[40]{0:T(128)} %param.12) | copy-start | bytes 484
  244.1 38.3 %all-to-all-start.1 = ((bf16[8,80,10,2,32]{1,4,3,2,0:T(8,128)(2,1)}), bf16[8,80,10,2,32]{1,4,3,2,0:T(8,128)(2,1)S(1)}, u32[]{:S(2)}, u32[]{:S(2)}) async-start(bf16[8,80,10,2,32]{1,4,3,2,0:T(8,128)(2,1)} %copy.89), calls=%async_computation.1 | async-start | bytes 2621440 | tf_op jit(solution)/shard_map/all_to_all | solution.py:125
  247.7 189.9 %reduce-scatter.2.cloned.1.call-start = ((), (), s32[]{:S(2)}) async-start(), calls=%async_computation.4 | async-start | bytes 7434240 | tf_op jit(solution)/shard_map/reduce_scatter | solution.py:147
Sparse Core Ops, SparseCore 0:
  10.0 58.1 all-gather.1
  345.0 92.5 reduce-scatter.1

commit v2 on v1

--- a/solution.py
+++ b/solution.py
@@ -3,25 +3,10 @@
 import jax
 import jax.numpy as jnp
 from jax import lax
+from jax.experimental import pallas as pl
 from jax.sharding import PartitionSpec as P
 
 NLON = 5120
-
-
-SLOT_CODES = (0, 0, 1, 1)
-PARITY_CODES = (0, 1, 0, 1)
-
-
-def pair_masks(first_pair, pair_count, packed):
-    pair_ids = first_pair + jnp.arange(pair_count, dtype=jnp.int32)
-    positions = jnp.arange(packed, dtype=jnp.int32)
-    boundary = packed - 1 - pair_ids
-    in_second = (positions[None, :] >= boundary[:, None]).astype(jnp.int32)
-    degree = positions[None, :] - in_second * boundary[:, None]
-    parity = degree % 2
-    slot_codes = jnp.array(SLOT_CODES, dtype=jnp.int32)
-    parity_codes = jnp.array(PARITY_CODES, dtype=jnp.int32)
-    return (in_second[:, :, None] == slot_codes) & (parity[:, :, None] == parity_codes)
 
 
 def wave_tables(total_pairs, truncation):
@@ -84,37 +69,101 @@
     return (out * kept_mask[..., None].astype(jnp.float32)).astype(jnp.bfloat16)
 
 
+def slot_codes(first_pair, pair_count, packed):
+    pair_ids = first_pair + jnp.arange(pair_count, dtype=jnp.int32)
+    positions = jnp.arange(packed, dtype=jnp.int32)
+    boundary = packed - 1 - pair_ids
+    in_second = (positions[None, :] >= boundary[:, None]).astype(jnp.int32)
+    degree = positions[None, :] - in_second * boundary[:, None]
+    return (2 * in_second + degree % 2).reshape(pair_count, 1, packed)
+
+
+def inverse_kernel(leg_ref, spec_ref, code_ref, out_ref):
+    block = leg_ref.shape[0]
+
+    def one_pair(pp, carry):
+        legendre_pair = leg_ref[pp]
+        spectrum = spec_ref[pp]
+        code = code_ref[pp]
+        slot = code // 2
+        sign = (1 - 2 * (code % 2)).astype(spectrum.dtype)
+        zero = jnp.zeros_like(spectrum)
+        first = jnp.where(slot == 0, spectrum, zero)
+        second = jnp.where(slot == 1, spectrum, zero)
+        masked = jnp.concatenate([first, second, first * sign, second * sign], axis=0)
+        sums = lax.dot_general(
+            legendre_pair, masked, (((1,), (1,)), ((), ())), preferred_element_type=jnp.float32
+        )
+        half = sums.shape[1] // 2
+        out_ref[pp] = jnp.concatenate([sums[:, :half], sums[:, half:]], axis=0).astype(
+            out_ref.dtype
+        )
+        return carry
+
+    lax.fori_loop(0, block, one_pair, 0)
+
+
+def direct_kernel(leg_ref, weight_ref, code_ref, out_ref):
+    block = leg_ref.shape[0]
+    channels = out_ref.shape[1]
+
+    def one_pair(pp, carry):
+        full = jnp.dot(weight_ref[pp], leg_ref[pp], preferred_element_type=jnp.float32)
+        code = code_ref[pp]
+        picked = jnp.where(code == 0, full[:channels], 0.0)
+        for x in range(1, 4):
+            picked = picked + jnp.where(code == x, full[x * channels : (x + 1) * channels], 0.0)
+        out_ref[pp] = picked.astype(out_ref.dtype)
+        return carry
+
+    lax.fori_loop(0, block, one_pair, 0)
+
+
+def legendre_inverse(legendre, spectrum, codes, block):
+    pair_count, lat_count, packed = legendre.shape
+    channels = spectrum.shape[1]
+    return pl.pallas_call(
+        inverse_kernel,
+        grid=(pair_count // block,),
+        in_specs=[
+            pl.BlockSpec((block, lat_count, packed), lambda i: (i, 0, 0)),
+            pl.BlockSpec((block, channels, packed), lambda i: (i, 0, 0)),
+            pl.BlockSpec((block, 1, packed), lambda i: (i, 0, 0)),
+        ],
+        out_specs=pl.BlockSpec((block, 2 * lat_count, 2 * channels), lambda i: (i, 0, 0)),
+        out_shape=jax.ShapeDtypeStruct((pair_count, 2 * lat_count, 2 * channels), jnp.bfloat16),
+    )(legendre, spectrum, codes)
+
+
+def legendre_direct(legendre, weights, codes, block):
+    pair_count, lat_count, packed = legendre.shape
+    rows = weights.shape[1]
+    channels = rows // 4
+    return pl.pallas_call(
+        direct_kernel,
+        grid=(pair_count // block,),
+        in_specs=[
+            pl.BlockSpec((block, lat_count, packed), lambda i: (i, 0, 0)),
+            pl.BlockSpec((block, rows, lat_count), lambda i: (i, 0, 0)),
+            pl.BlockSpec((block, 1, packed), lambda i: (i, 0, 0)),
+        ],
+        out_specs=pl.BlockSpec((block, channels, packed), lambda i: (i, 0, 0)),
+        out_shape=jax.ShapeDtypeStruct((pair_count, channels, packed), jnp.bfloat16),
+    )(legendre, weights, codes)
+
+
 def local(spec_in, legendre, gauss_weights, row_points):
     pair_count, lat_count, packed = legendre.shape
     truncation = packed - 2
     groups = lax.axis_size("lat")
     local_channels = spec_in.shape[0]
     channels = local_channels * lax.axis_size("lev")
-    tile_size = math.gcd(pair_count, 8)
-    tile_count = pair_count // tile_size
+    block = math.gcd(pair_count, 8)
     first_pair = lax.axis_index("lat") * pair_count
-    selector = pair_masks(first_pair, pair_count, packed)
-    select_half = selector.astype(jnp.bfloat16).reshape(tile_count, tile_size, packed, 4)
-    select_full = selector.astype(jnp.float32).reshape(tile_count, tile_size, packed, 4)
-    legendre_tiles = legendre.reshape(tile_count, tile_size, lat_count, packed)
-    gathered = lax.all_gather(spec_in, "lev", axis=0, tiled=True)
-    piece_width = gathered.shape[0]
-    spectral = jnp.moveaxis(gathered.reshape(piece_width, tile_count, tile_size, packed), 1, 0)
-
-    def inverse_tile(inputs):
-        legendre_tile, spectral_tile, select_tile = inputs
-        spread = spectral_tile[None] * jnp.moveaxis(select_tile, 2, 0)[:, None]
-        return jnp.einsum(
-            "pjq,xcpq->pjxc", legendre_tile, spread, preferred_element_type=jnp.float32
-        )
-
-    tile_sums = lax.map(inverse_tile, (legendre_tiles, spectral, select_half))
-    legendre_sums = tile_sums.reshape(pair_count, lat_count, 4, piece_width)
-    even_part = legendre_sums[:, :, 0::2]
-    odd_part = legendre_sums[:, :, 1::2]
-    fourier = jnp.concatenate([even_part + odd_part, even_part - odd_part], axis=1).astype(
-        jnp.bfloat16
-    )
+    codes = slot_codes(first_pair, pair_count, packed)
+    gathered = lax.all_gather(spec_in[0], "lev", axis=1, tiled=False)
+    fourier = legendre_inverse(legendre, gathered, codes, block)
+    fourier = fourier.reshape(pair_count, 2 * lat_count, 2, channels)
     table, wavenumbers = wave_tables(pair_count * groups, truncation)
     local_rows = row_points.reshape(1, 2 * lat_count)
     band_lats = 2 * lat_count // groups
@@ -130,28 +179,11 @@
     weighted = jnp.stack(
         [weights * (north_rows + south_rows), weights * (north_rows - south_rows)], axis=3
     )
-    weighted = weighted.reshape(pair_count, lat_count, 4, channels).astype(jnp.bfloat16)
-    part_tiles = weighted.reshape(
-        tile_count, tile_size, lat_count, 4, local_channels * lax.axis_size("lev")
-    )
-
-    def direct_tile(inputs):
-        legendre_tile, weighted_tile, select_tile = inputs
-        full_sums = jnp.einsum(
-            "pjq,pjxc->pqxc", legendre_tile, weighted_tile, preferred_element_type=jnp.float32
-        )
-        picked = jnp.sum(full_sums * select_tile[:, :, :, None], axis=2)
-        return jnp.moveaxis(picked, 2, 0)
-
-    picked_tiles = lax.map(direct_tile, (legendre_tiles, part_tiles, select_full))
-    return lax.psum_scatter(
-        jnp.moveaxis(picked_tiles, 0, 1)
-        .reshape(local_channels * lax.axis_size("lev"), pair_count, packed)
-        .astype(jnp.bfloat16),
-        "lev",
-        scatter_dimension=0,
-        tiled=True,
-    )
+    weighted = weighted.reshape(pair_count, lat_count, 4 * channels).astype(jnp.bfloat16)
+    weighted = jnp.swapaxes(weighted, 1, 2)
+    partial = legendre_direct(legendre, weighted, codes, block)
+    summed = lax.psum_scatter(partial, "lev", scatter_dimension=1, tiled=True)
+    return jnp.swapaxes(summed, 0, 1)
 
 
 def solution(mesh):

time: 447 us -> 477 us (1.067)
  Pallas kernels: 0 us -> 49.6 us
  matrix products: 65.7 us -> 24.5 us
  blocking collectives: 0 us -> 37.2 us
  other arithmetic: 55.8 us -> 40.9 us
  local copies, waits for them, and re-layouts: 111 us -> 121 us
  waiting for transfers between devices: 187 us -> 181 us
    all_gather x0 -> x2, local copies, waits for them, and re-layouts: none -> 56.4 us  [local(): gathered = lax.all_gather(spec_in[0], 'lev', axis=1, tiled=False)]
    pallas_call x0 -> x2, Pallas kernels: none -> 49.6 us  [the longest x1 28.4 us: legendre_inverse(): pl.pallas_call(inverse_kernel, grid=(pair_count // block,), in_specs=[pl....]
    while x20 -> x0, matrix products: 41.2 us -> none
    all_to_all x0 -> x1, blocking collectives: none -> 37.2 us  [local(): lax.all_to_all(answered, 'lat', split_axis=0, concat_axis=0, tiled=True)]
    all_to_all x1 -> x0, waiting for transfers between devices: 34.7 us -> none  [local(): lax.all_to_all(answered, 'lat', split_axis=0, concat_axis=0, tiled=True)]
    all_gather x1, waiting for transfers between devices: 42.6 us -> 72.2 us  [local(): gathered = lax.all_gather(spec_in[0], 'lev', axis=1, tiled=False)]
    mul x20 -> x0, local copies, waits for them, and re-layouts: 21.1 us -> none  [the longest x10 11.6 us: inverse_tile(): spread = spectral_tile[None] * jnp.moveaxis(select_tile, 2, 0)[:, None]]
    dynamic_update_slice x20 -> x0, local copies, waits for them, and re-layouts: 17.9 us -> none  [the longest x10 9.3 us: local(): lax.map(direct_tile, (legendre_tiles, part_tiles, select_full))]
  transfers between devices with their start and end apart: 4 -> 3, of which waited for: 4 -> 3; matrix products, arithmetic and copies ran while one was open for 8% -> 8% of each run, Pallas kernels for 0% -> 0%
where the time goes in v2:
time: 477 us; the launch traced here: 475 us
  waiting for transfers between devices  181 us (38%)
  local copies, waits for them, and re-layouts  121 us (25%)
  Pallas kernels  49.6 us (10%)
  other arithmetic  40.9 us (9%)
  blocking collectives  37.2 us (8%)
  matrix products  24.5 us (5%)
  between operations  13.6 us (3%)
  starting transfers between devices  7.23 us (2%)
    reduce_scatter x1, waiting for transfers between devices, local(): summed = lax.psum_scatter(partial, 'lev', scatter_dimension=1, tiled=True)  92.3 us
    all_gather x1, waiting for transfers between devices, local(): gathered = lax.all_gather(spec_in[0], 'lev', axis=1, tiled=False)  72.2 us
    all_gather x2, local copies, waits for them, and re-layouts, local(): gathered = lax.all_gather(spec_in[0], 'lev', axis=1, tiled=False)  56.4 us
    all_to_all x1, blocking collectives, local(): lax.all_to_all(answered, 'lat', split_axis=0, concat_axis=0, tiled=True)  37.2 us
    pallas_call x1, Pallas kernels, legendre_inverse(): pl.pallas_call(inverse_kernel, grid=(pair_count // block,), in_specs=[pl....  28.4 us
    concatenate x4, local copies, waits for them, and re-layouts, fourier_work(): jnp.concatenate([real_out.reshape(lats, half_channels, waves), imag_out.r...  23.8 us
    pallas_call x1, Pallas kernels, legendre_direct(): pl.pallas_call(direct_kernel, grid=(pair_count // block,), in_specs=[pl.B...  21.2 us
    concatenate x1, other arithmetic, wave_tables(): table = lax.optimization_barrier(jnp.concatenate([cosines, sines], axis=0))  18.1 us
  transfers between devices with their start and end apart: 3, of which 3 were waited for; matrix products, arithmetic and copies ran while one was open for 8% of the time, Pallas kernels for 0%

profile of v2, /device:TPU:2, one launch (start us, length us, event | category | flops | bytes accessed | tf_op | source)
XLA Modules:
  0.0 474.9 jit_solution(4738721421757322456)
XLA Ops:
  6.5 0.0 all-gather.3.cloned.1.call-start
  6.5 2.8 copy.78
  9.3 0.0 all-gather.3.cloned.1.call-update
  9.4 0.2 copy.86
  9.6 0.2 mul.232
  9.8 1.3 fusion.26
  11.1 1.7 fusion.19
  12.9 2.9 fusion.11.code_ref
  15.8 12.4 %subtract_convert_fusion = (bf16[1280,80,64]{0,2,1:T(8,128)(2,1)}, bf16[1280,80,64]{0,2,1:T(8,128)(2,1)}) fusion(f32[1280,64]{0,1:T(8,128)S(1)} %get-tuple-element.18, f32[1280,80]{0,1:T(8,128)S(1)} %get-tuple-element.16, f32[1280,64]{0,1:T(8,128)S(1)} %get-tuple-element.17, f32[1280,80]{0,1:T(8,128)S(1)} %get-tuple-element.15), kind=kLoop, calls=%fused_computation.2 | loop fusion | flops 52428800 | bytes 27688960 | tf_op jit(solution)/shard_map/convert_element_type | solution.py:28
  28.1 72.2 %all-gather.3.cloned.1.call-done = bf16[1,80,40992]{1,0,2:T(2,128)(2,1)} async-done(((bf16[1,80,1281]{1,0,2:T(2,128)(2,1)}), bf16[1,80,40992]{1,0,2:T(2,128)(2,1)}) %all-gather.3.cloned.1.call-update) | async-done | bytes 6558736 | tf_op jit(solution)/shard_map/all_gather | solution.py:164
  100.4 40.2 %copy.79 = bf16[1,80,40992]{2,1,0:T(8,128)(2,1)} copy(bf16[1,80,40992]{1,0,2:T(2,128)(2,1)} %all-gather.3.cloned.1.call-done) | data formatting | bytes 13117440 | tf_op jit(solution)/shard_map/all_gather | solution.py:164
  140.5 16.3 %reshape.303.spec_ref = bf16[80,32,1281]{2,1,0:T(8,128)(2,1)} reshape(bf16[1,80,40992]{2,1,0:T(8,128)(2,1)} %copy.79) | data formatting | bytes 13117440 | tf_op jit(solution)/shard_map/all_gather | solution.py:164
  156.8 28.4 %shard_map.46 = bf16[80,80,64]{2,1,0:T(8,128)(2,1)} custom-call(bf16[80,40,1281]{2,1,0:T(8,128)(2,1)} %leg_ref.3, bf16[80,32,1281]{2,1,0:T(8,128)(2,1)} %reshape.303.spec_ref, s32[80,1,1281]{2,1,0:T(1,128)} %fusion.11.code_ref), custom_call_target="tpu_custom_call" | custom-call | tf_op jit(solution)/shard_map/pallas_call | solution.py:125
  185.2 2.8 copy.94
  188.1 7.0 %all-to-all-start = ((bf16[80,80,2,32]{0,3,2,1:T(8,128)(2,1)}), bf16[80,80,2,32]{0,3,2,1:T(8,128)(2,1)S(1)}, u32[]{:S(2)}, u32[]{:S(2)}) async-start(bf16[80,80,2,32]{0,3,2,1:T(8,128)(2,1)} %bitcast.1), calls=%async_computation | async-start | bytes 2621440 | tf_op jit(solution)/shard_map/all_to_all | solution.py:170
  195.1 0.2 reduce-scatter.2.cloned.1.call-start
  195.3 0.0 copy-start.2
  195.3 18.1 %pad_maximum_fusion = bf16[2560,5120]{0,1:T(8,128)(2,1)} fusion(bf16[1280,5120]{0,1:T(8,128)(2,1)} %bitcast.47, bf16[1280,5120]{0,1:T(8,128)(2,1)} %bitcast.46), kind=kLoop, calls=%fused_computation | loop fusion | flops 52428800 | bytes 52428800 | tf_op jit(solution)/shard_map/concatenate | solution.py:30
  213.5 0.0 copy-done.2
  213.5 0.1 squeeze_reshape.3
  213.5 0.1 dynamic_slice.3
  213.6 0.1 fusion.29
  213.7 16.1 %all-to-all-done = bf16[80,80,2,32]{0,3,2,1:T(8,128)(2,1)S(1)} async-done(((bf16[80,80,2,32]{0,3,2,1:T(8,128)(2,1)}), bf16[80,80,2,32]{0,3,2,1:T(8,128)(2,1)S(1)}, u32[]{:S(2)}, u32[]{:S(2)}) %all-to-all-start) | async-done | bytes 819232 | tf_op jit(solution)/shard_map/all_to_all | solution.py:170
  229.9 1.0 copy.82
  230.8 1.0 all_to_all.19
  231.8 1.0 multiply_bitcast_fusion
  232.9 5.8 %copy.83 = bf16[10,32,640,2]{1,3,2,0:T(2,128)(2,1)S(1)} copy(bf16[10,32,640,2]{2,1,3,0:T(8,128)(2,1)} %multiply_bitcast_fusion) | data formatting | bytes 1638400 | tf_op jit(solution)/shard_map/transpose | solution.py:42
  238.7 4.0 fusion.30
  242.6 0.0 copy-start
  242.6 4.0 copy.84
  246.7 0.0 copy-done
  246.7 2.6 copy.95
  249.3 1.8 neg.6
  251.2 13.6 %convolution_multiply_fusion = f32[160,5120]{1,0:T(8,128)S(1)} fusion(bf16[2560,5120]{0,1:T(8,128)(2,1)} %pad_maximum_fusion, bf16[160,1280]{1,0:T(8,128)(2,1)} %bitcast.55, bf16[160,1280]{1,0:T(8,128)(2,1)} %bitcast.54), kind=kOutput, calls=%fused_computation.3 | convolution fusion | flops 4196761600 | bytes 30310400 | tf_op jit(solution)/shard_map/dot_general | solution.py:46
  264.8 0.4 multiply_convert_fusion.1
  265.2 0.1 pad_maximum_fusion.1
  265.3 10.8 %fusion.31 = f32[160,2560]{1,0:T(8,128)S(1)} fusion(bf16[160,5120]{1,0:T(8,128)(2,1)S(1)} %bitcast.53, bf16[2560,5120]{0,1:T(8,128)(2,1)} %pad_maximum_fusion), kind=kOutput, calls=%fused_computation.60 | convolution fusion | flops 4194304000 | bytes 29491200 | tf_op jit(solution)/shard_map/dot_general | solution.py:56
  276.1 0.1 slice_multiply_fusion.1
  276.3 0.4 copy.87
  276.7 0.4 copy.88
  277.1 5.9 %concatenate.26 = f32[10,16,640,2]{1,0,3,2:T(8,128)} reshape(f32[160,1280]{0,1:T(8,128)S(1)} %copy.88) | data formatting | bytes 1638400 | tf_op jit(solution)/shard_map/concatenate | solution.py:64
  283.0 6.0 %copy.90 = f32[10,16,640,2]{2,1,3,0:T(8,128)S(1)} copy(f32[10,16,640,2]{1,0,3,2:T(8,128)} %concatenate.26) | data formatting | bytes 1638400 | tf_op jit(solution)/shard_map/concatenate | solution.py:64
  289.0 5.9 %concatenate.25 = f32[10,16,640,2]{1,0,3,2:T(8,128)} reshape(f32[160,1280]{0,1:T(8,128)S(1)} %copy.87) | data formatting | bytes 1638400 | tf_op jit(solution)/shard_map/concatenate | solution.py:64
  294.9 6.0 %copy.89 = f32[10,16,640,2]{2,1,3,0:T(8,128)S(1)} copy(f32[10,16,640,2]{1,0,3,2:T(8,128)} %concatenate.25) | data formatting | bytes 1638400 | tf_op jit(solution)/shard_map/concatenate | solution.py:64
  300.9 0.2 fusion.1
  301.1 0.0 copy-start.1
  301.1 1.6 reshape.301
  302.7 0.3 copy.91
  303.0 37.2 %all_to_all.23 = bf16[8,80,10,2,32]{1,4,3,2,0:T(8,128)(2,1)S(1)} all-to-all(bf16[8,80,10,2,32]{1,4,3,2,0:T(8,128)(2,1)S(1)} %copy.91), channel_id=1, replica_groups=mesh['lat'=8,'lev'=32] {'lat'}, dimensions={0} | all-to-all | bytes 1638400 | tf_op jit(solution)/shard_map/all_to_all | solution.py:174
  340.3 0.0 copy-done.1
  340.3 0.4 fusion.10
  340.7 0.3 pad_maximum_fusion.2
  341.0 5.1 %copy.92 = bf16[80,40,2,2,32]{1,4,3,2,0:T(8,128)(2,1)} copy(bf16[80,40,2,2,32]{0,4,2,1,3:T(8,128)(2,1)S(1)} %pad_maximum_fusion.2) | data formatting | bytes 1638400 | tf_op jit(solution)/shard_map/stack | solution.py:179
  346.1 21.2 %shard_map.47 = bf16[80,32,1281]{2,1,0:T(8,128)(2,1)} custom-call(bf16[80,40,1281]{2,1,0:T(8,128)(2,1)} %leg_ref.3, bf16[80,128,40]{2,1,0:T(8,128)(2,1)} %bitcast.49, s32[80,1,1281]{2,1,0:T(1,128)} %fusion.11.code_ref), custom_call_target="tpu_custom_call" | custom-call | tf_op jit(solution)/shard_map/pallas_call | solution.py:142
  367.3 8.4 %copy.93 = bf16[80,32,1281]{2,0,1:T(8,128)(2,1)} copy(bf16[80,32,1281]{2,1,0:T(8,128)(2,1)} %shard_map.47) | data formatting | bytes 13117440 | tf_op jit(solution)/shard_map/pallas_call | solution.py:142
  375.7 0.0 reduce-scatter.2.cloned.1.call-update
  375.7 92.3 %reduce-scatter.2.cloned.1.call-done = bf16[80,1,1281]{2,0,1:T(8,128)(2,1)} async-done(((bf16[80,32,1281]{2,0,1:T(8,128)(2,1)}), bf16[80,1,1281]{2,0,1:T(8,128)(2,1)}) %reduce-scatter.2.cloned.1.call-update) | async-done | bytes 204976 | tf_op jit(solution)/shard_map/reduce_scatter | solution.py:185
  (5 shorter events, 0.0 us)
Async XLA Ops:
  6.5 93.8 %all-gather.3.cloned.1.call-start = ((), (), s32[]{:S(2)}) async-start(), calls=%async_computation.4 | async-start | bytes 21643776 | tf_op jit(solution)/shard_map/all_gather | solution.py:164
  188.1 41.8 %all-to-all-start = ((bf16[80,80,2,32]{0,3,2,1:T(8,128)(2,1)}), bf16[80,80,2,32]{0,3,2,1:T(8,128)(2,1)S(1)}, u32[]{:S(2)}, u32[]{:S(2)}) async-start(bf16[80,80,2,32]{0,3,2,1:T(8,128)(2,1)} %bitcast.1), calls=%async_computation | async-start | bytes 2621440 | tf_op jit(solution)/shard_map/all_to_all | solution.py:170
  195.1 272.9 %reduce-scatter.2.cloned.1.call-start = ((), (), s32[]{:S(2)}) async-start(), calls=%async_computation.3 | async-start | bytes 7434240 | tf_op jit(solution)/shard_map/reduce_scatter | solution.py:185
  195.3 18.1 %copy-start.2 = (s32[2,40]{1,0:T(2,128)S(1)}, s32[2,40]{1,0:T(2,128)}, u32[]{:S(2)}) copy-start(s32[2,40]{1,0:T(2,128)} %param.7) | copy-start | bytes 964
  242.6 4.0 copy-start
  301.1 39.2 %copy-start.1 = (f32[40]{0:T(128)S(1)}, f32[40]{0:T(128)}, u32[]{:S(2)}) copy-start(f32[40]{0:T(128)} %param.6) | copy-start | bytes 484
Sparse Core Ops, SparseCore 0:
  9.9 90.4 all-gather.2
  375.8 92.1 reduce-scatter.1

commit v3 on v2

--- a/solution.py
+++ b/solution.py
@@ -81,9 +81,9 @@
 def inverse_kernel(leg_ref, spec_ref, code_ref, out_ref):
     block = leg_ref.shape[0]
 
-    def one_pair(pp, carry):
+    for pp in range(block):
         legendre_pair = leg_ref[pp]
-        spectrum = spec_ref[pp]
+        spectrum = spec_ref[:, pp, :]
         code = code_ref[pp]
         slot = code // 2
         sign = (1 - 2 * (code % 2)).astype(spectrum.dtype)
@@ -98,36 +98,30 @@
         out_ref[pp] = jnp.concatenate([sums[:, :half], sums[:, half:]], axis=0).astype(
             out_ref.dtype
         )
-        return carry
-
-    lax.fori_loop(0, block, one_pair, 0)
 
 
 def direct_kernel(leg_ref, weight_ref, code_ref, out_ref):
     block = leg_ref.shape[0]
-    channels = out_ref.shape[1]
+    channels = out_ref.shape[0]
 
-    def one_pair(pp, carry):
+    for pp in range(block):
         full = jnp.dot(weight_ref[pp], leg_ref[pp], preferred_element_type=jnp.float32)
         code = code_ref[pp]
         picked = jnp.where(code == 0, full[:channels], 0.0)
         for x in range(1, 4):
             picked = picked + jnp.where(code == x, full[x * channels : (x + 1) * channels], 0.0)
-        out_ref[pp] = picked.astype(out_ref.dtype)
-        return carry
-
-    lax.fori_loop(0, block, one_pair, 0)
+        out_ref[:, pp, :] = picked.astype(out_ref.dtype)
 
 
 def legendre_inverse(legendre, spectrum, codes, block):
     pair_count, lat_count, packed = legendre.shape
-    channels = spectrum.shape[1]
+    channels = spectrum.shape[0]
     return pl.pallas_call(
         inverse_kernel,
         grid=(pair_count // block,),
         in_specs=[
             pl.BlockSpec((block, lat_count, packed), lambda i: (i, 0, 0)),
-            pl.BlockSpec((block, channels, packed), lambda i: (i, 0, 0)),
+            pl.BlockSpec((channels, block, packed), lambda i: (0, i, 0)),
             pl.BlockSpec((block, 1, packed), lambda i: (i, 0, 0)),
         ],
         out_specs=pl.BlockSpec((block, 2 * lat_count, 2 * channels), lambda i: (i, 0, 0)),
@@ -147,8 +141,8 @@
             pl.BlockSpec((block, rows, lat_count), lambda i: (i, 0, 0)),
             pl.BlockSpec((block, 1, packed), lambda i: (i, 0, 0)),
         ],
-        out_specs=pl.BlockSpec((block, channels, packed), lambda i: (i, 0, 0)),
-        out_shape=jax.ShapeDtypeStruct((pair_count, channels, packed), jnp.bfloat16),
+        out_specs=pl.BlockSpec((channels, block, packed), lambda i: (0, i, 0)),
+        out_shape=jax.ShapeDtypeStruct((channels, pair_count, packed), jnp.bfloat16),
     )(legendre, weights, codes)
 
 
@@ -161,7 +155,7 @@
     block = math.gcd(pair_count, 8)
     first_pair = lax.axis_index("lat") * pair_count
     codes = slot_codes(first_pair, pair_count, packed)
-    gathered = lax.all_gather(spec_in[0], "lev", axis=1, tiled=False)
+    gathered = lax.all_gather(spec_in, "lev", axis=0, tiled=True)
     fourier = legendre_inverse(legendre, gathered, codes, block)
     fourier = fourier.reshape(pair_count, 2 * lat_count, 2, channels)
     table, wavenumbers = wave_tables(pair_count * groups, truncation)
@@ -182,8 +176,7 @@
     weighted = weighted.reshape(pair_count, lat_count, 4 * channels).astype(jnp.bfloat16)
     weighted = jnp.swapaxes(weighted, 1, 2)
     partial = legendre_direct(legendre, weighted, codes, block)
-    summed = lax.psum_scatter(partial, "lev", scatter_dimension=1, tiled=True)
-    return jnp.swapaxes(summed, 0, 1)
+    return lax.psum_scatter(partial, "lev", scatter_dimension=0, tiled=True)
 
 
 def solution(mesh):

time: 477 us -> 367 us (0.77)
  local copies, waits for them, and re-layouts: 121 us -> 53.3 us
  waiting for transfers between devices: 181 us -> 152 us
  Pallas kernels: 49.6 us -> 37.9 us
    all_gather x2 -> x0, local copies, waits for them, and re-layouts: 56.4 us -> none  [local(): gathered = lax.all_gather(spec_in[0], 'lev', axis=1, tiled=False)]
    all_gather x1, waiting for transfers between devices: 72.2 us -> 42.2 us  [local(): gathered = lax.all_gather(spec_in, 'lev', axis=0, tiled=True)]
    pallas_call x1, Pallas kernels: 28.4 us -> 20 us  [legendre_inverse(): pl.pallas_call(inverse_kernel, grid=(pair_count // block,), in_specs=[pl....]
    pallas_call x1 -> x0, local copies, waits for them, and re-layouts: 8.41 us -> none  [legendre_direct(): pl.pallas_call(direct_kernel, grid=(pair_count // block,), in_specs=[pl.B...]
  transfers between devices with their start and end apart: 3 -> 3, of which waited for: 3 -> 3; matrix products, arithmetic and copies ran while one was open for 8% -> 10% of each run, Pallas kernels for 0% -> 0%
where the time goes in v3:
time: 367 us; the launch traced here: 366 us
  waiting for transfers between devices  152 us (41%)
  local copies, waits for them, and re-layouts  53.3 us (15%)
  other arithmetic  40.8 us (11%)
  Pallas kernels  37.9 us (10%)
  blocking collectives  37.2 us (10%)
  matrix products  24.5 us (7%)
  between operations  13.6 us (4%)
  starting transfers between devices  7.23 us (2%)
    reduce_scatter x1, waiting for transfers between devices, local(): return lax.psum_scatter(partial, 'lev', scatter_dimension=0, tiled=True)  92.6 us
    all_gather x1, waiting for transfers between devices, local(): gathered = lax.all_gather(spec_in, 'lev', axis=0, tiled=True)  42.2 us
    all_to_all x1, blocking collectives, local(): lax.all_to_all(answered, 'lat', split_axis=0, concat_axis=0, tiled=True)  37.2 us
    concatenate x4, local copies, waits for them, and re-layouts, fourier_work(): jnp.concatenate([real_out.reshape(lats, half_channels, waves), imag_out.r...  23.8 us
    pallas_call x1, Pallas kernels, legendre_inverse(): pl.pallas_call(inverse_kernel, grid=(pair_count // block,), in_specs=[pl....  20 us
    concatenate x1, other arithmetic, wave_tables(): table = lax.optimization_barrier(jnp.concatenate([cosines, sines], axis=0))  18.2 us
    pallas_call x1, Pallas kernels, legendre_direct(): pl.pallas_call(direct_kernel, grid=(pair_count // block,), in_specs=[pl.B...  17.9 us
    all_to_all x1, waiting for transfers between devices, local(): lax.all_to_all(fourier, 'lat', split_axis=1, concat_axis=0, tiled=True)  16.1 us
  transfers between devices with their start and end apart: 3, of which 3 were waited for; matrix products, arithmetic and copies ran while one was open for 10% of the time, Pallas kernels for 0%

profile of v3, /device:TPU:2, one launch (start us, length us, event | category | flops | bytes accessed | tf_op | source)
XLA Modules:
  0.0 366.2 jit_solution(11265960895668373499)
XLA Ops:
  6.5 0.0 all-gather.2.cloned.1.call-start
  6.5 0.7 all-gather.2.cloned.1.call-update
  7.3 0.2 copy.75
  7.5 0.2 mul.232
  7.7 1.3 fusion.26
  9.1 1.7 fusion.19
  10.8 2.9 fusion.11.code_ref
  13.7 12.2 %subtract_convert_fusion = (bf16[1280,80,64]{0,2,1:T(8,128)(2,1)}, bf16[1280,80,64]{0,2,1:T(8,128)(2,1)}) fusion(f32[1280,64]{0,1:T(8,128)S(1)} %get-tuple-element.18, f32[1280,80]{0,1:T(8,128)S(1)} %get-tuple-element.16, f32[1280,64]{0,1:T(8,128)S(1)} %get-tuple-element.17, f32[1280,80]{0,1:T(8,128)S(1)} %get-tuple-element.15), kind=kLoop, calls=%fused_computation.2 | loop fusion | flops 52428800 | bytes 27688960 | tf_op jit(solution)/shard_map/convert_element_type | solution.py:28
  25.9 42.2 %all-gather.2.cloned.1.call-done.spec_ref = bf16[32,80,1281]{2,1,0:T(8,128)(2,1)} async-done(((bf16[1,80,1281]{2,1,0:T(8,128)(2,1)}), bf16[32,80,1281]{2,1,0:T(8,128)(2,1)}) %all-gather.2.cloned.1.call-update) | async-done | bytes 6558736 | tf_op jit(solution)/shard_map/all_gather | solution.py:158
  68.2 20.0 %shard_map.46 = bf16[80,80,64]{2,1,0:T(8,128)(2,1)} custom-call(bf16[80,40,1281]{2,1,0:T(8,128)(2,1)} %leg_ref.3, bf16[32,80,1281]{2,1,0:T(8,128)(2,1)} %all-gather.2.cloned.1.call-done.spec_ref, s32[80,1,1281]{2,1,0:T(1,128)} %fusion.11.code_ref), custom_call_target="tpu_custom_call" | custom-call | tf_op jit(solution)/shard_map/pallas_call | solution.py:119
  88.1 2.8 copy.82
  90.9 7.0 %all-to-all-start = ((bf16[80,80,2,32]{0,3,2,1:T(8,128)(2,1)}), bf16[80,80,2,32]{0,3,2,1:T(8,128)(2,1)S(1)}, u32[]{:S(2)}, u32[]{:S(2)}) async-start(bf16[80,80,2,32]{0,3,2,1:T(8,128)(2,1)} %bitcast.1), calls=%async_computation | async-start | bytes 2621440 | tf_op jit(solution)/shard_map/all_to_all | solution.py:164
  98.0 0.2 reduce-scatter.2.cloned.1.call-start
  98.2 0.0 copy-start.2
  98.2 18.2 %pad_maximum_fusion = bf16[2560,5120]{0,1:T(8,128)(2,1)} fusion(bf16[1280,5120]{0,1:T(8,128)(2,1)} %bitcast.46, bf16[1280,5120]{0,1:T(8,128)(2,1)} %bitcast.45), kind=kLoop, calls=%fused_computation | loop fusion | flops 52428800 | bytes 52428800 | tf_op jit(solution)/shard_map/concatenate | solution.py:30
  116.3 0.0 copy-done.2
  116.4 0.1 squeeze_reshape.3
  116.4 0.1 dynamic_slice.3
  116.5 0.1 fusion.29
  116.6 16.1 %all-to-all-done = bf16[80,80,2,32]{0,3,2,1:T(8,128)(2,1)S(1)} async-done(((bf16[80,80,2,32]{0,3,2,1:T(8,128)(2,1)}), bf16[80,80,2,32]{0,3,2,1:T(8,128)(2,1)S(1)}, u32[]{:S(2)}, u32[]{:S(2)}) %all-to-all-start) | async-done | bytes 819232 | tf_op jit(solution)/shard_map/all_to_all | solution.py:164
  132.7 1.0 copy.71
  133.7 1.0 all_to_all.19
  134.7 1.0 multiply_bitcast_fusion
  135.7 5.8 %copy.72 = bf16[10,32,640,2]{1,3,2,0:T(2,128)(2,1)S(1)} copy(bf16[10,32,640,2]{2,1,3,0:T(8,128)(2,1)} %multiply_bitcast_fusion) | data formatting | bytes 1638400 | tf_op jit(solution)/shard_map/transpose | solution.py:42
  141.5 3.9 %fusion.30 = (bf16[10,16,1280]{1,2,0:T(8,128)(2,1)}, bf16[10,16,1280]{1,2,0:T(8,128)(2,1)}) fusion(bf16[10,32,1280]{1,2,0:T(8,128)(2,1)S(1)} %bitcast.47), kind=kLoop, calls=%fused_computation.59 | loop fusion | bytes 1638400 | tf_op jit(solution)/shard_map/slice | solution.py:43
  145.4 0.0 copy-start
  145.4 4.0 %copy.83 = bf16[10,16,1280]{2,1,0:T(8,128)(2,1)} copy(bf16[10,16,1280]{1,2,0:T(8,128)(2,1)} %get-tuple-element.8) | data formatting | bytes 819200
  149.4 1.8 neg.6
  151.2 0.0 copy-done
  151.2 2.6 copy.73
  153.8 13.6 %convolution_multiply_fusion = f32[160,5120]{1,0:T(8,128)S(1)} fusion(bf16[2560,5120]{0,1:T(8,128)(2,1)} %pad_maximum_fusion, bf16[160,1280]{1,0:T(8,128)(2,1)} %bitcast.54, bf16[160,1280]{1,0:T(8,128)(2,1)} %bitcast.53), kind=kOutput, calls=%fused_computation.3 | convolution fusion | flops 4196761600 | bytes 30310400 | tf_op jit(solution)/shard_map/dot_general | solution.py:46
  167.5 0.4 multiply_convert_fusion.1
  167.9 0.1 pad_maximum_fusion.1
  168.0 10.8 %fusion.31 = f32[160,2560]{1,0:T(8,128)S(1)} fusion(bf16[160,5120]{1,0:T(8,128)(2,1)S(1)} %bitcast.52, bf16[2560,5120]{0,1:T(8,128)(2,1)} %pad_maximum_fusion), kind=kOutput, calls=%fused_computation.60 | convolution fusion | flops 4194304000 | bytes 29491200 | tf_op jit(solution)/shard_map/dot_general | solution.py:56
  178.8 0.1 slice_multiply_fusion.1
  179.0 0.4 copy.76
  179.4 5.9 %concatenate.25 = f32[10,16,640,2]{1,0,3,2:T(8,128)} reshape(f32[160,1280]{0,1:T(8,128)S(1)} %copy.76) | data formatting | bytes 1638400 | tf_op jit(solution)/shard_map/concatenate | solution.py:64
  185.3 6.0 %copy.78 = f32[10,16,640,2]{2,1,3,0:T(8,128)S(1)} copy(f32[10,16,640,2]{1,0,3,2:T(8,128)} %concatenate.25) | data formatting | bytes 1638400 | tf_op jit(solution)/shard_map/concatenate | solution.py:64
  191.3 0.4 copy.77
  191.7 5.9 %concatenate.26 = f32[10,16,640,2]{1,0,3,2:T(8,128)} reshape(f32[160,1280]{0,1:T(8,128)S(1)} %copy.77) | data formatting | bytes 1638400 | tf_op jit(solution)/shard_map/concatenate | solution.py:64
  197.6 6.0 %copy.79 = f32[10,16,640,2]{2,1,3,0:T(8,128)S(1)} copy(f32[10,16,640,2]{1,0,3,2:T(8,128)} %concatenate.26) | data formatting | bytes 1638400 | tf_op jit(solution)/shard_map/concatenate | solution.py:64
  203.6 0.2 fusion.1
  203.8 0.0 copy-start.1
  203.8 1.6 reshape.301
  205.4 0.3 copy.80
  205.7 37.2 %all_to_all.23 = bf16[8,80,10,2,32]{1,4,3,2,0:T(8,128)(2,1)S(1)} all-to-all(bf16[8,80,10,2,32]{1,4,3,2,0:T(8,128)(2,1)S(1)} %copy.80), channel_id=1, replica_groups=mesh['lat'=8,'lev'=32] {'lat'}, dimensions={0} | all-to-all | bytes 1638400 | tf_op jit(solution)/shard_map/all_to_all | solution.py:168
  243.0 0.0 copy-done.1
  243.0 0.4 fusion.10
  243.4 0.3 pad_maximum_fusion.2
  243.7 5.1 %copy.81 = bf16[80,40,2,2,32]{1,4,3,2,0:T(8,128)(2,1)} copy(bf16[80,40,2,2,32]{0,4,2,1,3:T(8,128)(2,1)S(1)} %pad_maximum_fusion.2) | data formatting | bytes 1638400 | tf_op jit(solution)/shard_map/stack | solution.py:173
  248.8 17.9 %shard_map.47 = bf16[32,80,1281]{2,1,0:T(8,128)(2,1)} custom-call(bf16[80,40,1281]{2,1,0:T(8,128)(2,1)} %leg_ref.3, bf16[80,128,40]{2,1,0:T(8,128)(2,1)} %bitcast.48, s32[80,1,1281]{2,1,0:T(1,128)} %fusion.11.code_ref), custom_call_target="tpu_custom_call" | custom-call | tf_op jit(solution)/shard_map/pallas_call | solution.py:136
  266.7 0.0 reduce-scatter.2.cloned.1.call-update
  266.7 92.6 %reduce-scatter.2.cloned.1.call-done = bf16[1,80,1281]{2,1,0:T(8,128)(2,1)} async-done(((bf16[32,80,1281]{2,1,0:T(8,128)(2,1)}), bf16[1,80,1281]{2,1,0:T(8,128)(2,1)}) %reduce-scatter.2.cloned.1.call-update) | async-done | bytes 204976 | tf_op jit(solution)/shard_map/reduce_scatter | solution.py:179
  (5 shorter events, 0.0 us)
Async XLA Ops:
  6.5 61.6 %all-gather.2.cloned.1.call-start = ((), (), s32[]{:S(2)}) async-start(), calls=%async_computation.3 | async-start | bytes 7434240 | tf_op jit(solution)/shard_map/all_gather | solution.py:158
  90.9 41.8 %all-to-all-start = ((bf16[80,80,2,32]{0,3,2,1:T(8,128)(2,1)}), bf16[80,80,2,32]{0,3,2,1:T(8,128)(2,1)S(1)}, u32[]{:S(2)}, u32[]{:S(2)}) async-start(bf16[80,80,2,32]{0,3,2,1:T(8,128)(2,1)} %bitcast.1), calls=%async_computation | async-start | bytes 2621440 | tf_op jit(solution)/shard_map/all_to_all | solution.py:164
  98.0 261.4 %reduce-scatter.2.cloned.1.call-start = ((), (), s32[]{:S(2)}) async-start(), calls=%async_computation.4 | async-start | bytes 7434240 | tf_op jit(solution)/shard_map/reduce_scatter | solution.py:179
  98.2 18.2 %copy-start.2 = (s32[2,40]{1,0:T(2,128)S(1)}, s32[2,40]{1,0:T(2,128)}, u32[]{:S(2)}) copy-start(s32[2,40]{1,0:T(2,128)} %param.7) | copy-start | bytes 964
  145.4 5.8 %copy-start = (bf16[10,16,1280]{1,2,0:T(8,128)(2,1)S(1)}, bf16[10,16,1280]{1,2,0:T(8,128)(2,1)}, u32[]{:S(2)}) copy-start(bf16[10,16,1280]{1,2,0:T(8,128)(2,1)} %get-tuple-element.7) | copy-start | bytes 1228804
  203.8 39.2 %copy-start.1 = (f32[40]{0:T(128)S(1)}, f32[40]{0:T(128)}, u32[]{:S(2)}) copy-start(f32[40]{0:T(128)} %param.6) | copy-start | bytes 484
Sparse Core Ops, SparseCore 0:
  10.0 58.1 all-gather.1
  266.9 92.4 reduce-scatter.1

commit v4 on v3

--- a/solution.py
+++ b/solution.py
@@ -4,6 +4,7 @@
 import jax.numpy as jnp
 from jax import lax
 from jax.experimental import pallas as pl
+from jax.sharding import Mesh
 from jax.sharding import PartitionSpec as P
 
 NLON = 5120
@@ -150,14 +151,17 @@
     pair_count, lat_count, packed = legendre.shape
     truncation = packed - 2
     groups = lax.axis_size("lat")
-    local_channels = spec_in.shape[0]
-    channels = local_channels * lax.axis_size("lev")
+    cores = lax.axis_size("core")
+    chips = lax.axis_size("chip")
+    channels = spec_in.shape[0] * chips * cores
     block = math.gcd(pair_count, 8)
     first_pair = lax.axis_index("lat") * pair_count
     codes = slot_codes(first_pair, pair_count, packed)
-    gathered = lax.all_gather(spec_in, "lev", axis=0, tiled=True)
+    gathered = lax.all_gather(spec_in, "chip", axis=0, tiled=True)
+    gathered = lax.all_gather(gathered, "core", axis=0, tiled=True)
     fourier = legendre_inverse(legendre, gathered, codes, block)
-    fourier = fourier.reshape(pair_count, 2 * lat_count, 2, channels)
+    fourier = fourier.reshape(pair_count, 2 * lat_count, 2, cores, chips)
+    fourier = jnp.swapaxes(fourier, 3, 4).reshape(pair_count, 2 * lat_count, 2, channels)
     table, wavenumbers = wave_tables(pair_count * groups, truncation)
     local_rows = row_points.reshape(1, 2 * lat_count)
     band_lats = 2 * lat_count // groups
@@ -173,17 +177,23 @@
     weighted = jnp.stack(
         [weights * (north_rows + south_rows), weights * (north_rows - south_rows)], axis=3
     )
-    weighted = weighted.reshape(pair_count, lat_count, 4 * channels).astype(jnp.bfloat16)
+    weighted = weighted.reshape(pair_count, lat_count, 4, chips, cores).astype(jnp.bfloat16)
+    weighted = jnp.swapaxes(weighted, 3, 4).reshape(pair_count, lat_count, 4 * channels)
     weighted = jnp.swapaxes(weighted, 1, 2)
     partial = legendre_direct(legendre, weighted, codes, block)
-    return lax.psum_scatter(partial, "lev", scatter_dimension=0, tiled=True)
+    partial = lax.psum_scatter(partial, "core", scatter_dimension=0, tiled=True)
+    return lax.psum_scatter(partial, "chip", scatter_dimension=0, tiled=True)
 
 
 def solution(mesh):
+    lat_size, lev_size = mesh.devices.shape
+    cores = 2 if lev_size % 2 == 0 else 1
+    inner = Mesh(mesh.devices.reshape(lat_size, lev_size // cores, cores), ("lat", "chip", "core"))
+    lev = ("chip", "core")
     return jax.shard_map(
         local,
-        mesh=mesh,
-        in_specs=(P("lev", "lat", None), P("lat", "lev", None), P("lev"), P(None, "lev")),
-        out_specs=P("lev", "lat", None),
+        mesh=inner,
+        in_specs=(P(lev, "lat", None), P("lat", lev, None), P(lev), P(None, lev)),
+        out_specs=P(lev, "lat", None),
         check_vma=False,
     )

time: 367 us -> 407 us (1.11)
  waiting for transfers between devices: 152 us -> 188 us
    unnamed x2 -> x5, waiting for transfers between devices: 0.73 us -> 90 us
    reduce_scatter x1, waiting for transfers between devices: 92.6 us -> 17.1 us  [local(): partial = lax.psum_scatter(partial, 'core', scatter_dimension=0, tiled=True)]
    all_gather x1 -> x2, waiting for transfers between devices: 42.2 us -> 64.9 us  [the longest x1 59.4 us: local(): gathered = lax.all_gather(spec_in, 'chip', axis=0, tiled=True)]
    transpose x0 -> x2, local copies, waits for them, and re-layouts: none -> 5.39 us  [the longest x1 4.54 us: local(): jnp.swapaxes(weighted, 3, 4).reshape(pair_count, lat_count, 4 * channels)]
    another operation x1, local copies, waits for them, and re-layouts: 5.1 us -> 0.85 us  [local(): jnp.stack([weights * (north_rows + south_rows), weights * (north_rows - s...]
  transfers between devices with their start and end apart: 3 -> 5, of which waited for: 3 -> 5; matrix products, arithmetic and copies ran while one was open for 10% -> 9% of each run, Pallas kernels for 0% -> 0%
where the time goes in v4:
time: 407 us; the launch traced here: 406 us
  waiting for transfers between devices  188 us (46%)
  local copies, waits for them, and re-layouts  56.2 us (14%)
  other arithmetic  41.6 us (10%)
  Pallas kernels  37.9 us (9%)
  blocking collectives  37.2 us (9%)
  matrix products  24.5 us (6%)
  between operations  13.4 us (3%)
  starting transfers between devices  7.31 us (2%)
    unnamed x5, waiting for transfers between devices  90 us
    all_gather x1, waiting for transfers between devices, local(): gathered = lax.all_gather(spec_in, 'chip', axis=0, tiled=True)  59.4 us
    all_to_all x1, blocking collectives, local(): lax.all_to_all(answered, 'lat', split_axis=0, concat_axis=0, tiled=True)  37.2 us
    concatenate x4, local copies, waits for them, and re-layouts, fourier_work(): jnp.concatenate([real_out.reshape(lats, half_channels, waves), imag_out.r...  23.8 us
    pallas_call x1, Pallas kernels, legendre_inverse(): pl.pallas_call(inverse_kernel, grid=(pair_count // block,), in_specs=[pl....  20 us
    concatenate x1, other arithmetic, wave_tables(): table = lax.optimization_barrier(jnp.concatenate([cosines, sines], axis=0))  18.2 us
    pallas_call x1, Pallas kernels, legendre_direct(): pl.pallas_call(direct_kernel, grid=(pair_count // block,), in_specs=[pl.B...  18 us
    reduce_scatter x1, waiting for transfers between devices, local(): partial = lax.psum_scatter(partial, 'core', scatter_dimension=0, tiled=True)  17.1 us
  transfers between devices with their start and end apart: 5, of which 5 were waited for; matrix products, arithmetic and copies ran while one was open for 9% of the time, Pallas kernels for 0%

profile of v4, /device:TPU:2, one launch (start us, length us, event | category | flops | bytes accessed | tf_op | source)
XLA Modules:
  0.0 406.3 jit_solution(17317300655444209699)
XLA Ops:
  6.5 0.0 all-gather.3.cloned.1.call-start
  6.5 0.7 all-gather.3.cloned.1.call-update
  7.3 0.0 all-gather.5.cloned.1.call-start
  7.3 59.4 %all-gather.3.cloned.1.call-done = bf16[16,80,1281]{2,1,0:T(8,128)(2,1)} async-done(((bf16[1,80,1281]{2,1,0:T(8,128)(2,1)}), bf16[16,80,1281]{2,1,0:T(8,128)(2,1)}) %all-gather.3.cloned.1.call-update) | async-done | bytes 3279376 | tf_op jit(solution)/shard_map/all_gather | solution.py:160
  66.7 0.0 all-gather.5.cloned.1.call-update
  66.8 0.2 copy.82
  67.0 0.2 mul.232
  67.2 1.3 fusion.26
  68.6 1.7 fusion.19
  70.3 2.9 fusion.11.code_ref
  73.2 13.1 %subtract_convert_fusion = (bf16[1280,80,64]{0,2,1:T(8,128)(2,1)}, bf16[1280,80,64]{0,2,1:T(8,128)(2,1)}) fusion(f32[1280,64]{0,1:T(8,128)S(1)} %get-tuple-element.18, f32[1280,80]{0,1:T(8,128)S(1)} %get-tuple-element.16, f32[1280,64]{0,1:T(8,128)S(1)} %get-tuple-element.17, f32[1280,80]{0,1:T(8,128)S(1)} %get-tuple-element.15), kind=kLoop, calls=%fused_computation.2 | loop fusion | flops 52428800 | bytes 27688960 | tf_op jit(solution)/shard_map/convert_element_type | solution.py:29
  86.2 5.5 %all-gather.5.cloned.1.call-done.spec_ref = bf16[32,80,1281]{2,1,0:T(8,128)(2,1)} async-done(((bf16[16,80,1281]{2,1,0:T(8,128)(2,1)}), bf16[32,80,1281]{2,1,0:T(8,128)(2,1)}) %all-gather.5.cloned.1.call-update) | async-done | bytes 6558736 | tf_op jit(solution)/shard_map/all_gather | solution.py:161
  91.7 20.0 %shard_map.46 = bf16[80,80,64]{2,1,0:T(8,128)(2,1)} custom-call(bf16[80,40,1281]{2,1,0:T(8,128)(2,1)} %leg_ref.3, bf16[32,80,1281]{2,1,0:T(8,128)(2,1)} %all-gather.5.cloned.1.call-done.spec_ref, s32[80,1,1281]{2,1,0:T(1,128)} %fusion.11.code_ref), custom_call_target="tpu_custom_call" | custom-call | tf_op jit(solution)/shard_map/pallas_call | solution.py:120
  111.7 1.9 copy.75
  113.6 0.8 copy.76
  114.4 2.7 copy.77
  117.2 7.0 %all-to-all-start = ((bf16[80,80,2,32]{0,3,2,1:T(8,128)(2,1)}), bf16[80,80,2,32]{0,3,2,1:T(8,128)(2,1)S(1)}, u32[]{:S(2)}, u32[]{:S(2)}) async-start(bf16[80,80,2,32]{0,3,2,1:T(8,128)(2,1)} %copy.77), calls=%async_computation | async-start | bytes 2621440 | tf_op jit(solution)/shard_map/all_to_all | solution.py:168
  124.2 0.2 reduce-scatter.5.cloned.1.call-start
  124.4 0.0 copy-start.2
  124.4 18.2 %pad_maximum_fusion = bf16[2560,5120]{0,1:T(8,128)(2,1)} fusion(bf16[1280,5120]{0,1:T(8,128)(2,1)} %bitcast.52, bf16[1280,5120]{0,1:T(8,128)(2,1)} %bitcast.51), kind=kLoop, calls=%fused_computation | loop fusion | flops 52428800 | bytes 52428800 | tf_op jit(solution)/shard_map/concatenate | solution.py:31
  142.6 0.0 copy-done.2
  142.6 0.1 squeeze_reshape.3
  142.7 0.1 dynamic_slice.3
  142.8 0.1 fusion.29
  142.9 16.1 %all-to-all-done = bf16[80,80,2,32]{0,3,2,1:T(8,128)(2,1)S(1)} async-done(((bf16[80,80,2,32]{0,3,2,1:T(8,128)(2,1)}), bf16[80,80,2,32]{0,3,2,1:T(8,128)(2,1)S(1)}, u32[]{:S(2)}, u32[]{:S(2)}) %all-to-all-start) | async-done | bytes 819232 | tf_op jit(solution)/shard_map/all_to_all | solution.py:168
  159.0 1.0 copy.78
  160.0 1.0 all_to_all.19
  161.0 1.0 multiply_bitcast_fusion
  162.0 5.8 %copy.79 = bf16[10,32,640,2]{1,3,2,0:T(2,128)(2,1)S(1)} copy(bf16[10,32,640,2]{2,1,3,0:T(8,128)(2,1)} %multiply_bitcast_fusion) | data formatting | bytes 1638400 | tf_op jit(solution)/shard_map/transpose | solution.py:43
  167.8 3.9 fusion.30
  171.6 0.0 copy-start
  171.6 4.0 copy.90
  175.7 1.8 neg.6
  177.5 0.0 copy-done
  177.5 2.6 copy.80
  180.1 13.6 %convolution_multiply_fusion = f32[160,5120]{1,0:T(8,128)S(1)} fusion(bf16[2560,5120]{0,1:T(8,128)(2,1)} %pad_maximum_fusion, bf16[160,1280]{1,0:T(8,128)(2,1)} %bitcast.63, bf16[160,1280]{1,0:T(8,128)(2,1)} %bitcast.62), kind=kOutput, calls=%fused_computation.3 | convolution fusion | flops 4196761600 | bytes 30310400 | tf_op jit(solution)/shard_map/dot_general | solution.py:47
  193.8 0.4 multiply_convert_fusion.1
  194.2 0.1 pad_maximum_fusion.1
  194.3 10.8 %fusion.31 = f32[160,2560]{1,0:T(8,128)S(1)} fusion(bf16[160,5120]{1,0:T(8,128)(2,1)S(1)} %bitcast.61, bf16[2560,5120]{0,1:T(8,128)(2,1)} %pad_maximum_fusion), kind=kOutput, calls=%fused_computation.60 | convolution fusion | flops 4194304000 | bytes 29491200 | tf_op jit(solution)/shard_map/dot_general | solution.py:57
  205.1 0.1 slice_multiply_fusion.1
  205.3 0.4 copy.83
  205.7 5.9 %concatenate.25 = f32[10,16,640,2]{1,0,3,2:T(8,128)} reshape(f32[160,1280]{0,1:T(8,128)S(1)} %copy.83) | data formatting | bytes 1638400 | tf_op jit(solution)/shard_map/concatenate | solution.py:65
  211.6 6.0 %copy.85 = f32[10,16,640,2]{2,1,3,0:T(8,128)S(1)} copy(f32[10,16,640,2]{1,0,3,2:T(8,128)} %concatenate.25) | data formatting | bytes 1638400 | tf_op jit(solution)/shard_map/concatenate | solution.py:65
  217.6 0.4 copy.84
  218.0 5.9 %concatenate.26 = f32[10,16,640,2]{1,0,3,2:T(8,128)} reshape(f32[160,1280]{0,1:T(8,128)S(1)} %copy.84) | data formatting | bytes 1638400 | tf_op jit(solution)/shard_map/concatenate | solution.py:65
  223.9 6.0 %copy.86 = f32[10,16,640,2]{2,1,3,0:T(8,128)S(1)} copy(f32[10,16,640,2]{1,0,3,2:T(8,128)} %concatenate.26) | data formatting | bytes 1638400 | tf_op jit(solution)/shard_map/concatenate | solution.py:65
  229.9 0.2 fusion.1
  230.1 1.6 reshape.308
  231.7 0.0 copy-start.1
  231.7 0.3 copy.87
  232.0 37.2 %all_to_all.23 = bf16[8,80,10,2,32]{1,4,3,2,0:T(8,128)(2,1)S(1)} all-to-all(bf16[8,80,10,2,32]{1,4,3,2,0:T(8,128)(2,1)S(1)} %copy.87), channel_id=1, replica_groups=mesh['lat'=8,'chip'=16,'core'=2] {'lat'}, dimensions={0} | all-to-all | bytes 1638400 | tf_op jit(solution)/shard_map/all_to_all | solution.py:172
  269.3 0.0 copy-done.1
  269.3 0.4 fusion.10
  269.7 0.3 pad_maximum_fusion.2
  270.0 0.8 copy.88
  270.8 4.5 %copy.89 = bf16[80,40,4,2,16]{1,4,3,2,0:T(8,128)(2,1)} copy(bf16[80,40,4,2,16]{0,1,3,4,2:T(8,128)(2,1)S(1)} %bitcast.59) | data formatting | bytes 1638400 | tf_op jit(solution)/shard_map/transpose | solution.py:181
  275.4 18.0 %shard_map.47 = bf16[32,80,1281]{2,1,0:T(8,128)(2,1)} custom-call(bf16[80,40,1281]{2,1,0:T(8,128)(2,1)} %leg_ref.3, bf16[80,128,40]{2,1,0:T(8,128)(2,1)} %bitcast.54, s32[80,1,1281]{2,1,0:T(1,128)} %fusion.11.code_ref), custom_call_target="tpu_custom_call" | custom-call | tf_op jit(solution)/shard_map/pallas_call | solution.py:137
  293.4 0.0 reduce-scatter.5.cloned.1.call-update
  293.4 0.0 reduce-scatter.7.cloned.1.call-start
  293.4 17.1 %reduce-scatter.5.cloned.1.call-done = bf16[16,80,1281]{2,1,0:T(8,128)(2,1)} async-done(((bf16[32,80,1281]{2,1,0:T(8,128)(2,1)}), bf16[16,80,1281]{2,1,0:T(8,128)(2,1)}) %reduce-scatter.5.cloned.1.call-update) | async-done | bytes 3279376 | tf_op jit(solution)/shard_map/reduce_scatter | solution.py:184
  310.6 0.0 reduce-scatter.7.cloned.1.call-update
  310.6 89.2 %reduce-scatter.7.cloned.1.call-done = bf16[1,80,1281]{2,1,0:T(8,128)(2,1)} async-done(((bf16[16,80,1281]{2,1,0:T(8,128)(2,1)}), bf16[1,80,1281]{2,1,0:T(8,128)(2,1)}) %reduce-scatter.7.cloned.1.call-update) | async-done | bytes 204976
  (5 shorter events, 0.0 us)
Async XLA Ops:
  6.5 60.2 %all-gather.3.cloned.1.call-start = ((), (), s32[]{:S(2)}) async-start(), calls=%async_computation.4 | async-start | bytes 3829760 | tf_op jit(solution)/shard_map/all_gather | solution.py:160
  7.3 84.5 %all-gather.5.cloned.1.call-start = ((), (), s32[]{:S(2)}) async-start(), calls=%async_computation.5 | async-start | bytes 10813440 | tf_op jit(solution)/shard_map/all_gather | solution.py:161
  117.2 41.8 %all-to-all-start = ((bf16[80,80,2,32]{0,3,2,1:T(8,128)(2,1)}), bf16[80,80,2,32]{0,3,2,1:T(8,128)(2,1)S(1)}, u32[]{:S(2)}, u32[]{:S(2)}) async-start(bf16[80,80,2,32]{0,3,2,1:T(8,128)(2,1)} %copy.77), calls=%async_computation | async-start | bytes 2621440 | tf_op jit(solution)/shard_map/all_to_all | solution.py:168
  124.2 186.4 %reduce-scatter.5.cloned.1.call-start = ((), (), s32[]{:S(2)}) async-start(), calls=%async_computation.6 | async-start | bytes 10813440 | tf_op jit(solution)/shard_map/reduce_scatter | solution.py:184
  124.4 18.2 %copy-start.2 = (s32[2,40]{1,0:T(2,128)S(1)}, s32[2,40]{1,0:T(2,128)}, u32[]{:S(2)}) copy-start(s32[2,40]{1,0:T(2,128)} %param.7) | copy-start | bytes 964
  171.6 5.9 %copy-start = (bf16[10,16,1280]{1,2,0:T(8,128)(2,1)S(1)}, bf16[10,16,1280]{1,2,0:T(8,128)(2,1)}, u32[]{:S(2)}) copy-start(bf16[10,16,1280]{1,2,0:T(8,128)(2,1)} %get-tuple-element.7) | copy-start | bytes 1228804
  231.7 37.6 %copy-start.1 = (f32[40]{0:T(128)S(1)}, f32[40]{0:T(128)}, u32[]{:S(2)}) copy-start(f32[40]{0:T(128)} %param.6) | copy-start | bytes 484
  293.4 106.4 %reduce-scatter.7.cloned.1.call-start = ((), (), s32[]{:S(2)}) async-start(), calls=%async_computation.7 | async-start | bytes 3829760
Sparse Core Ops, SparseCore 0:
  9.8 56.8 all-gather.2
  68.5 23.1 all-gather.4
  293.5 17.0 reduce-scatter.4
  314.7 85.0 reduce-scatter.6

commit v5 on v3

--- a/solution.py
+++ b/solution.py
@@ -59,14 +59,11 @@
         (((1,), (1,)), ((), ())),
         preferred_element_type=jnp.float32,
     )
-    real_out = back[:, :waves] * scale_back
-    imag_out = back[:, waves:] * (-scale_back)
-    out = jnp.concatenate(
-        [real_out.reshape(lats, half_channels, waves), imag_out.reshape(lats, half_channels, waves)],
-        axis=1,
-    )
-    out = jnp.transpose(out.reshape(lats, channels, pairs, slots), (2, 0, 3, 1))
-    return (out * kept_mask[..., None].astype(jnp.float32)).astype(jnp.bfloat16)
+    sign = jnp.where(jnp.arange(2) == 0, scale_back, -scale_back).astype(jnp.float32)
+    keep = jnp.transpose(kept_mask, (1, 0, 2)).astype(jnp.float32).reshape(lats, 1, 1, waves)
+    back = lax.optimization_barrier(back).reshape(lats, half_channels, 2, waves) * sign[:, None] * keep
+    out = jnp.transpose(back.astype(jnp.bfloat16).reshape(lats, half_channels, 2, pairs, slots), (3, 0, 4, 2, 1))
+    return out.reshape(pairs, lats, slots, channels)
 
 
 def slot_codes(first_pair, pair_count, packed):

time: 367 us -> 378 us (1.030)
  other arithmetic: 40.8 us -> 53.8 us
    concatenate x4 -> x0, local copies, waits for them, and re-layouts: 23.8 us -> none  [fourier_work(): jnp.concatenate([real_out.reshape(lats, half_channels, waves), imag_out.r...]
    transpose x0 -> x1, other arithmetic: none -> 13.1 us  [fourier_work(): jnp.transpose(back.astype(jnp.bfloat16).reshape(lats, half_channels, 2, p...]
    transpose x0 -> x1, local copies, waits for them, and re-layouts: none -> 9.19 us  [fourier_work(): jnp.transpose(back.astype(jnp.bfloat16).reshape(lats, half_channels, 2, p...]
    reshape x2 -> x1, local copies, waits for them, and re-layouts: 1.93 us -> 10.4 us  [fourier_work(): lax.optimization_barrier(back).reshape(lats, half_channels, 2, waves)]
where the time goes in v5:
time: 378 us; the launch traced here: 377 us
  waiting for transfers between devices  151 us (40%)
  other arithmetic  53.8 us (14%)
  local copies, waits for them, and re-layouts  51.2 us (14%)
  Pallas kernels  37.9 us (10%)
  blocking collectives  37 us (10%)
  matrix products  25.6 us (7%)
  between operations  13.6 us (4%)
  starting transfers between devices  7.23 us (2%)
    reduce_scatter x1, waiting for transfers between devices, local(): return lax.psum_scatter(partial, 'lev', scatter_dimension=0, tiled=True)  92.9 us
    all_gather x1, waiting for transfers between devices, local(): gathered = lax.all_gather(spec_in, 'lev', axis=0, tiled=True)  42.1 us
    all_to_all x1, blocking collectives, local(): lax.all_to_all(answered, 'lat', split_axis=0, concat_axis=0, tiled=True)  37 us
    pallas_call x1, Pallas kernels, legendre_inverse(): pl.pallas_call(inverse_kernel, grid=(pair_count // block,), in_specs=[pl....  20 us
    concatenate x1, other arithmetic, wave_tables(): table = lax.optimization_barrier(jnp.concatenate([cosines, sines], axis=0))  18.2 us
    pallas_call x1, Pallas kernels, legendre_direct(): pl.pallas_call(direct_kernel, grid=(pair_count // block,), in_specs=[pl.B...  17.9 us
    all_to_all x1, waiting for transfers between devices, local(): lax.all_to_all(fourier, 'lat', split_axis=1, concat_axis=0, tiled=True)  14.9 us
    dot_general x1, matrix products, fourier_work(): jnp.dot(lhs, table, preferred_element_type=jnp.float32)  13.6 us
  transfers between devices with their start and end apart: 3, of which 3 were waited for; matrix products, arithmetic and copies ran while one was open for 10% of the time, Pallas kernels for 0%

profile of v5, /device:TPU:2, one launch (start us, length us, event | category | flops | bytes accessed | tf_op | source)
XLA Modules:
  0.0 377.0 jit_solution(9323739583739455213)
XLA Ops:
  6.5 0.0 all-gather.2.cloned.1.call-start
  6.5 0.7 all-gather.2.cloned.1.call-update
  7.3 0.2 copy.56
  7.5 0.2 mul.239
  7.7 1.3 fusion.25
  9.1 1.7 fusion.18
  10.8 2.9 fusion.10.code_ref
  13.7 12.4 %subtract_convert_fusion = (bf16[1280,80,64]{0,2,1:T(8,128)(2,1)}, bf16[1280,80,64]{0,2,1:T(8,128)(2,1)}) fusion(f32[1280,64]{0,1:T(8,128)S(1)} %get-tuple-element.16, f32[1280,80]{0,1:T(8,128)S(1)} %get-tuple-element.14, f32[1280,64]{0,1:T(8,128)S(1)} %get-tuple-element.15, f32[1280,80]{0,1:T(8,128)S(1)} %get-tuple-element.13), kind=kLoop, calls=%fused_computation.2 | loop fusion | flops 52428800 | bytes 27688960 | tf_op jit(solution)/shard_map/convert_element_type | solution.py:28
  26.1 42.1 %all-gather.2.cloned.1.call-done.spec_ref = bf16[32,80,1281]{2,1,0:T(8,128)(2,1)} async-done(((bf16[1,80,1281]{2,1,0:T(8,128)(2,1)}), bf16[32,80,1281]{2,1,0:T(8,128)(2,1)}) %all-gather.2.cloned.1.call-update) | async-done | bytes 6558736 | tf_op jit(solution)/shard_map/all_gather | solution.py:155
  68.2 20.0 %shard_map.46 = bf16[80,80,64]{2,1,0:T(8,128)(2,1)} custom-call(bf16[80,40,1281]{2,1,0:T(8,128)(2,1)} %leg_ref.3, bf16[32,80,1281]{2,1,0:T(8,128)(2,1)} %all-gather.2.cloned.1.call-done.spec_ref, s32[80,1,1281]{2,1,0:T(1,128)} %fusion.10.code_ref), custom_call_target="tpu_custom_call" | custom-call | tf_op jit(solution)/shard_map/pallas_call | solution.py:116
  88.1 2.8 copy.62
  90.9 7.0 %all-to-all-start = ((bf16[80,80,2,32]{0,3,2,1:T(8,128)(2,1)}), bf16[80,80,2,32]{0,3,2,1:T(8,128)(2,1)S(1)}, u32[]{:S(2)}, u32[]{:S(2)}) async-start(bf16[80,80,2,32]{0,3,2,1:T(8,128)(2,1)} %bitcast.1), calls=%async_computation | async-start | bytes 2621440 | tf_op jit(solution)/shard_map/all_to_all | solution.py:161
  98.0 0.2 reduce-scatter.2.cloned.1.call-start
  98.2 0.0 copy-start.3
  98.2 18.2 %pad_maximum_fusion = bf16[2560,5120]{0,1:T(8,128)(2,1)} fusion(bf16[1280,5120]{0,1:T(8,128)(2,1)} %bitcast.42, bf16[1280,5120]{0,1:T(8,128)(2,1)} %bitcast.41), kind=kLoop, calls=%fused_computation | loop fusion | flops 52428800 | bytes 52428800 | tf_op jit(solution)/shard_map/concatenate | solution.py:30
  116.4 0.0 copy-done.3
  116.4 0.1 squeeze_reshape.3
  116.4 0.1 dynamic_slice.3
  116.6 0.1 fusion.27
  116.6 1.1 copy.58
  117.8 0.1 compare_convert_fusion.1
  117.9 14.9 %all-to-all-done = bf16[80,80,2,32]{0,3,2,1:T(8,128)(2,1)S(1)} async-done(((bf16[80,80,2,32]{0,3,2,1:T(8,128)(2,1)}), bf16[80,80,2,32]{0,3,2,1:T(8,128)(2,1)S(1)}, u32[]{:S(2)}, u32[]{:S(2)}) %all-to-all-start) | async-done | bytes 819232 | tf_op jit(solution)/shard_map/all_to_all | solution.py:161
  132.7 1.0 copy.52
  133.7 1.0 all_to_all.19
  134.7 1.0 multiply_bitcast_fusion
  135.7 5.8 %copy.53 = bf16[10,32,640,2]{1,3,2,0:T(2,128)(2,1)S(1)} copy(bf16[10,32,640,2]{2,1,3,0:T(8,128)(2,1)} %multiply_bitcast_fusion) | data formatting | bytes 1638400 | tf_op jit(solution)/shard_map/transpose | solution.py:42
  141.5 3.9 %fusion.30 = (bf16[10,16,1280]{1,2,0:T(8,128)(2,1)}, bf16[10,16,1280]{1,2,0:T(8,128)(2,1)}) fusion(bf16[10,32,1280]{1,2,0:T(8,128)(2,1)S(1)} %bitcast.43), kind=kLoop, calls=%fused_computation.61 | loop fusion | bytes 1638400 | tf_op jit(solution)/shard_map/slice | solution.py:43
  145.4 0.0 copy-start
  145.4 4.0 %copy.63 = bf16[10,16,1280]{2,1,0:T(8,128)(2,1)} copy(bf16[10,16,1280]{1,2,0:T(8,128)(2,1)} %get-tuple-element.8) | data formatting | bytes 819200
  149.4 1.8 neg.6
  151.2 0.0 copy-done
  151.2 2.6 copy.54
  153.8 13.6 %convolution_multiply_fusion = f32[160,5120]{1,0:T(8,128)S(1)} fusion(bf16[2560,5120]{0,1:T(8,128)(2,1)} %pad_maximum_fusion, bf16[160,1280]{1,0:T(8,128)(2,1)} %bitcast.50, bf16[160,1280]{1,0:T(8,128)(2,1)} %bitcast.49), kind=kOutput, calls=%fused_computation.5 | convolution fusion | flops 4196761600 | bytes 30310400 | tf_op jit(solution)/shard_map/dot_general | solution.py:46
  167.5 0.4 multiply_convert_fusion.2
  167.9 0.1 pad_maximum_fusion.1
  168.0 11.9 %fusion.31 = f32[160,2560]{1,0:T(8,128)} fusion(bf16[160,5120]{1,0:T(8,128)(2,1)S(1)} %bitcast.48, bf16[2560,5120]{0,1:T(8,128)(2,1)} %pad_maximum_fusion), kind=kOutput, calls=%fused_computation.62 | convolution fusion | flops 4194304000 | bytes 29491200 | tf_op jit(solution)/shard_map/dot_general | solution.py:56
  179.9 2.0 copy.57
  181.9 0.0 copy-start.1
  181.9 10.4 %reshape.324 = f32[10,16,2,640,2]{1,0,4,3,2:T(8,128)} reshape(f32[160,2560]{0,1:T(8,128)S(1)} %copy.57) | data formatting | bytes 3276800 | tf_op jit(solution)/shard_map/reshape | solution.py:64
  192.3 0.0 copy-done.1
  192.3 13.1 %fusion = bf16[640,10,2,2,16]{4,1,2,0,3:T(8,128)(2,1)} fusion(f32[10,16,2,640,2]{1,0,4,3,2:T(8,128)} %reshape.324, f32[10,640,2]{0,2,1:T(2,128)S(1)} %copy-done.1, f32[2]{0:T(128)S(1)} %compare_select_fusion.4), kind=kLoop, calls=%fused_computation.4 | loop fusion | flops 1228800 | bytes 2508808 | tf_op jit(solution)/shard_map/transpose | solution.py:65
  205.4 9.2 %copy.59 = bf16[640,10,2,2,16]{0,4,3,2,1:T(8,128)(2,1)S(1)} copy(bf16[640,10,2,2,16]{4,1,2,0,3:T(8,128)(2,1)} %fusion) | data formatting | bytes 1638400 | tf_op jit(solution)/shard_map/transpose | solution.py:65
  214.6 0.0 copy-start.2
  214.7 1.4 reshape_reshape.3
  216.0 0.3 copy.60
  216.4 37.0 %all_to_all.23 = bf16[8,80,10,2,32]{1,4,3,2,0:T(8,128)(2,1)S(1)} all-to-all(bf16[8,80,10,2,32]{1,4,3,2,0:T(8,128)(2,1)S(1)} %copy.60), channel_id=1, replica_groups=mesh['lat'=8,'lev'=32] {'lat'}, dimensions={0} | all-to-all | bytes 1638400 | tf_op jit(solution)/shard_map/all_to_all | solution.py:165
  253.4 0.0 copy-done.2
  253.4 0.4 fusion.9
  253.8 0.3 pad_maximum_fusion.2
  254.1 5.2 %copy.61 = bf16[80,40,2,2,32]{1,4,3,2,0:T(8,128)(2,1)} copy(bf16[80,40,2,2,32]{0,4,2,1,3:T(8,128)(2,1)S(1)} %pad_maximum_fusion.2) | data formatting | bytes 1638400 | tf_op jit(solution)/shard_map/stack | solution.py:170
  259.3 17.9 %shard_map.47 = bf16[32,80,1281]{2,1,0:T(8,128)(2,1)} custom-call(bf16[80,40,1281]{2,1,0:T(8,128)(2,1)} %leg_ref.3, bf16[80,128,40]{2,1,0:T(8,128)(2,1)} %bitcast.44, s32[80,1,1281]{2,1,0:T(1,128)} %fusion.10.code_ref), custom_call_target="tpu_custom_call" | custom-call | tf_op jit(solution)/shard_map/pallas_call | solution.py:133
  277.2 0.0 reduce-scatter.2.cloned.1.call-update
  277.2 92.9 %reduce-scatter.2.cloned.1.call-done = bf16[1,80,1281]{2,1,0:T(8,128)(2,1)} async-done(((bf16[32,80,1281]{2,1,0:T(8,128)(2,1)}), bf16[1,80,1281]{2,1,0:T(8,128)(2,1)}) %reduce-scatter.2.cloned.1.call-update) | async-done | bytes 204976 | tf_op jit(solution)/shard_map/reduce_scatter | solution.py:176
  (9 shorter events, 0.1 us)
Async XLA Ops:
  6.5 61.6 %all-gather.2.cloned.1.call-start = ((), (), s32[]{:S(2)}) async-start(), calls=%async_computation.3 | async-start | bytes 7434240 | tf_op jit(solution)/shard_map/all_gather | solution.py:155
  90.9 41.8 %all-to-all-start = ((bf16[80,80,2,32]{0,3,2,1:T(8,128)(2,1)}), bf16[80,80,2,32]{0,3,2,1:T(8,128)(2,1)S(1)}, u32[]{:S(2)}, u32[]{:S(2)}) async-start(bf16[80,80,2,32]{0,3,2,1:T(8,128)(2,1)} %bitcast.1), calls=%async_computation | async-start | bytes 2621440 | tf_op jit(solution)/shard_map/all_to_all | solution.py:161
  98.0 272.2 %reduce-scatter.2.cloned.1.call-start = ((), (), s32[]{:S(2)}) async-start(), calls=%async_computation.4 | async-start | bytes 7434240 | tf_op jit(solution)/shard_map/reduce_scatter | solution.py:176
  98.2 18.2 %copy-start.3 = (s32[2,40]{1,0:T(2,128)S(1)}, s32[2,40]{1,0:T(2,128)}, u32[]{:S(2)}) copy-start(s32[2,40]{1,0:T(2,128)} %param.7) | copy-start | bytes 964
  145.4 5.8 %copy-start = (bf16[10,16,1280]{1,2,0:T(8,128)(2,1)S(1)}, bf16[10,16,1280]{1,2,0:T(8,128)(2,1)}, u32[]{:S(2)}) copy-start(bf16[10,16,1280]{1,2,0:T(8,128)(2,1)} %get-tuple-element.7) | copy-start | bytes 1228804
  181.9 10.5 %copy-start.1 = (f32[10,640,2]{0,2,1:T(2,128)S(1)}, f32[10,640,2]{0,2,1:T(2,128)}, u32[]{:S(2)}) copy-start(f32[10,640,2]{0,2,1:T(2,128)} %copy.58) | copy-start | bytes 153604
  214.6 38.8 %copy-start.2 = (f32[40]{0:T(128)S(1)}, f32[40]{0:T(128)}, u32[]{:S(2)}) copy-start(f32[40]{0:T(128)} %param.6) | copy-start | bytes 484
Sparse Core Ops, SparseCore 0:
  10.0 58.1 all-gather.1
  277.3 92.7 reduce-scatter.1

commit v6 on v3

--- a/solution.py
+++ b/solution.py
@@ -156,9 +156,10 @@
     first_pair = lax.axis_index("lat") * pair_count
     codes = slot_codes(first_pair, pair_count, packed)
     gathered = lax.all_gather(spec_in, "lev", axis=0, tiled=True)
+    table, wavenumbers = wave_tables(pair_count * groups, truncation)
+    gathered, table = lax.optimization_barrier((gathered, table))
     fourier = legendre_inverse(legendre, gathered, codes, block)
     fourier = fourier.reshape(pair_count, 2 * lat_count, 2, channels)
-    table, wavenumbers = wave_tables(pair_count * groups, truncation)
     local_rows = row_points.reshape(1, 2 * lat_count)
     band_lats = 2 * lat_count // groups
     lat_rows = lax.all_to_all(fourier, "lat", split_axis=1, concat_axis=0, tiled=True)

time: 367 us -> 367 us (level)
    all_gather x1, waiting for transfers between devices: 42.2 us -> 23.8 us  [local(): gathered = lax.all_gather(spec_in, 'lev', axis=0, tiled=True)]
    all_to_all x1, waiting for transfers between devices: 16.1 us -> 34.5 us  [local(): lax.all_to_all(fourier, 'lat', split_axis=1, concat_axis=0, tiled=True)]
where the time goes in v6:
time: 367 us; the launch traced here: 366 us
  waiting for transfers between devices  152 us (41%)
  local copies, waits for them, and re-layouts  53.2 us (14%)
  other arithmetic  41.1 us (11%)
  Pallas kernels  37.9 us (10%)
  blocking collectives  37 us (10%)
  matrix products  24.5 us (7%)
  between operations  13.6 us (4%)
  starting transfers between devices  7.05 us (2%)
    reduce_scatter x1, waiting for transfers between devices, local(): return lax.psum_scatter(partial, 'lev', scatter_dimension=0, tiled=True)  92.8 us
    all_to_all x1, blocking collectives, local(): lax.all_to_all(answered, 'lat', split_axis=0, concat_axis=0, tiled=True)  37 us
    all_to_all x1, waiting for transfers between devices, local(): lax.all_to_all(fourier, 'lat', split_axis=1, concat_axis=0, tiled=True)  34.5 us
    concatenate x4, local copies, waits for them, and re-layouts, fourier_work(): jnp.concatenate([real_out.reshape(lats, half_channels, waves), imag_out.r...  23.8 us
    all_gather x1, waiting for transfers between devices, local(): gathered = lax.all_gather(spec_in, 'lev', axis=0, tiled=True)  23.8 us
    pallas_call x1, Pallas kernels, legendre_inverse(): pl.pallas_call(inverse_kernel, grid=(pair_count // block,), in_specs=[pl....  20 us
    concatenate x1, other arithmetic, wave_tables(): table = lax.optimization_barrier(jnp.concatenate([cosines, sines], axis=0))  18.4 us
    pallas_call x1, Pallas kernels, legendre_direct(): pl.pallas_call(direct_kernel, grid=(pair_count // block,), in_specs=[pl.B...  18 us
  transfers between devices with their start and end apart: 3, of which 3 were waited for; matrix products, arithmetic and copies ran while one was open for 10% of the time, Pallas kernels for 0%

profile of v6, /device:TPU:2, one launch (start us, length us, event | category | flops | bytes accessed | tf_op | source)
XLA Modules:
  0.0 366.1 jit_solution(2513165414984400483)
XLA Ops:
  6.5 0.0 all-gather.2.cloned.1.call-start
  6.5 0.7 all-gather.2.cloned.1.call-update
  7.3 0.2 copy.69
  7.5 0.2 mul.223
  7.7 1.3 fusion.26
  9.0 1.7 fusion.19
  10.8 12.3 %subtract_convert_fusion = (bf16[1280,80,64]{0,2,1:T(8,128)(2,1)}, bf16[1280,80,64]{0,2,1:T(8,128)(2,1)}) fusion(f32[1280,64]{0,1:T(8,128)S(1)} %get-tuple-element.22, f32[1280,80]{0,1:T(8,128)S(1)} %get-tuple-element.20, f32[1280,64]{0,1:T(8,128)S(1)} %get-tuple-element.21, f32[1280,80]{0,1:T(8,128)S(1)} %get-tuple-element.19), kind=kLoop, calls=%fused_computation.2 | loop fusion | flops 52428800 | bytes 27688960 | tf_op jit(solution)/shard_map/convert_element_type | solution.py:28
  23.0 18.4 %pad_maximum_fusion = bf16[2560,5120]{0,1:T(8,128)(2,1)} fusion(bf16[1280,5120]{0,1:T(8,128)(2,1)} %bitcast.46, bf16[1280,5120]{0,1:T(8,128)(2,1)} %bitcast.45), kind=kLoop, calls=%fused_computation | loop fusion | flops 52428800 | bytes 52428800 | tf_op jit(solution)/shard_map/concatenate | solution.py:30
  41.5 2.9 fusion.11.code_ref
  44.4 23.8 %all-gather.2.cloned.1.call-done.spec_ref = bf16[32,80,1281]{2,1,0:T(8,128)(2,1)} async-done(((bf16[1,80,1281]{2,1,0:T(8,128)(2,1)}), bf16[32,80,1281]{2,1,0:T(8,128)(2,1)}) %all-gather.2.cloned.1.call-update) | async-done | bytes 6558736 | tf_op jit(solution)/shard_map/all_gather | solution.py:158
  68.2 20.0 %shard_map.46 = bf16[80,80,64]{2,1,0:T(8,128)(2,1)} custom-call(bf16[80,40,1281]{2,1,0:T(8,128)(2,1)} %leg_ref.3, bf16[32,80,1281]{2,1,0:T(8,128)(2,1)} %all-gather.2.cloned.1.call-done.spec_ref, s32[80,1,1281]{2,1,0:T(1,128)} %fusion.11.code_ref), custom_call_target="tpu_custom_call" | custom-call | tf_op jit(solution)/shard_map/pallas_call | solution.py:119
  88.1 0.0 copy-start.2
  88.1 2.8 copy.82
  91.0 7.0 %all-to-all-start = ((bf16[80,80,2,32]{0,3,2,1:T(8,128)(2,1)}), bf16[80,80,2,32]{0,3,2,1:T(8,128)(2,1)S(1)}, u32[]{:S(2)}, u32[]{:S(2)}) async-start(bf16[80,80,2,32]{0,3,2,1:T(8,128)(2,1)} %bitcast.3), calls=%async_computation | async-start | bytes 2621440 | tf_op jit(solution)/shard_map/all_to_all | solution.py:165
  98.0 0.0 reduce-scatter.2.cloned.1.call-start
  98.0 0.0 copy-done.2
  98.0 0.1 squeeze_reshape.3
  98.1 0.1 dynamic_slice.3
  98.2 0.1 fusion.29
  98.3 34.5 %all-to-all-done = bf16[80,80,2,32]{0,3,2,1:T(8,128)(2,1)S(1)} async-done(((bf16[80,80,2,32]{0,3,2,1:T(8,128)(2,1)}), bf16[80,80,2,32]{0,3,2,1:T(8,128)(2,1)S(1)}, u32[]{:S(2)}, u32[]{:S(2)}) %all-to-all-start) | async-done | bytes 819232 | tf_op jit(solution)/shard_map/all_to_all | solution.py:165
  132.7 1.0 copy.72
  133.7 1.2 all_to_all.19
  134.9 1.0 multiply_bitcast_fusion
  135.9 5.8 %copy.73 = bf16[10,32,640,2]{1,3,2,0:T(2,128)(2,1)S(1)} copy(bf16[10,32,640,2]{2,1,3,0:T(8,128)(2,1)} %multiply_bitcast_fusion) | data formatting | bytes 1638400 | tf_op jit(solution)/shard_map/transpose | solution.py:42
  141.7 3.9 %fusion.30 = (bf16[10,16,1280]{1,2,0:T(8,128)(2,1)}, bf16[10,16,1280]{1,2,0:T(8,128)(2,1)}) fusion(bf16[10,32,1280]{1,2,0:T(8,128)(2,1)S(1)} %bitcast.47), kind=kLoop, calls=%fused_computation.59 | loop fusion | bytes 1638400 | tf_op jit(solution)/shard_map/slice | solution.py:43
  145.6 0.0 copy-start
  145.6 4.0 %copy.83 = bf16[10,16,1280]{2,1,0:T(8,128)(2,1)} copy(bf16[10,16,1280]{1,2,0:T(8,128)(2,1)} %get-tuple-element.12) | data formatting | bytes 819200
  149.6 1.8 neg.6
  151.4 0.0 copy-done
  151.4 2.6 copy.74
  154.0 13.6 %convolution_multiply_fusion = f32[160,5120]{1,0:T(8,128)S(1)} fusion(bf16[2560,5120]{0,1:T(8,128)(2,1)} %pad_maximum_fusion, bf16[160,1280]{1,0:T(8,128)(2,1)} %bitcast.54, bf16[160,1280]{1,0:T(8,128)(2,1)} %bitcast.53), kind=kOutput, calls=%fused_computation.3 | convolution fusion | flops 4196761600 | bytes 30310400 | tf_op jit(solution)/shard_map/dot_general | solution.py:46
  167.7 0.4 multiply_convert_fusion.1
  168.0 0.1 pad_maximum_fusion.1
  168.2 10.8 %fusion.31 = f32[160,2560]{1,0:T(8,128)S(1)} fusion(bf16[160,5120]{1,0:T(8,128)(2,1)S(1)} %bitcast.52, bf16[2560,5120]{0,1:T(8,128)(2,1)} %pad_maximum_fusion), kind=kOutput, calls=%fused_computation.60 | convolution fusion | flops 4194304000 | bytes 29491200 | tf_op jit(solution)/shard_map/dot_general | solution.py:56
  179.0 0.1 slice_multiply_fusion.1
  179.2 0.4 copy.76
  179.6 5.9 %concatenate.25 = f32[10,16,640,2]{1,0,3,2:T(8,128)} reshape(f32[160,1280]{0,1:T(8,128)S(1)} %copy.76) | data formatting | bytes 1638400 | tf_op jit(solution)/shard_map/concatenate | solution.py:64
  185.5 6.0 %copy.78 = f32[10,16,640,2]{2,1,3,0:T(8,128)S(1)} copy(f32[10,16,640,2]{1,0,3,2:T(8,128)} %concatenate.25) | data formatting | bytes 1638400 | tf_op jit(solution)/shard_map/concatenate | solution.py:64
  191.5 0.4 copy.77
  191.9 5.9 %concatenate.26 = f32[10,16,640,2]{1,0,3,2:T(8,128)} reshape(f32[160,1280]{0,1:T(8,128)S(1)} %copy.77) | data formatting | bytes 1638400 | tf_op jit(solution)/shard_map/concatenate | solution.py:64
  197.8 6.0 %copy.79 = f32[10,16,640,2]{2,1,3,0:T(8,128)S(1)} copy(f32[10,16,640,2]{1,0,3,2:T(8,128)} %concatenate.26) | data formatting | bytes 1638400 | tf_op jit(solution)/shard_map/concatenate | solution.py:64
  203.8 0.2 fusion.1
  203.9 0.0 copy-start.1
  204.0 1.4 reshape.301
  205.3 0.3 copy.80
  205.7 37.0 %all_to_all.23 = bf16[8,80,10,2,32]{1,4,3,2,0:T(8,128)(2,1)S(1)} all-to-all(bf16[8,80,10,2,32]{1,4,3,2,0:T(8,128)(2,1)S(1)} %copy.80), channel_id=1, replica_groups=mesh['lat'=8,'lev'=32] {'lat'}, dimensions={0} | all-to-all | bytes 1638400 | tf_op jit(solution)/shard_map/all_to_all | solution.py:169
  242.7 0.0 copy-done.1
  242.7 0.4 fusion.10
  243.1 0.3 pad_maximum_fusion.2
  243.4 5.1 %copy.81 = bf16[80,40,2,2,32]{1,4,3,2,0:T(8,128)(2,1)} copy(bf16[80,40,2,2,32]{0,4,2,1,3:T(8,128)(2,1)S(1)} %pad_maximum_fusion.2) | data formatting | bytes 1638400 | tf_op jit(solution)/shard_map/stack | solution.py:174
  248.5 18.0 %shard_map.47 = bf16[32,80,1281]{2,1,0:T(8,128)(2,1)} custom-call(bf16[80,40,1281]{2,1,0:T(8,128)(2,1)} %leg_ref.3, bf16[80,128,40]{2,1,0:T(8,128)(2,1)} %bitcast.48, s32[80,1,1281]{2,1,0:T(1,128)} %fusion.11.code_ref), custom_call_target="tpu_custom_call" | custom-call | tf_op jit(solution)/shard_map/pallas_call | solution.py:136
  266.5 0.0 reduce-scatter.2.cloned.1.call-update
  266.5 92.8 %reduce-scatter.2.cloned.1.call-done = bf16[1,80,1281]{2,1,0:T(8,128)(2,1)} async-done(((bf16[32,80,1281]{2,1,0:T(8,128)(2,1)}), bf16[1,80,1281]{2,1,0:T(8,128)(2,1)}) %reduce-scatter.2.cloned.1.call-update) | async-done | bytes 204976 | tf_op jit(solution)/shard_map/reduce_scatter | solution.py:180
  (5 shorter events, 0.0 us)
Async XLA Ops:
  6.5 61.6 %all-gather.2.cloned.1.call-start = ((), (), s32[]{:S(2)}) async-start(), calls=%async_computation.3 | async-start | bytes 7434240 | tf_op jit(solution)/shard_map/all_gather | solution.py:158
  88.1 9.9 %copy-start.2 = (s32[2,40]{1,0:T(2,128)S(1)}, s32[2,40]{1,0:T(2,128)}, u32[]{:S(2)}) copy-start(s32[2,40]{1,0:T(2,128)} %param.7) | copy-start | bytes 964
  91.0 41.8 %all-to-all-start = ((bf16[80,80,2,32]{0,3,2,1:T(8,128)(2,1)}), bf16[80,80,2,32]{0,3,2,1:T(8,128)(2,1)S(1)}, u32[]{:S(2)}, u32[]{:S(2)}) async-start(bf16[80,80,2,32]{0,3,2,1:T(8,128)(2,1)} %bitcast.3), calls=%async_computation | async-start | bytes 2621440 | tf_op jit(solution)/shard_map/all_to_all | solution.py:165
  98.0 261.3 %reduce-scatter.2.cloned.1.call-start = ((), (), s32[]{:S(2)}) async-start(), calls=%async_computation.4 | async-start | bytes 7434240 | tf_op jit(solution)/shard_map/reduce_scatter | solution.py:180
  145.6 5.8 %copy-start = (bf16[10,16,1280]{1,2,0:T(8,128)(2,1)S(1)}, bf16[10,16,1280]{1,2,0:T(8,128)(2,1)}, u32[]{:S(2)}) copy-start(bf16[10,16,1280]{1,2,0:T(8,128)(2,1)} %get-tuple-element.11) | copy-start | bytes 1228804
  203.9 38.8 %copy-start.1 = (f32[40]{0:T(128)S(1)}, f32[40]{0:T(128)}, u32[]{:S(2)}) copy-start(f32[40]{0:T(128)} %param.6) | copy-start | bytes 484
Sparse Core Ops, SparseCore 0:
  10.0 58.1 all-gather.1
  266.6 92.5 reduce-scatter.1

commit v7 on v6

--- a/solution.py
+++ b/solution.py
@@ -42,7 +42,7 @@
     flat = jnp.transpose(masked, (1, 3, 0, 2)).reshape(lats, channels, waves)
     real_part = flat[:, :half_channels].reshape(rows, waves)
     imag_part = flat[:, half_channels:].reshape(rows, waves)
-    lhs = jnp.concatenate([real_part, -imag_part], axis=1)
+    lhs = jnp.concatenate([real_part, imag_part], axis=1)
     grid_values = jnp.dot(lhs, table, preferred_element_type=jnp.float32) * (
         1.0 / math.sqrt(truncation + 1)
     )
@@ -84,6 +84,8 @@
     for pp in range(block):
         legendre_pair = leg_ref[pp]
         spectrum = spec_ref[:, pp, :]
+        rows = lax.broadcasted_iota(jnp.int32, spectrum.shape, 0)
+        spectrum = jnp.where(rows < spectrum.shape[0] // 2, spectrum, -spectrum)
         code = code_ref[pp]
         slot = code // 2
         sign = (1 - 2 * (code % 2)).astype(spectrum.dtype)

time: 367 us -> 375 us (1.022)
  Pallas kernels: 37.9 us -> 48.3 us
    pallas_call x1, Pallas kernels: 20 us -> 30.4 us  [legendre_inverse(): pl.pallas_call(inverse_kernel, grid=(pair_count // block,), in_specs=[pl....]
    unnamed x7 -> x6, local copies, waits for them, and re-layouts: 4.01 us -> 0.01 us
where the time goes in v7:
time: 375 us
  waiting for transfers between devices  152 us (41%)
  local copies, waits for them, and re-layouts  53.2 us (14%)
  Pallas kernels  48.3 us (13%)
  other arithmetic  39.2 us (10%)
  blocking collectives  37 us (10%)
  matrix products  24.5 us (7%)
  between operations  13.6 us (4%)
  starting transfers between devices  7.05 us (2%)
    reduce_scatter x1, waiting for transfers between devices, local(): return lax.psum_scatter(partial, 'lev', scatter_dimension=0, tiled=True)  92.9 us
    all_to_all x1, blocking collectives, local(): lax.all_to_all(answered, 'lat', split_axis=0, concat_axis=0, tiled=True)  37 us
    all_to_all x1, waiting for transfers between devices, local(): lax.all_to_all(fourier, 'lat', split_axis=1, concat_axis=0, tiled=True)  34.5 us
    pallas_call x1, Pallas kernels, legendre_inverse(): pl.pallas_call(inverse_kernel, grid=(pair_count // block,), in_specs=[pl....  30.4 us
    concatenate x4, local copies, waits for them, and re-layouts, fourier_work(): jnp.concatenate([real_out.reshape(lats, half_channels, waves), imag_out.r...  23.8 us
    all_gather x1, waiting for transfers between devices, local(): gathered = lax.all_gather(spec_in, 'lev', axis=0, tiled=True)  23.8 us
    concatenate x1, other arithmetic, wave_tables(): table = lax.optimization_barrier(jnp.concatenate([cosines, sines], axis=0))  18.4 us
    pallas_call x1, Pallas kernels, legendre_direct(): pl.pallas_call(direct_kernel, grid=(pair_count // block,), in_specs=[pl.B...  18 us
  transfers between devices with their start and end apart: 3, of which 3 were waited for; matrix products, arithmetic and copies ran while one was open for 10% of the time, Pallas kernels for 0%

profile of v7, /device:TPU:2, one launch (start us, length us, event | category | flops | bytes accessed | tf_op | source)
XLA Modules:
  0.0 374.8 jit_solution(7983645970101660505)
XLA Ops:
  6.5 0.0 all-gather.2.cloned.1.call-start
  6.5 0.7 all-gather.2.cloned.1.call-update
  7.3 0.2 copy.56
  7.5 0.2 mul.223
  7.7 1.3 fusion.26
  9.0 1.7 fusion.19
  10.8 12.3 %subtract_convert_fusion = (bf16[1280,80,64]{0,2,1:T(8,128)(2,1)}, bf16[1280,80,64]{0,2,1:T(8,128)(2,1)}) fusion(f32[1280,64]{0,1:T(8,128)S(1)} %get-tuple-element.22, f32[1280,80]{0,1:T(8,128)S(1)} %get-tuple-element.20, f32[1280,64]{0,1:T(8,128)S(1)} %get-tuple-element.21, f32[1280,80]{0,1:T(8,128)S(1)} %get-tuple-element.19), kind=kLoop, calls=%fused_computation.2 | loop fusion | flops 52428800 | bytes 27688960 | tf_op jit(solution)/shard_map/convert_element_type | solution.py:28
  23.0 18.4 %pad_maximum_fusion = bf16[2560,5120]{0,1:T(8,128)(2,1)} fusion(bf16[1280,5120]{0,1:T(8,128)(2,1)} %bitcast.46, bf16[1280,5120]{0,1:T(8,128)(2,1)} %bitcast.45), kind=kLoop, calls=%fused_computation | loop fusion | flops 52428800 | bytes 52428800 | tf_op jit(solution)/shard_map/concatenate | solution.py:30
  41.5 2.9 fusion.11.code_ref
  44.4 23.8 %all-gather.2.cloned.1.call-done.spec_ref = bf16[32,80,1281]{2,1,0:T(8,128)(2,1)} async-done(((bf16[1,80,1281]{2,1,0:T(8,128)(2,1)}), bf16[32,80,1281]{2,1,0:T(8,128)(2,1)}) %all-gather.2.cloned.1.call-update) | async-done | bytes 6558736 | tf_op jit(solution)/shard_map/all_gather | solution.py:160
  68.2 30.4 %shard_map.46 = bf16[80,80,64]{2,1,0:T(8,128)(2,1)} custom-call(bf16[80,40,1281]{2,1,0:T(8,128)(2,1)} %leg_ref.3, bf16[32,80,1281]{2,1,0:T(8,128)(2,1)} %all-gather.2.cloned.1.call-done.spec_ref, s32[80,1,1281]{2,1,0:T(1,128)} %fusion.11.code_ref), custom_call_target="tpu_custom_call" | custom-call | tf_op jit(solution)/shard_map/pallas_call | solution.py:121
  98.5 0.0 copy-start.2
  98.5 2.8 copy.69
  101.4 7.0 %all-to-all-start = ((bf16[80,80,2,32]{0,3,2,1:T(8,128)(2,1)}), bf16[80,80,2,32]{0,3,2,1:T(8,128)(2,1)S(1)}, u32[]{:S(2)}, u32[]{:S(2)}) async-start(bf16[80,80,2,32]{0,3,2,1:T(8,128)(2,1)} %bitcast.3), calls=%async_computation | async-start | bytes 2621440 | tf_op jit(solution)/shard_map/all_to_all | solution.py:167
  108.4 0.0 reduce-scatter.2.cloned.1.call-start
  108.4 0.0 copy-done.2
  108.4 0.1 squeeze_reshape.3
  108.5 0.1 dynamic_slice.3
  108.6 0.1 fusion.29
  108.7 34.5 %all-to-all-done = bf16[80,80,2,32]{0,3,2,1:T(8,128)(2,1)S(1)} async-done(((bf16[80,80,2,32]{0,3,2,1:T(8,128)(2,1)}), bf16[80,80,2,32]{0,3,2,1:T(8,128)(2,1)S(1)}, u32[]{:S(2)}, u32[]{:S(2)}) %all-to-all-start) | async-done | bytes 819232 | tf_op jit(solution)/shard_map/all_to_all | solution.py:167
  143.1 1.0 copy.59
  144.1 1.2 all_to_all.19
  145.3 1.0 multiply_bitcast_fusion
  146.3 5.8 %copy.60 = bf16[10,32,640,2]{1,3,2,0:T(2,128)(2,1)S(1)} copy(bf16[10,32,640,2]{2,1,3,0:T(8,128)(2,1)} %multiply_bitcast_fusion) | data formatting | bytes 1638400 | tf_op jit(solution)/shard_map/transpose | solution.py:42
  152.1 3.9 %fusion.30 = (bf16[10,16,1280]{1,2,0:T(8,128)(2,1)}, bf16[10,16,1280]{1,2,0:T(8,128)(2,1)}) fusion(bf16[10,32,1280]{1,2,0:T(8,128)(2,1)S(1)} %bitcast.47), kind=kLoop, calls=%fused_computation.59 | loop fusion | bytes 1638400 | tf_op jit(solution)/shard_map/slice | solution.py:43
  156.0 0.0 copy-start
  156.0 4.0 %copy.61 = bf16[10,16,1280]{2,1,0:T(8,128)(2,1)} copy(bf16[10,16,1280]{1,2,0:T(8,128)(2,1)} %get-tuple-element.11) | data formatting | bytes 819200 | tf_op jit(solution)/shard_map/slice | solution.py:43
  160.0 0.0 copy-done
  160.0 2.6 copy.62
  162.6 13.6 %convolution_multiply_fusion = f32[160,5120]{1,0:T(8,128)S(1)} fusion(bf16[2560,5120]{0,1:T(8,128)(2,1)} %pad_maximum_fusion, bf16[160,1280]{1,0:T(8,128)(2,1)} %bitcast.54, bf16[160,1280]{1,0:T(8,128)(2,1)} %bitcast.53), kind=kOutput, calls=%fused_computation.3 | convolution fusion | flops 4196761600 | bytes 30310400 | tf_op jit(solution)/shard_map/dot_general | solution.py:46
  176.3 0.4 multiply_convert_fusion.1
  176.6 0.1 pad_maximum_fusion.1
  176.8 10.8 %fusion.31 = f32[160,2560]{1,0:T(8,128)S(1)} fusion(bf16[160,5120]{1,0:T(8,128)(2,1)S(1)} %bitcast.52, bf16[2560,5120]{0,1:T(8,128)(2,1)} %pad_maximum_fusion), kind=kOutput, calls=%fused_computation.60 | convolution fusion | flops 4194304000 | bytes 29491200 | tf_op jit(solution)/shard_map/dot_general | solution.py:56
  187.6 0.1 slice_multiply_fusion.1
  187.7 0.4 copy.63
  188.1 5.9 %concatenate.25 = f32[10,16,640,2]{1,0,3,2:T(8,128)} reshape(f32[160,1280]{0,1:T(8,128)S(1)} %copy.63) | data formatting | bytes 1638400 | tf_op jit(solution)/shard_map/concatenate | solution.py:64
  194.1 6.0 %copy.65 = f32[10,16,640,2]{2,1,3,0:T(8,128)S(1)} copy(f32[10,16,640,2]{1,0,3,2:T(8,128)} %concatenate.25) | data formatting | bytes 1638400 | tf_op jit(solution)/shard_map/concatenate | solution.py:64
  200.0 0.4 copy.64
  200.5 5.9 %concatenate.26 = f32[10,16,640,2]{1,0,3,2:T(8,128)} reshape(f32[160,1280]{0,1:T(8,128)S(1)} %copy.64) | data formatting | bytes 1638400 | tf_op jit(solution)/shard_map/concatenate | solution.py:64
  206.4 6.0 %copy.66 = f32[10,16,640,2]{2,1,3,0:T(8,128)S(1)} copy(f32[10,16,640,2]{1,0,3,2:T(8,128)} %concatenate.26) | data formatting | bytes 1638400 | tf_op jit(solution)/shard_map/concatenate | solution.py:64
  212.4 0.2 fusion.1
  212.5 0.0 copy-start.1
  212.5 1.4 reshape.303
  213.9 0.3 copy.67
  214.3 37.0 %all_to_all.23 = bf16[8,80,10,2,32]{1,4,3,2,0:T(8,128)(2,1)S(1)} all-to-all(bf16[8,80,10,2,32]{1,4,3,2,0:T(8,128)(2,1)S(1)} %copy.67), channel_id=1, replica_groups=mesh['lat'=8,'lev'=32] {'lat'}, dimensions={0} | all-to-all | bytes 1638400 | tf_op jit(solution)/shard_map/all_to_all | solution.py:171
  251.3 0.0 copy-done.1
  251.3 0.4 fusion.10
  251.7 0.3 pad_maximum_fusion.2
  252.0 5.1 %copy.68 = bf16[80,40,2,2,32]{1,4,3,2,0:T(8,128)(2,1)} copy(bf16[80,40,2,2,32]{0,4,2,1,3:T(8,128)(2,1)S(1)} %pad_maximum_fusion.2) | data formatting | bytes 1638400 | tf_op jit(solution)/shard_map/stack | solution.py:176
  257.1 18.0 %shard_map.47 = bf16[32,80,1281]{2,1,0:T(8,128)(2,1)} custom-call(bf16[80,40,1281]{2,1,0:T(8,128)(2,1)} %leg_ref.3, bf16[80,128,40]{2,1,0:T(8,128)(2,1)} %bitcast.48, s32[80,1,1281]{2,1,0:T(1,128)} %fusion.11.code_ref), custom_call_target="tpu_custom_call" | custom-call | tf_op jit(solution)/shard_map/pallas_call | solution.py:138
  275.0 0.0 reduce-scatter.2.cloned.1.call-update
  275.1 92.9 %reduce-scatter.2.cloned.1.call-done = bf16[1,80,1281]{2,1,0:T(8,128)(2,1)} async-done(((bf16[32,80,1281]{2,1,0:T(8,128)(2,1)}), bf16[1,80,1281]{2,1,0:T(8,128)(2,1)}) %reduce-scatter.2.cloned.1.call-update) | async-done | bytes 204976 | tf_op jit(solution)/shard_map/reduce_scatter | solution.py:182
  (5 shorter events, 0.0 us)
Async XLA Ops:
  6.5 61.6 %all-gather.2.cloned.1.call-start = ((), (), s32[]{:S(2)}) async-start(), calls=%async_computation.3 | async-start | bytes 7434240 | tf_op jit(solution)/shard_map/all_gather | solution.py:160
  98.5 9.9 %copy-start.2 = (s32[2,40]{1,0:T(2,128)S(1)}, s32[2,40]{1,0:T(2,128)}, u32[]{:S(2)}) copy-start(s32[2,40]{1,0:T(2,128)} %param.7) | copy-start | bytes 964
  101.4 41.8 %all-to-all-start = ((bf16[80,80,2,32]{0,3,2,1:T(8,128)(2,1)}), bf16[80,80,2,32]{0,3,2,1:T(8,128)(2,1)S(1)}, u32[]{:S(2)}, u32[]{:S(2)}) async-start(bf16[80,80,2,32]{0,3,2,1:T(8,128)(2,1)} %bitcast.3), calls=%async_computation | async-start | bytes 2621440 | tf_op jit(solution)/shard_map/all_to_all | solution.py:167
  108.4 259.6 %reduce-scatter.2.cloned.1.call-start = ((), (), s32[]{:S(2)}) async-start(), calls=%async_computation.4 | async-start | bytes 7434240 | tf_op jit(solution)/shard_map/reduce_scatter | solution.py:182
  156.0 4.0 %copy-start = (bf16[10,16,1280]{1,2,0:T(8,128)(2,1)S(1)}, bf16[10,16,1280]{1,2,0:T(8,128)(2,1)}, u32[]{:S(2)}) copy-start(bf16[10,16,1280]{1,2,0:T(8,128)(2,1)} %get-tuple-element.12) | copy-start | bytes 1228804
  212.5 38.8 %copy-start.1 = (f32[40]{0:T(128)S(1)}, f32[40]{0:T(128)}, u32[]{:S(2)}) copy-start(f32[40]{0:T(128)} %param.6) | copy-start | bytes 484
Sparse Core Ops, SparseCore 0:
  10.0 58.1 all-gather.1
  275.2 92.7 reduce-scatter.1

commit v8 on v6

--- a/solution.py
+++ b/solution.py
@@ -78,19 +78,14 @@
     return (2 * in_second + degree % 2).reshape(pair_count, 1, packed)
 
 
-def inverse_kernel(leg_ref, spec_ref, code_ref, out_ref):
+def inverse_kernel(leg_ref, spec_ref, factor_ref, out_ref):
     block = leg_ref.shape[0]
 
     for pp in range(block):
         legendre_pair = leg_ref[pp]
         spectrum = spec_ref[:, pp, :]
-        code = code_ref[pp]
-        slot = code // 2
-        sign = (1 - 2 * (code % 2)).astype(spectrum.dtype)
-        zero = jnp.zeros_like(spectrum)
-        first = jnp.where(slot == 0, spectrum, zero)
-        second = jnp.where(slot == 1, spectrum, zero)
-        masked = jnp.concatenate([first, second, first * sign, second * sign], axis=0)
+        factors = factor_ref[pp]
+        masked = jnp.concatenate([spectrum * factors[x : x + 1] for x in range(4)], axis=0)
         sums = lax.dot_general(
             legendre_pair, masked, (((1,), (1,)), ((), ())), preferred_element_type=jnp.float32
         )
@@ -122,7 +117,7 @@
         in_specs=[
             pl.BlockSpec((block, lat_count, packed), lambda i: (i, 0, 0)),
             pl.BlockSpec((channels, block, packed), lambda i: (0, i, 0)),
-            pl.BlockSpec((block, 1, packed), lambda i: (i, 0, 0)),
+            pl.BlockSpec((block, 4, packed), lambda i: (i, 0, 0)),
         ],
         out_specs=pl.BlockSpec((block, 2 * lat_count, 2 * channels), lambda i: (i, 0, 0)),
         out_shape=jax.ShapeDtypeStruct((pair_count, 2 * lat_count, 2 * channels), jnp.bfloat16),
@@ -158,7 +153,12 @@
     gathered = lax.all_gather(spec_in, "lev", axis=0, tiled=True)
     table, wavenumbers = wave_tables(pair_count * groups, truncation)
     gathered, table = lax.optimization_barrier((gathered, table))
-    fourier = legendre_inverse(legendre, gathered, codes, block)
+    slots = codes // 2
+    signs = 1 - 2 * (codes % 2)
+    factors = jnp.concatenate(
+        [(slots == 0), (slots == 1), (slots == 0) * signs, (slots == 1) * signs], axis=1
+    ).astype(jnp.bfloat16)
+    fourier = legendre_inverse(legendre, gathered, factors, block)
     fourier = fourier.reshape(pair_count, 2 * lat_count, 2, channels)
     local_rows = row_points.reshape(1, 2 * lat_count)
     band_lats = 2 * lat_count // groups

time: 367 us -> 366 us (level)
  waiting for transfers between devices: 152 us -> 139 us
  other arithmetic: 41.1 us -> 53.3 us
    all_gather x1, waiting for transfers between devices: 23.8 us -> 11.5 us  [local(): gathered = lax.all_gather(spec_in, 'lev', axis=0, tiled=True)]
    another operation x1 -> x2, other arithmetic: 0.36 us -> 5.12 us
    add x1, other arithmetic: 2.89 us -> 6.98 us  [slot_codes(): return (2 * in_second + degree % 2).reshape(pair_count, 1, packed)]
  transfers between devices with their start and end apart: 3 -> 3, of which waited for: 3 -> 3; matrix products, arithmetic and copies ran while one was open for 10% -> 14% of each run, Pallas kernels for 0% -> 0%
where the time goes in v8:
time: 366 us; the launch traced here: 365 us
  waiting for transfers between devices  139 us (38%)
  other arithmetic  53.3 us (15%)
  local copies, waits for them, and re-layouts  53.3 us (15%)
  blocking collectives  37.2 us (10%)
  Pallas kernels  36.8 us (10%)
  matrix products  24.5 us (7%)
  between operations  13.6 us (4%)
  starting transfers between devices  7.19 us (2%)
    reduce_scatter x1, waiting for transfers between devices, local(): return lax.psum_scatter(partial, 'lev', scatter_dimension=0, tiled=True)  92.5 us
    all_to_all x1, blocking collectives, local(): lax.all_to_all(answered, 'lat', split_axis=0, concat_axis=0, tiled=True)  37.2 us
    all_to_all x1, waiting for transfers between devices, local(): lax.all_to_all(fourier, 'lat', split_axis=1, concat_axis=0, tiled=True)  34.5 us
    concatenate x4, local copies, waits for them, and re-layouts, fourier_work(): jnp.concatenate([real_out.reshape(lats, half_channels, waves), imag_out.r...  23.8 us
    pallas_call x1, Pallas kernels, legendre_inverse(): pl.pallas_call(inverse_kernel, grid=(pair_count // block,), in_specs=[pl....  18.9 us
    concatenate x1, other arithmetic, wave_tables(): table = lax.optimization_barrier(jnp.concatenate([cosines, sines], axis=0))  18.5 us
    pallas_call x1, Pallas kernels, legendre_direct(): pl.pallas_call(direct_kernel, grid=(pair_count // block,), in_specs=[pl.B...  18 us
    dot_general x1, matrix products, fourier_work(): jnp.dot(lhs, table, preferred_element_type=jnp.float32)  13.6 us
  transfers between devices with their start and end apart: 3, of which 3 were waited for; matrix products, arithmetic and copies ran while one was open for 14% of the time, Pallas kernels for 0%

profile of v8, /device:TPU:2, one launch (start us, length us, event | category | flops | bytes accessed | tf_op | source)
XLA Modules:
  0.0 365.2 jit_solution(3327834728116799166)
XLA Ops:
  6.5 0.0 all-gather.2.cloned.1.call-start
  6.5 0.7 all-gather.2.cloned.1.call-update
  7.3 0.2 copy.69
  7.5 0.2 mul.245
  7.7 1.3 fusion.32
  9.0 1.7 fusion.25
  10.8 12.6 %subtract_convert_fusion = (bf16[1280,80,64]{0,2,1:T(8,128)(2,1)}, bf16[1280,80,64]{0,2,1:T(8,128)(2,1)}) fusion(f32[1280,64]{0,1:T(8,128)S(1)} %get-tuple-element.22, f32[1280,80]{0,1:T(8,128)S(1)} %get-tuple-element.20, f32[1280,64]{0,1:T(8,128)S(1)} %get-tuple-element.21, f32[1280,80]{0,1:T(8,128)S(1)} %get-tuple-element.19), kind=kLoop, calls=%fused_computation.2 | loop fusion | flops 52428800 | bytes 27688960 | tf_op jit(solution)/shard_map/convert_element_type | solution.py:28
  23.4 18.5 %pad_maximum_fusion = bf16[2560,5120]{0,1:T(8,128)(2,1)} fusion(bf16[1280,5120]{0,1:T(8,128)(2,1)} %bitcast.46, bf16[1280,5120]{0,1:T(8,128)(2,1)} %bitcast.45), kind=kLoop, calls=%fused_computation | loop fusion | flops 52428800 | bytes 52428800 | tf_op jit(solution)/shard_map/concatenate | solution.py:30
  41.9 4.8 %fusion.13 = (bf16[80,1,1281]{2,1,0:T(2,128)(2,1)S(1)}, bf16[80,1,1281]{2,1,0:T(2,128)(2,1)S(1)}) fusion(s32[80]{0:T(128)S(1)} %add_subtract_fusion), kind=kLoop, calls=%fused_computation.44 | loop fusion | flops 3791760 | bytes 410240 | tf_op jit(solution)/shard_map/convert.6
  46.6 7.0 %fusion.11 = (s32[80,1,1281]{2,1,0:T(1,128)}, bf16[80,1,1281]{2,1,0:T(2,128)(2,1)S(1)}, bf16[80,1,1281]{2,1,0:T(2,128)(2,1)S(1)}) fusion(s32[80]{0:T(128)S(1)} %add_subtract_fusion), kind=kLoop, calls=%fused_computation.42 | loop fusion | flops 4406640 | bytes 820160 | tf_op jit(solution)/shard_map/add | solution.py:78
  53.6 3.0 pad_maximum_fusion.3.factor_ref
  56.7 11.5 %all-gather.2.cloned.1.call-done.spec_ref = bf16[32,80,1281]{2,1,0:T(8,128)(2,1)} async-done(((bf16[1,80,1281]{2,1,0:T(8,128)(2,1)}), bf16[32,80,1281]{2,1,0:T(8,128)(2,1)}) %all-gather.2.cloned.1.call-update) | async-done | bytes 6558736 | tf_op jit(solution)/shard_map/all_gather | solution.py:153
  68.2 18.9 %shard_map.46 = bf16[80,80,64]{2,1,0:T(8,128)(2,1)} custom-call(bf16[80,40,1281]{2,1,0:T(8,128)(2,1)} %leg_ref.3, bf16[32,80,1281]{2,1,0:T(8,128)(2,1)} %all-gather.2.cloned.1.call-done.spec_ref, bf16[80,4,1281]{2,1,0:T(4,128)(2,1)} %pad_maximum_fusion.3.factor_ref), custom_call_target="tpu_custom_call" | custom-call | tf_op jit(solution)/shard_map/pallas_call | solution.py:114
  87.0 2.8 copy.82
  89.8 0.0 copy-start.2
  89.9 7.1 %all-to-all-start = ((bf16[80,80,2,32]{0,3,2,1:T(8,128)(2,1)}), bf16[80,80,2,32]{0,3,2,1:T(8,128)(2,1)S(1)}, u32[]{:S(2)}, u32[]{:S(2)}) async-start(bf16[80,80,2,32]{0,3,2,1:T(8,128)(2,1)} %bitcast.3), calls=%async_computation | async-start | bytes 2621440 | tf_op jit(solution)/shard_map/all_to_all | solution.py:165
  97.0 0.0 reduce-scatter.2.cloned.1.call-start
  97.0 0.0 copy-done.2
  97.1 0.1 squeeze_reshape.3
  97.1 0.1 dynamic_slice.3
  97.2 0.1 fusion.35
  97.3 34.5 %all-to-all-done = bf16[80,80,2,32]{0,3,2,1:T(8,128)(2,1)S(1)} async-done(((bf16[80,80,2,32]{0,3,2,1:T(8,128)(2,1)}), bf16[80,80,2,32]{0,3,2,1:T(8,128)(2,1)S(1)}, u32[]{:S(2)}, u32[]{:S(2)}) %all-to-all-start) | async-done | bytes 819232 | tf_op jit(solution)/shard_map/all_to_all | solution.py:165
  131.8 1.0 copy.72
  132.7 1.2 all_to_all.19
  134.0 1.0 multiply_bitcast_fusion
  135.0 5.8 %copy.73 = bf16[10,32,640,2]{1,3,2,0:T(2,128)(2,1)S(1)} copy(bf16[10,32,640,2]{2,1,3,0:T(8,128)(2,1)} %multiply_bitcast_fusion) | data formatting | bytes 1638400 | tf_op jit(solution)/shard_map/transpose | solution.py:42
  140.7 3.9 %fusion.36 = (bf16[10,16,1280]{1,2,0:T(8,128)(2,1)}, bf16[10,16,1280]{1,2,0:T(8,128)(2,1)}) fusion(bf16[10,32,1280]{1,2,0:T(8,128)(2,1)S(1)} %bitcast.47), kind=kLoop, calls=%fused_computation.75 | loop fusion | bytes 1638400 | tf_op jit(solution)/shard_map/slice | solution.py:43
  144.6 0.0 copy-start
  144.6 4.0 %copy.83 = bf16[10,16,1280]{2,1,0:T(8,128)(2,1)} copy(bf16[10,16,1280]{1,2,0:T(8,128)(2,1)} %get-tuple-element.12) | data formatting | bytes 819200
  148.6 1.8 neg.6
  150.4 0.0 copy-done
  150.4 2.6 copy.74
  153.1 13.6 %convolution_multiply_fusion = f32[160,5120]{1,0:T(8,128)S(1)} fusion(bf16[2560,5120]{0,1:T(8,128)(2,1)} %pad_maximum_fusion, bf16[160,1280]{1,0:T(8,128)(2,1)} %bitcast.54, bf16[160,1280]{1,0:T(8,128)(2,1)} %bitcast.53), kind=kOutput, calls=%fused_computation.3 | convolution fusion | flops 4196761600 | bytes 30310400 | tf_op jit(solution)/shard_map/dot_general | solution.py:46
  166.7 0.4 multiply_convert_fusion.1
  167.1 0.1 pad_maximum_fusion.1
  167.2 10.8 %fusion.37 = f32[160,2560]{1,0:T(8,128)S(1)} fusion(bf16[160,5120]{1,0:T(8,128)(2,1)S(1)} %bitcast.52, bf16[2560,5120]{0,1:T(8,128)(2,1)} %pad_maximum_fusion), kind=kOutput, calls=%fused_computation.76 | convolution fusion | flops 4194304000 | bytes 29491200 | tf_op jit(solution)/shard_map/dot_general | solution.py:56
  178.1 0.1 slice_multiply_fusion.1
  178.2 0.4 copy.76
  178.6 5.9 %concatenate.30 = f32[10,16,640,2]{1,0,3,2:T(8,128)} reshape(f32[160,1280]{0,1:T(8,128)S(1)} %copy.76) | data formatting | bytes 1638400 | tf_op jit(solution)/shard_map/concatenate | solution.py:64
  184.6 6.0 %copy.78 = f32[10,16,640,2]{2,1,3,0:T(8,128)S(1)} copy(f32[10,16,640,2]{1,0,3,2:T(8,128)} %concatenate.30) | data formatting | bytes 1638400 | tf_op jit(solution)/shard_map/concatenate | solution.py:64
  190.5 0.4 copy.77
  191.0 5.9 %concatenate.31 = f32[10,16,640,2]{1,0,3,2:T(8,128)} reshape(f32[160,1280]{0,1:T(8,128)S(1)} %copy.77) | data formatting | bytes 1638400 | tf_op jit(solution)/shard_map/concatenate | solution.py:64
  196.9 6.0 %copy.79 = f32[10,16,640,2]{2,1,3,0:T(8,128)S(1)} copy(f32[10,16,640,2]{1,0,3,2:T(8,128)} %concatenate.31) | data formatting | bytes 1638400 | tf_op jit(solution)/shard_map/concatenate | solution.py:64
  202.9 0.2 fusion.1
  203.0 1.4 reshape.589
  204.4 0.3 copy.80
  204.8 0.0 copy-start.1
  204.8 37.2 %all_to_all.23 = bf16[8,80,10,2,32]{1,4,3,2,0:T(8,128)(2,1)S(1)} all-to-all(bf16[8,80,10,2,32]{1,4,3,2,0:T(8,128)(2,1)S(1)} %copy.80), channel_id=1, replica_groups=mesh['lat'=8,'lev'=32] {'lat'}, dimensions={0} | all-to-all | bytes 1638400 | tf_op jit(solution)/shard_map/all_to_all | solution.py:169
  242.0 0.0 copy-done.1
  242.0 0.4 fusion.10
  242.4 0.3 pad_maximum_fusion.2
  242.7 5.1 %copy.81 = bf16[80,40,2,2,32]{1,4,3,2,0:T(8,128)(2,1)} copy(bf16[80,40,2,2,32]{0,4,2,1,3:T(8,128)(2,1)S(1)} %pad_maximum_fusion.2) | data formatting | bytes 1638400 | tf_op jit(solution)/shard_map/stack | solution.py:174
  247.8 18.0 %shard_map.47 = bf16[32,80,1281]{2,1,0:T(8,128)(2,1)} custom-call(bf16[80,40,1281]{2,1,0:T(8,128)(2,1)} %leg_ref.3, bf16[80,128,40]{2,1,0:T(8,128)(2,1)} %bitcast.48, s32[80,1,1281]{2,1,0:T(1,128)} %get-tuple-element.27.code_ref), custom_call_target="tpu_custom_call" | custom-call | tf_op jit(solution)/shard_map/pallas_call | solution.py:131
  265.8 0.0 reduce-scatter.2.cloned.1.call-update
  265.8 92.5 %reduce-scatter.2.cloned.1.call-done = bf16[1,80,1281]{2,1,0:T(8,128)(2,1)} async-done(((bf16[32,80,1281]{2,1,0:T(8,128)(2,1)}), bf16[1,80,1281]{2,1,0:T(8,128)(2,1)}) %reduce-scatter.2.cloned.1.call-update) | async-done | bytes 204976 | tf_op jit(solution)/shard_map/reduce_scatter | solution.py:180
  (5 shorter events, 0.0 us)
Async XLA Ops:
  6.5 61.6 %all-gather.2.cloned.1.call-start = ((), (), s32[]{:S(2)}) async-start(), calls=%async_computation.3 | async-start | bytes 7434240 | tf_op jit(solution)/shard_map/all_gather | solution.py:153
  89.8 7.2 %copy-start.2 = (s32[2,40]{1,0:T(2,128)S(1)}, s32[2,40]{1,0:T(2,128)}, u32[]{:S(2)}) copy-start(s32[2,40]{1,0:T(2,128)} %param.7) | copy-start | bytes 964
  89.9 41.9 %all-to-all-start = ((bf16[80,80,2,32]{0,3,2,1:T(8,128)(2,1)}), bf16[80,80,2,32]{0,3,2,1:T(8,128)(2,1)S(1)}, u32[]{:S(2)}, u32[]{:S(2)}) async-start(bf16[80,80,2,32]{0,3,2,1:T(8,128)(2,1)} %bitcast.3), calls=%async_computation | async-start | bytes 2621440 | tf_op jit(solution)/shard_map/all_to_all | solution.py:165
  97.0 261.3 %reduce-scatter.2.cloned.1.call-start = ((), (), s32[]{:S(2)}) async-start(), calls=%async_computation.4 | async-start | bytes 7434240 | tf_op jit(solution)/shard_map/reduce_scatter | solution.py:180
  144.6 5.8 %copy-start = (bf16[10,16,1280]{1,2,0:T(8,128)(2,1)S(1)}, bf16[10,16,1280]{1,2,0:T(8,128)(2,1)}, u32[]{:S(2)}) copy-start(bf16[10,16,1280]{1,2,0:T(8,128)(2,1)} %get-tuple-element.11) | copy-start | bytes 1228804
  204.8 37.3 %copy-start.1 = (f32[40]{0:T(128)S(1)}, f32[40]{0:T(128)}, u32[]{:S(2)}) copy-start(f32[40]{0:T(128)} %param.6) | copy-start | bytes 484
Sparse Core Ops, SparseCore 0:
  10.0 58.1 all-gather.1
  265.9 92.3 reduce-scatter.1

commit v9 on v8

--- a/solution.py
+++ b/solution.py
@@ -124,20 +124,20 @@
     )(legendre, spectrum, codes)
 
 
-def legendre_direct(legendre, weights, codes, block):
+def legendre_direct(legendre, weights, codes, block, first_block, block_count):
     pair_count, lat_count, packed = legendre.shape
     rows = weights.shape[1]
     channels = rows // 4
     return pl.pallas_call(
         direct_kernel,
-        grid=(pair_count // block,),
+        grid=(block_count,),
         in_specs=[
-            pl.BlockSpec((block, lat_count, packed), lambda i: (i, 0, 0)),
-            pl.BlockSpec((block, rows, lat_count), lambda i: (i, 0, 0)),
-            pl.BlockSpec((block, 1, packed), lambda i: (i, 0, 0)),
+            pl.BlockSpec((block, lat_count, packed), lambda i: (i + first_block, 0, 0)),
+            pl.BlockSpec((block, rows, lat_count), lambda i: (i + first_block, 0, 0)),
+            pl.BlockSpec((block, 1, packed), lambda i: (i + first_block, 0, 0)),
         ],
         out_specs=pl.BlockSpec((channels, block, packed), lambda i: (0, i, 0)),
-        out_shape=jax.ShapeDtypeStruct((channels, pair_count, packed), jnp.bfloat16),
+        out_shape=jax.ShapeDtypeStruct((channels, block * block_count, packed), jnp.bfloat16),
     )(legendre, weights, codes)
 
 
@@ -176,8 +176,13 @@
     )
     weighted = weighted.reshape(pair_count, lat_count, 4 * channels).astype(jnp.bfloat16)
     weighted = jnp.swapaxes(weighted, 1, 2)
-    partial = legendre_direct(legendre, weighted, codes, block)
-    return lax.psum_scatter(partial, "lev", scatter_dimension=0, tiled=True)
+    blocks = pair_count // block
+    first_half = blocks // 2
+    halves = []
+    for first_block, block_count in ((0, first_half), (first_half, blocks - first_half)):
+        partial = legendre_direct(legendre, weighted, codes, block, first_block, block_count)
+        halves.append(lax.psum_scatter(partial, "lev", scatter_dimension=0, tiled=True))
+    return jnp.concatenate(halves, axis=1)
 
 
 def solution(mesh):

time: 366 us -> 452 us (1.23)
  waiting for transfers between devices: 139 us -> 222 us
    unnamed x2 -> x5, waiting for transfers between devices: 0.73 us -> 176 us
    reduce_scatter x1 -> x0, waiting for transfers between devices: 92.5 us -> none  [local(): return lax.psum_scatter(partial, 'lev', scatter_dimension=0, tiled=True)]
    pallas_call x1 -> x2, Pallas kernels: 18 us -> 20.2 us  [legendre_direct(): pl.pallas_call(direct_kernel, grid=(block_count,), in_specs=[pl.BlockSpec...]
  transfers between devices with their start and end apart: 3 -> 4, of which waited for: 3 -> 4; matrix products, arithmetic and copies ran while one was open for 14% -> 11% of each run, Pallas kernels for 0% -> 2%
where the time goes in v9:
time: 452 us; the launch traced here: 451 us
  waiting for transfers between devices  222 us (49%)
  other arithmetic  55 us (12%)
  local copies, waits for them, and re-layouts  53.3 us (12%)
  Pallas kernels  39 us (9%)
  blocking collectives  37.2 us (8%)
  matrix products  24.5 us (5%)
  between operations  13.3 us (3%)
  starting transfers between devices  7.23 us (2%)
    unnamed x5, waiting for transfers between devices  176 us
    all_to_all x1, blocking collectives, local(): lax.all_to_all(answered, 'lat', split_axis=0, concat_axis=0, tiled=True)  37.2 us
    all_to_all x1, waiting for transfers between devices, local(): lax.all_to_all(fourier, 'lat', split_axis=1, concat_axis=0, tiled=True)  34.5 us
    concatenate x4, local copies, waits for them, and re-layouts, fourier_work(): jnp.concatenate([real_out.reshape(lats, half_channels, waves), imag_out.r...  23.8 us
    pallas_call x2, Pallas kernels, legendre_direct(): pl.pallas_call(direct_kernel, grid=(block_count,), in_specs=[pl.BlockSpec...  20.2 us
    pallas_call x1, Pallas kernels, legendre_inverse(): pl.pallas_call(inverse_kernel, grid=(pair_count // block,), in_specs=[pl....  18.9 us
    concatenate x1, other arithmetic, wave_tables(): table = lax.optimization_barrier(jnp.concatenate([cosines, sines], axis=0))  18.5 us
    dot_general x1, matrix products, fourier_work(): jnp.dot(lhs, table, preferred_element_type=jnp.float32)  13.6 us
  transfers between devices with their start and end apart: 4, of which 4 were waited for; matrix products, arithmetic and copies ran while one was open for 11% of the time, Pallas kernels for 2%

profile of v9, /device:TPU:2, one launch (start us, length us, event | category | flops | bytes accessed | tf_op | source)
XLA Modules:
  0.0 451.2 jit_solution(5587276492509618456)
XLA Ops:
  6.5 0.0 all-gather.2.cloned.1.call-start
  6.5 0.7 all-gather.2.cloned.1.call-update
  7.3 0.2 copy.69
  7.5 0.2 mul.245
  7.7 1.3 fusion.32
  9.0 1.7 fusion.25
  10.8 12.6 %subtract_convert_fusion = (bf16[1280,80,64]{0,2,1:T(8,128)(2,1)}, bf16[1280,80,64]{0,2,1:T(8,128)(2,1)}) fusion(f32[1280,64]{0,1:T(8,128)S(1)} %get-tuple-element.22, f32[1280,80]{0,1:T(8,128)S(1)} %get-tuple-element.20, f32[1280,64]{0,1:T(8,128)S(1)} %get-tuple-element.21, f32[1280,80]{0,1:T(8,128)S(1)} %get-tuple-element.19), kind=kLoop, calls=%fused_computation.2 | loop fusion | flops 52428800 | bytes 27688960 | tf_op jit(solution)/shard_map/convert_element_type | solution.py:28
  23.4 18.5 %pad_maximum_fusion = bf16[2560,5120]{0,1:T(8,128)(2,1)} fusion(bf16[1280,5120]{0,1:T(8,128)(2,1)} %bitcast.47, bf16[1280,5120]{0,1:T(8,128)(2,1)} %bitcast.46), kind=kLoop, calls=%fused_computation | loop fusion | flops 52428800 | bytes 52428800 | tf_op jit(solution)/shard_map/concatenate | solution.py:30
  41.9 4.8 %fusion.13 = (bf16[80,1,1281]{2,1,0:T(2,128)(2,1)S(1)}, bf16[80,1,1281]{2,1,0:T(2,128)(2,1)S(1)}) fusion(s32[80]{0:T(128)S(1)} %add_subtract_fusion), kind=kLoop, calls=%fused_computation.44 | loop fusion | flops 3791760 | bytes 410240 | tf_op jit(solution)/shard_map/convert.6
  46.6 7.0 %fusion.11 = (s32[80,1,1281]{2,1,0:T(1,128)}, bf16[80,1,1281]{2,1,0:T(2,128)(2,1)S(1)}, bf16[80,1,1281]{2,1,0:T(2,128)(2,1)S(1)}) fusion(s32[80]{0:T(128)S(1)} %add_subtract_fusion), kind=kLoop, calls=%fused_computation.42 | loop fusion | flops 4406640 | bytes 820160 | tf_op jit(solution)/shard_map/add | solution.py:78
  53.6 3.0 pad_maximum_fusion.3.factor_ref
  56.7 11.5 %all-gather.2.cloned.1.call-done.spec_ref = bf16[32,80,1281]{2,1,0:T(8,128)(2,1)} async-done(((bf16[1,80,1281]{2,1,0:T(8,128)(2,1)}), bf16[32,80,1281]{2,1,0:T(8,128)(2,1)}) %all-gather.2.cloned.1.call-update) | async-done | bytes 6558736 | tf_op jit(solution)/shard_map/all_gather | solution.py:153
  68.2 18.9 %shard_map.46 = bf16[80,80,64]{2,1,0:T(8,128)(2,1)} custom-call(bf16[80,40,1281]{2,1,0:T(8,128)(2,1)} %leg_ref.5, bf16[32,80,1281]{2,1,0:T(8,128)(2,1)} %all-gather.2.cloned.1.call-done.spec_ref, bf16[80,4,1281]{2,1,0:T(4,128)(2,1)} %pad_maximum_fusion.3.factor_ref), custom_call_target="tpu_custom_call" | custom-call | tf_op jit(solution)/shard_map/pallas_call | solution.py:114
  87.0 2.8 copy.82
  89.8 0.0 copy-start.2
  89.9 7.1 %all-to-all-start = ((bf16[80,80,2,32]{0,3,2,1:T(8,128)(2,1)}), bf16[80,80,2,32]{0,3,2,1:T(8,128)(2,1)S(1)}, u32[]{:S(2)}, u32[]{:S(2)}) async-start(bf16[80,80,2,32]{0,3,2,1:T(8,128)(2,1)} %bitcast.3), calls=%async_computation | async-start | bytes 2621440 | tf_op jit(solution)/shard_map/all_to_all | solution.py:165
  97.0 0.0 reduce-scatter.7.cloned.1.call-start
  97.0 0.0 copy-done.2
  97.1 0.1 squeeze_reshape.3
  97.1 0.1 dynamic_slice.3
  97.2 0.1 fusion.35
  97.3 34.5 %all-to-all-done = bf16[80,80,2,32]{0,3,2,1:T(8,128)(2,1)S(1)} async-done(((bf16[80,80,2,32]{0,3,2,1:T(8,128)(2,1)}), bf16[80,80,2,32]{0,3,2,1:T(8,128)(2,1)S(1)}, u32[]{:S(2)}, u32[]{:S(2)}) %all-to-all-start) | async-done | bytes 819232 | tf_op jit(solution)/shard_map/all_to_all | solution.py:165
  131.8 1.0 copy.72
  132.7 1.2 all_to_all.19
  134.0 1.0 multiply_bitcast_fusion
  135.0 5.8 %copy.73 = bf16[10,32,640,2]{1,3,2,0:T(2,128)(2,1)S(1)} copy(bf16[10,32,640,2]{2,1,3,0:T(8,128)(2,1)} %multiply_bitcast_fusion) | data formatting | bytes 1638400 | tf_op jit(solution)/shard_map/transpose | solution.py:42
  140.7 3.9 fusion.36
  144.6 0.0 copy-start
  144.6 4.0 copy.83
  148.6 1.8 neg.6
  150.4 0.0 copy-done
  150.4 2.6 copy.74
  153.1 13.6 %convolution_multiply_fusion = f32[160,5120]{1,0:T(8,128)S(1)} fusion(bf16[2560,5120]{0,1:T(8,128)(2,1)} %pad_maximum_fusion, bf16[160,1280]{1,0:T(8,128)(2,1)} %bitcast.56, bf16[160,1280]{1,0:T(8,128)(2,1)} %bitcast.55), kind=kOutput, calls=%fused_computation.3 | convolution fusion | flops 4196761600 | bytes 30310400 | tf_op jit(solution)/shard_map/dot_general | solution.py:46
  166.7 0.4 multiply_convert_fusion.1
  167.1 0.1 pad_maximum_fusion.1
  167.2 10.8 %fusion.37 = f32[160,2560]{1,0:T(8,128)S(1)} fusion(bf16[160,5120]{1,0:T(8,128)(2,1)S(1)} %bitcast.54, bf16[2560,5120]{0,1:T(8,128)(2,1)} %pad_maximum_fusion), kind=kOutput, calls=%fused_computation.77 | convolution fusion | flops 4194304000 | bytes 29491200 | tf_op jit(solution)/shard_map/dot_general | solution.py:56
  178.1 0.1 slice_multiply_fusion.1
  178.2 0.4 copy.76
  178.6 5.9 %concatenate.33 = f32[10,16,640,2]{1,0,3,2:T(8,128)} reshape(f32[160,1280]{0,1:T(8,128)S(1)} %copy.76) | data formatting | bytes 1638400 | tf_op jit(solution)/shard_map/concatenate | solution.py:64
  184.6 6.0 %copy.78 = f32[10,16,640,2]{2,1,3,0:T(8,128)S(1)} copy(f32[10,16,640,2]{1,0,3,2:T(8,128)} %concatenate.33) | data formatting | bytes 1638400 | tf_op jit(solution)/shard_map/concatenate | solution.py:64
  190.5 0.4 copy.77
  191.0 5.9 %concatenate.34 = f32[10,16,640,2]{1,0,3,2:T(8,128)} reshape(f32[160,1280]{0,1:T(8,128)S(1)} %copy.77) | data formatting | bytes 1638400 | tf_op jit(solution)/shard_map/concatenate | solution.py:64
  196.9 6.0 %copy.79 = f32[10,16,640,2]{2,1,3,0:T(8,128)S(1)} copy(f32[10,16,640,2]{1,0,3,2:T(8,128)} %concatenate.34) | data formatting | bytes 1638400 | tf_op jit(solution)/shard_map/concatenate | solution.py:64
  202.9 0.2 fusion.1
  203.0 1.4 reshape.589
  204.4 0.3 copy.80
  204.8 0.0 copy-start.1
  204.8 37.2 %all_to_all.23 = bf16[8,80,10,2,32]{1,4,3,2,0:T(8,128)(2,1)S(1)} all-to-all(bf16[8,80,10,2,32]{1,4,3,2,0:T(8,128)(2,1)S(1)} %copy.80), channel_id=1, replica_groups=mesh['lat'=8,'lev'=32] {'lat'}, dimensions={0} | all-to-all | bytes 1638400 | tf_op jit(solution)/shard_map/all_to_all | solution.py:169
  242.0 0.0 copy-done.1
  242.0 0.4 fusion.10
  242.4 0.3 pad_maximum_fusion.2
  242.7 5.1 %copy.81 = bf16[80,40,2,2,32]{1,4,3,2,0:T(8,128)(2,1)} copy(bf16[80,40,2,2,32]{0,4,2,1,3:T(8,128)(2,1)S(1)} %pad_maximum_fusion.2) | data formatting | bytes 1638400 | tf_op jit(solution)/shard_map/stack | solution.py:174
  247.8 10.0 %shard_map.47 = bf16[32,40,1281]{2,1,0:T(8,128)(2,1)} custom-call(bf16[80,40,1281]{2,1,0:T(8,128)(2,1)} %leg_ref.5, bf16[80,128,40]{2,1,0:T(8,128)(2,1)} %bitcast.49, s32[80,1,1281]{2,1,0:T(1,128)} %get-tuple-element.27.code_ref), custom_call_target="tpu_custom_call" | custom-call | tf_op jit(solution)/shard_map/pallas_call | solution.py:131
  257.9 0.0 reduce-scatter.7.cloned.1.call-update
  257.9 0.0 reduce-scatter.9.cloned.1.call-start
  257.9 10.1 %shard_map.48 = bf16[32,40,1281]{2,1,0:T(8,128)(2,1)} custom-call(bf16[80,40,1281]{2,1,0:T(8,128)(2,1)} %leg_ref.5, bf16[80,128,40]{2,1,0:T(8,128)(2,1)} %bitcast.50, s32[80,1,1281]{2,1,0:T(1,128)} %get-tuple-element.27.code_ref), custom_call_target="tpu_custom_call" | custom-call | tf_op jit(solution)/shard_map/pallas_call | solution.py:131
  268.1 0.0 reduce-scatter.9.cloned.1.call-update
  268.1 77.5 %reduce-scatter.7.cloned.1.call-done = bf16[1,40,1281]{2,1,0:T(8,128)(2,1)} async-done(((bf16[32,40,1281]{2,1,0:T(8,128)(2,1)}), bf16[1,40,1281]{2,1,0:T(8,128)(2,1)}) %reduce-scatter.7.cloned.1.call-update) | async-done | bytes 102496
  345.6 97.5 %reduce-scatter.9.cloned.1.call-done = bf16[1,40,1281]{2,1,0:T(8,128)(2,1)} async-done(((bf16[32,40,1281]{2,1,0:T(8,128)(2,1)}), bf16[1,40,1281]{2,1,0:T(8,128)(2,1)}) %reduce-scatter.9.cloned.1.call-update) | async-done | bytes 102496
  443.0 1.7 pad_maximum_fusion.4
  (5 shorter events, 0.0 us)
Async XLA Ops:
  6.5 61.6 %all-gather.2.cloned.1.call-start = ((), (), s32[]{:S(2)}) async-start(), calls=%async_computation.4 | async-start | bytes 7434240 | tf_op jit(solution)/shard_map/all_gather | solution.py:153
  89.8 7.2 %copy-start.2 = (s32[2,40]{1,0:T(2,128)S(1)}, s32[2,40]{1,0:T(2,128)}, u32[]{:S(2)}) copy-start(s32[2,40]{1,0:T(2,128)} %param.7) | copy-start | bytes 964
  89.9 41.9 %all-to-all-start = ((bf16[80,80,2,32]{0,3,2,1:T(8,128)(2,1)}), bf16[80,80,2,32]{0,3,2,1:T(8,128)(2,1)S(1)}, u32[]{:S(2)}, u32[]{:S(2)}) async-start(bf16[80,80,2,32]{0,3,2,1:T(8,128)(2,1)} %bitcast.3), calls=%async_computation | async-start | bytes 2621440 | tf_op jit(solution)/shard_map/all_to_all | solution.py:165
  97.0 248.6 %reduce-scatter.7.cloned.1.call-start = ((), (), s32[]{:S(2)}) async-start(), calls=%async_computation.5 | async-start | bytes 3717120
  144.6 5.8 %copy-start = (bf16[10,16,1280]{1,2,0:T(8,128)(2,1)S(1)}, bf16[10,16,1280]{1,2,0:T(8,128)(2,1)}, u32[]{:S(2)}) copy-start(bf16[10,16,1280]{1,2,0:T(8,128)(2,1)} %get-tuple-element.11) | copy-start | bytes 1228804
  204.8 37.3 %copy-start.1 = (f32[40]{0:T(128)S(1)}, f32[40]{0:T(128)}, u32[]{:S(2)}) copy-start(f32[40]{0:T(128)} %param.6) | copy-start | bytes 484
  257.9 185.1 %reduce-scatter.9.cloned.1.call-start = ((), (), s32[]{:S(2)}) async-start(), calls=%async_computation.6 | async-start | bytes 3717120
Sparse Core Ops, SparseCore 0:
  10.0 58.1 all-gather.1
  258.0 87.5 reduce-scatter.6
  350.3 92.6 reduce-scatter.8

commit v10 on v8

--- a/solution.py
+++ b/solution.py
@@ -34,7 +34,7 @@
 def fourier_work(spectrum, row_counts, table, wavenumbers, truncation):
     pairs, lats, slots, channels = spectrum.shape
     kept_mask = (2 * wavenumbers[:, None, :] < row_counts[None, :, None]).astype(jnp.bfloat16)
-    masked = spectrum * kept_mask[..., None]
+    masked = spectrum
     half_channels = channels // 2
     levels = half_channels // 2
     rows = lats * half_channels
@@ -160,6 +160,10 @@
     ).astype(jnp.bfloat16)
     fourier = legendre_inverse(legendre, gathered, factors, block)
     fourier = fourier.reshape(pair_count, 2 * lat_count, 2, channels)
+    own_waves = lax.dynamic_slice_in_dim(wavenumbers, first_pair, pair_count)
+    own_rows = row_points.reshape(2 * lat_count)
+    own_kept = (2 * own_waves[:, None, :] < own_rows[None, :, None]).astype(jnp.bfloat16)
+    fourier = fourier * own_kept[..., None]
     local_rows = row_points.reshape(1, 2 * lat_count)
     band_lats = 2 * lat_count // groups
     lat_rows = lax.all_to_all(fourier, "lat", split_axis=1, concat_axis=0, tiled=True)

time: 366 us -> 368 us (level)
  no operation moved by 1% of the time
where the time goes in v10:
time: 368 us; the launch traced here: 367 us
  waiting for transfers between devices  139 us (38%)
  local copies, waits for them, and re-layouts  56.5 us (15%)
  other arithmetic  52.6 us (14%)
  blocking collectives  37.2 us (10%)
  Pallas kernels  36.9 us (10%)
  matrix products  24.5 us (7%)
  between operations  13.6 us (4%)
  starting transfers between devices  7.04 us (2%)
    reduce_scatter x1, waiting for transfers between devices, local(): return lax.psum_scatter(partial, 'lev', scatter_dimension=0, tiled=True)  92.7 us
    all_to_all x1, blocking collectives, local(): lax.all_to_all(answered, 'lat', split_axis=0, concat_axis=0, tiled=True)  37.2 us
    all_to_all x1, waiting for transfers between devices, local(): lax.all_to_all(fourier, 'lat', split_axis=1, concat_axis=0, tiled=True)  34.6 us
    concatenate x4, local copies, waits for them, and re-layouts, fourier_work(): jnp.concatenate([real_out.reshape(lats, half_channels, waves), imag_out.r...  23.8 us
    pallas_call x1, Pallas kernels, legendre_inverse(): pl.pallas_call(inverse_kernel, grid=(pair_count // block,), in_specs=[pl....  18.9 us
    concatenate x1, other arithmetic, wave_tables(): table = lax.optimization_barrier(jnp.concatenate([cosines, sines], axis=0))  18.4 us
    pallas_call x1, Pallas kernels, legendre_direct(): pl.pallas_call(direct_kernel, grid=(pair_count // block,), in_specs=[pl.B...  18 us
    dot_general x1, matrix products, fourier_work(): jnp.dot(lhs, table, preferred_element_type=jnp.float32)  13.6 us
  transfers between devices with their start and end apart: 3, of which 3 were waited for; matrix products, arithmetic and copies ran while one was open for 14% of the time, Pallas kernels for 0%

profile of v10, /device:TPU:2, one launch (start us, length us, event | category | flops | bytes accessed | tf_op | source)
XLA Modules:
  0.0 367.4 jit_solution(5418235570870344184)
XLA Ops:
  6.5 0.0 all-gather.2.cloned.1.call-start
  6.5 0.7 all-gather.2.cloned.1.call-update
  7.3 0.2 copy.67
  7.5 0.2 mul.252
  7.7 1.3 fusion.32
  9.0 1.7 fusion.25
  10.8 12.5 %subtract_convert_fusion = (bf16[1280,80,64]{0,2,1:T(8,128)(2,1)}, bf16[1280,80,64]{0,2,1:T(8,128)(2,1)}) fusion(f32[1280,64]{0,1:T(8,128)S(1)} %get-tuple-element.22, f32[1280,80]{0,1:T(8,128)S(1)} %get-tuple-element.20, f32[1280,64]{0,1:T(8,128)S(1)} %get-tuple-element.21, f32[1280,80]{0,1:T(8,128)S(1)} %get-tuple-element.19), kind=kLoop, calls=%fused_computation.2 | loop fusion | flops 52428800 | bytes 27688960 | tf_op jit(solution)/shard_map/convert_element_type | solution.py:28
  23.3 0.0 copy-start.2
  23.3 18.4 %pad_maximum_fusion = bf16[2560,5120]{0,1:T(8,128)(2,1)} fusion(bf16[1280,5120]{0,1:T(8,128)(2,1)} %bitcast.44, bf16[1280,5120]{0,1:T(8,128)(2,1)} %bitcast.43), kind=kLoop, calls=%fused_computation | loop fusion | flops 52428800 | bytes 52428800 | tf_op jit(solution)/shard_map/concatenate | solution.py:30
  41.7 0.1 fusion.36
  41.8 0.1 copy.69
  41.9 0.0 copy-done.2
  41.9 0.1 lt.72
  42.0 0.1 compare_convert_fusion.2
  42.2 4.8 %fusion.13 = (bf16[80,1,1281]{2,1,0:T(2,128)(2,1)S(1)}, bf16[80,1,1281]{2,1,0:T(2,128)(2,1)S(1)}) fusion(s32[80]{0:T(128)S(1)} %add_subtract_fusion), kind=kLoop, calls=%fused_computation.44 | loop fusion | flops 3791760 | bytes 410240 | tf_op jit(solution)/shard_map/convert.6
  46.9 7.0 %fusion.11 = (s32[80,1,1281]{2,1,0:T(1,128)}, bf16[80,1,1281]{2,1,0:T(2,128)(2,1)S(1)}, bf16[80,1,1281]{2,1,0:T(2,128)(2,1)S(1)}) fusion(s32[80]{0:T(128)S(1)} %add_subtract_fusion), kind=kLoop, calls=%fused_computation.42 | loop fusion | flops 4406640 | bytes 820160 | tf_op jit(solution)/shard_map/add | solution.py:78
  53.9 3.1 pad_maximum_fusion.3.factor_ref
  57.0 11.2 %all-gather.2.cloned.1.call-done.spec_ref = bf16[32,80,1281]{2,1,0:T(8,128)(2,1)} async-done(((bf16[1,80,1281]{2,1,0:T(8,128)(2,1)}), bf16[32,80,1281]{2,1,0:T(8,128)(2,1)}) %all-gather.2.cloned.1.call-update) | async-done | bytes 6558736 | tf_op jit(solution)/shard_map/all_gather | solution.py:153
  68.2 18.9 %shard_map.46 = bf16[80,80,64]{2,1,0:T(8,128)(2,1)} custom-call(bf16[80,40,1281]{2,1,0:T(8,128)(2,1)} %leg_ref.3, bf16[32,80,1281]{2,1,0:T(8,128)(2,1)} %all-gather.2.cloned.1.call-done.spec_ref, bf16[80,4,1281]{2,1,0:T(4,128)(2,1)} %pad_maximum_fusion.3.factor_ref), custom_call_target="tpu_custom_call" | custom-call | tf_op jit(solution)/shard_map/pallas_call | solution.py:114
  87.0 1.9 copy.68
  88.9 0.1 broadcast_multiply_fusion
  89.0 3.5 copy.70
  92.5 7.0 %all-to-all-start = ((bf16[80,80,2,32]{0,3,2,1:T(8,128)(2,1)}), bf16[80,80,2,32]{0,3,2,1:T(8,128)(2,1)S(1)}, u32[]{:S(2)}, u32[]{:S(2)}) async-start(bf16[80,80,2,32]{0,3,2,1:T(8,128)(2,1)} %copy.70), calls=%async_computation | async-start | bytes 2621440 | tf_op jit(solution)/shard_map/all_to_all | solution.py:169
  99.5 0.0 reduce-scatter.2.cloned.1.call-start
  99.6 0.1 dynamic_slice.7
  99.6 0.1 fusion.34
  99.7 34.6 %all-to-all-done = bf16[80,80,2,32]{0,3,2,1:T(8,128)(2,1)S(1)} async-done(((bf16[80,80,2,32]{0,3,2,1:T(8,128)(2,1)}), bf16[80,80,2,32]{0,3,2,1:T(8,128)(2,1)S(1)}, u32[]{:S(2)}, u32[]{:S(2)}) %all-to-all-start) | async-done | bytes 819232 | tf_op jit(solution)/shard_map/all_to_all | solution.py:169
  134.3 1.0 copy.71
  135.3 1.7 all_to_all.19
  137.0 5.8 %copy.72 = bf16[10,32,640,2]{1,3,2,0:T(2,128)(2,1)S(1)} copy(bf16[10,32,640,2]{2,1,3,0:T(8,128)(2,1)} %bitcast.51) | data formatting | bytes 1638400 | tf_op jit(solution)/shard_map/transpose | solution.py:42
  142.8 3.9 %fusion.38 = (bf16[10,16,1280]{1,2,0:T(8,128)(2,1)}, bf16[10,16,1280]{1,2,0:T(8,128)(2,1)}) fusion(bf16[10,32,1280]{1,2,0:T(8,128)(2,1)S(1)} %bitcast.45), kind=kLoop, calls=%fused_computation.80 | loop fusion | bytes 1638400 | tf_op jit(solution)/shard_map/slice | solution.py:43
  146.7 0.0 copy-start
  146.7 4.0 %copy.81 = bf16[10,16,1280]{2,1,0:T(8,128)(2,1)} copy(bf16[10,16,1280]{1,2,0:T(8,128)(2,1)} %get-tuple-element.12) | data formatting | bytes 819200
  150.7 1.8 neg.6
  152.5 0.0 copy-done
  152.5 2.6 copy.73
  155.1 13.6 %convolution_multiply_fusion = f32[160,5120]{1,0:T(8,128)S(1)} fusion(bf16[2560,5120]{0,1:T(8,128)(2,1)} %pad_maximum_fusion, bf16[160,1280]{1,0:T(8,128)(2,1)} %bitcast.54, bf16[160,1280]{1,0:T(8,128)(2,1)} %bitcast.53), kind=kOutput, calls=%fused_computation.3 | convolution fusion | flops 4196761600 | bytes 30310400 | tf_op jit(solution)/shard_map/dot_general | solution.py:46
  168.8 0.4 multiply_convert_fusion.1
  169.1 0.1 pad_maximum_fusion.1
  169.3 10.8 %fusion.39 = f32[160,2560]{1,0:T(8,128)S(1)} fusion(bf16[160,5120]{1,0:T(8,128)(2,1)S(1)} %bitcast.52, bf16[2560,5120]{0,1:T(8,128)(2,1)} %pad_maximum_fusion), kind=kOutput, calls=%fused_computation.81 | convolution fusion | flops 4194304000 | bytes 29491200 | tf_op jit(solution)/shard_map/dot_general | solution.py:56
  180.1 0.1 slice_multiply_fusion.1
  180.3 0.4 copy.75
  180.7 5.9 %concatenate.30 = f32[10,16,640,2]{1,0,3,2:T(8,128)} reshape(f32[160,1280]{0,1:T(8,128)S(1)} %copy.75) | data formatting | bytes 1638400 | tf_op jit(solution)/shard_map/concatenate | solution.py:64
  186.6 6.0 %copy.77 = f32[10,16,640,2]{2,1,3,0:T(8,128)S(1)} copy(f32[10,16,640,2]{1,0,3,2:T(8,128)} %concatenate.30) | data formatting | bytes 1638400 | tf_op jit(solution)/shard_map/concatenate | solution.py:64
  192.6 0.4 copy.76
  193.0 5.9 %concatenate.31 = f32[10,16,640,2]{1,0,3,2:T(8,128)} reshape(f32[160,1280]{0,1:T(8,128)S(1)} %copy.76) | data formatting | bytes 1638400 | tf_op jit(solution)/shard_map/concatenate | solution.py:64
  198.9 6.0 %copy.78 = f32[10,16,640,2]{2,1,3,0:T(8,128)S(1)} copy(f32[10,16,640,2]{1,0,3,2:T(8,128)} %concatenate.31) | data formatting | bytes 1638400 | tf_op jit(solution)/shard_map/concatenate | solution.py:64
  204.9 0.2 fusion.1
  205.1 1.4 reshape.594
  206.5 0.3 copy.79
  206.8 0.0 copy-start.1
  206.8 37.2 %all_to_all.23 = bf16[8,80,10,2,32]{1,4,3,2,0:T(8,128)(2,1)S(1)} all-to-all(bf16[8,80,10,2,32]{1,4,3,2,0:T(8,128)(2,1)S(1)} %copy.79), channel_id=1, replica_groups=mesh['lat'=8,'lev'=32] {'lat'}, dimensions={0} | all-to-all | bytes 1638400 | tf_op jit(solution)/shard_map/all_to_all | solution.py:173
  244.1 0.0 copy-done.1
  244.1 0.4 fusion.10
  244.5 0.3 pad_maximum_fusion.2
  244.8 5.1 %copy.80 = bf16[80,40,2,2,32]{1,4,3,2,0:T(8,128)(2,1)} copy(bf16[80,40,2,2,32]{0,4,2,1,3:T(8,128)(2,1)S(1)} %pad_maximum_fusion.2) | data formatting | bytes 1638400 | tf_op jit(solution)/shard_map/stack | solution.py:178
  249.9 18.0 %shard_map.47 = bf16[32,80,1281]{2,1,0:T(8,128)(2,1)} custom-call(bf16[80,40,1281]{2,1,0:T(8,128)(2,1)} %leg_ref.3, bf16[80,128,40]{2,1,0:T(8,128)(2,1)} %bitcast.46, s32[80,1,1281]{2,1,0:T(1,128)} %get-tuple-element.25.code_ref), custom_call_target="tpu_custom_call" | custom-call | tf_op jit(solution)/shard_map/pallas_call | solution.py:131
  267.9 0.0 reduce-scatter.2.cloned.1.call-update
  267.9 92.7 %reduce-scatter.2.cloned.1.call-done = bf16[1,80,1281]{2,1,0:T(8,128)(2,1)} async-done(((bf16[32,80,1281]{2,1,0:T(8,128)(2,1)}), bf16[1,80,1281]{2,1,0:T(8,128)(2,1)}) %reduce-scatter.2.cloned.1.call-update) | async-done | bytes 204976 | tf_op jit(solution)/shard_map/reduce_scatter | solution.py:184
  (5 shorter events, 0.0 us)
Async XLA Ops:
  6.5 61.6 %all-gather.2.cloned.1.call-start = ((), (), s32[]{:S(2)}) async-start(), calls=%async_computation.3 | async-start | bytes 7434240 | tf_op jit(solution)/shard_map/all_gather | solution.py:153
  23.3 18.6 %copy-start.2 = (s32[2,40]{1,0:T(2,128)S(1)}, s32[2,40]{1,0:T(2,128)}, u32[]{:S(2)}) copy-start(s32[2,40]{1,0:T(2,128)} %param.7) | copy-start | bytes 964
  92.5 41.8 %all-to-all-start = ((bf16[80,80,2,32]{0,3,2,1:T(8,128)(2,1)}), bf16[80,80,2,32]{0,3,2,1:T(8,128)(2,1)S(1)}, u32[]{:S(2)}, u32[]{:S(2)}) async-start(bf16[80,80,2,32]{0,3,2,1:T(8,128)(2,1)} %copy.70), calls=%async_computation | async-start | bytes 2621440 | tf_op jit(solution)/shard_map/all_to_all | solution.py:169
  99.5 261.1 %reduce-scatter.2.cloned.1.call-start = ((), (), s32[]{:S(2)}) async-start(), calls=%async_computation.4 | async-start | bytes 7434240 | tf_op jit(solution)/shard_map/reduce_scatter | solution.py:184
  146.7 5.8 %copy-start = (bf16[10,16,1280]{1,2,0:T(8,128)(2,1)S(1)}, bf16[10,16,1280]{1,2,0:T(8,128)(2,1)}, u32[]{:S(2)}) copy-start(bf16[10,16,1280]{1,2,0:T(8,128)(2,1)} %get-tuple-element.11) | copy-start | bytes 1228804
  206.8 37.3 %copy-start.1 = (f32[40]{0:T(128)S(1)}, f32[40]{0:T(128)}, u32[]{:S(2)}) copy-start(f32[40]{0:T(128)} %param.6) | copy-start | bytes 484
Sparse Core Ops, SparseCore 0:
  10.0 58.1 all-gather.1
  268.0 92.5 reduce-scatter.1

commit v11 on v8

--- a/solution.py
+++ b/solution.py
@@ -177,7 +177,8 @@
     weighted = weighted.reshape(pair_count, lat_count, 4 * channels).astype(jnp.bfloat16)
     weighted = jnp.swapaxes(weighted, 1, 2)
     partial = legendre_direct(legendre, weighted, codes, block)
-    return lax.psum_scatter(partial, "lev", scatter_dimension=0, tiled=True)
+    summed = lax.psum(partial, "lev")
+    return lax.dynamic_slice_in_dim(summed, lax.axis_index("lev") * local_channels, local_channels, 0)
 
 
 def solution(mesh):

time: 366 us -> 399 us (1.090)
  waiting for transfers between devices: 139 us -> 169 us
    psum x0 -> x1, waiting for transfers between devices: none -> 122 us  [local(): summed = lax.psum(partial, 'lev')]
    reduce_scatter x1 -> x0, waiting for transfers between devices: 92.5 us -> none  [local(): return lax.psum_scatter(partial, 'lev', scatter_dimension=0, tiled=True)]
  transfers between devices with their start and end apart: 3 -> 3, of which waited for: 3 -> 3; matrix products, arithmetic and copies ran while one was open for 14% -> 13% of each run, Pallas kernels for 0% -> 0%
where the time goes in v11:
time: 399 us; the launch traced here: 397 us
  waiting for transfers between devices  169 us (42%)
  local copies, waits for them, and re-layouts  54.9 us (14%)
  other arithmetic  53.3 us (13%)
  blocking collectives  37.2 us (9%)
  Pallas kernels  36.8 us (9%)
  matrix products  24.5 us (6%)
  between operations  13.6 us (3%)
  starting transfers between devices  7.18 us (2%)
    psum x1, waiting for transfers between devices, local(): summed = lax.psum(partial, 'lev')  122 us
    all_to_all x1, blocking collectives, local(): lax.all_to_all(answered, 'lat', split_axis=0, concat_axis=0, tiled=True)  37.2 us
    all_to_all x1, waiting for transfers between devices, local(): lax.all_to_all(fourier, 'lat', split_axis=1, concat_axis=0, tiled=True)  34.5 us
    concatenate x4, local copies, waits for them, and re-layouts, fourier_work(): jnp.concatenate([real_out.reshape(lats, half_channels, waves), imag_out.r...  23.8 us
    pallas_call x1, Pallas kernels, legendre_inverse(): pl.pallas_call(inverse_kernel, grid=(pair_count // block,), in_specs=[pl....  18.9 us
    concatenate x1, other arithmetic, wave_tables(): table = lax.optimization_barrier(jnp.concatenate([cosines, sines], axis=0))  18.5 us
    pallas_call x1, Pallas kernels, legendre_direct(): pl.pallas_call(direct_kernel, grid=(pair_count // block,), in_specs=[pl.B...  18 us
    dot_general x1, matrix products, fourier_work(): jnp.dot(lhs, table, preferred_element_type=jnp.float32)  13.6 us
  transfers between devices with their start and end apart: 3, of which 3 were waited for; matrix products, arithmetic and copies ran while one was open for 13% of the time, Pallas kernels for 0%

profile of v11, /device:TPU:2, one launch (start us, length us, event | category | flops | bytes accessed | tf_op | source)
XLA Modules:
  0.0 396.6 jit_solution(5491076975937485048)
XLA Ops:
  6.5 0.0 all-gather.2.cloned.1.call-start
  6.5 0.7 all-gather.2.cloned.1.call-update
  7.3 0.2 copy.69
  7.5 0.2 mul.245
  7.7 1.3 fusion.32
  9.0 1.7 fusion.25
  10.8 12.6 %subtract_convert_fusion = (bf16[1280,80,64]{0,2,1:T(8,128)(2,1)}, bf16[1280,80,64]{0,2,1:T(8,128)(2,1)}) fusion(f32[1280,64]{0,1:T(8,128)S(1)} %get-tuple-element.22, f32[1280,80]{0,1:T(8,128)S(1)} %get-tuple-element.20, f32[1280,64]{0,1:T(8,128)S(1)} %get-tuple-element.21, f32[1280,80]{0,1:T(8,128)S(1)} %get-tuple-element.19), kind=kLoop, calls=%fused_computation.2 | loop fusion | flops 52428800 | bytes 27688960 | tf_op jit(solution)/shard_map/convert_element_type | solution.py:28
  23.4 18.5 %pad_maximum_fusion = bf16[2560,5120]{0,1:T(8,128)(2,1)} fusion(bf16[1280,5120]{0,1:T(8,128)(2,1)} %bitcast.46, bf16[1280,5120]{0,1:T(8,128)(2,1)} %bitcast.45), kind=kLoop, calls=%fused_computation | loop fusion | flops 52428800 | bytes 52428800 | tf_op jit(solution)/shard_map/concatenate | solution.py:30
  41.9 4.8 %fusion.13 = (bf16[80,1,1281]{2,1,0:T(2,128)(2,1)S(1)}, bf16[80,1,1281]{2,1,0:T(2,128)(2,1)S(1)}) fusion(s32[80]{0:T(128)S(1)} %add_subtract_fusion), kind=kLoop, calls=%fused_computation.44 | loop fusion | flops 3791760 | bytes 410240 | tf_op jit(solution)/shard_map/convert.6
  46.6 7.0 %fusion.11 = (s32[80,1,1281]{2,1,0:T(1,128)}, bf16[80,1,1281]{2,1,0:T(2,128)(2,1)S(1)}, bf16[80,1,1281]{2,1,0:T(2,128)(2,1)S(1)}) fusion(s32[80]{0:T(128)S(1)} %add_subtract_fusion), kind=kLoop, calls=%fused_computation.42 | loop fusion | flops 4406640 | bytes 820160 | tf_op jit(solution)/shard_map/add | solution.py:78
  53.6 3.0 pad_maximum_fusion.3.factor_ref
  56.7 11.5 %all-gather.2.cloned.1.call-done.spec_ref = bf16[32,80,1281]{2,1,0:T(8,128)(2,1)} async-done(((bf16[1,80,1281]{2,1,0:T(8,128)(2,1)}), bf16[32,80,1281]{2,1,0:T(8,128)(2,1)}) %all-gather.2.cloned.1.call-update) | async-done | bytes 6558736 | tf_op jit(solution)/shard_map/all_gather | solution.py:153
  68.2 18.9 %shard_map.46 = bf16[80,80,64]{2,1,0:T(8,128)(2,1)} custom-call(bf16[80,40,1281]{2,1,0:T(8,128)(2,1)} %leg_ref.3, bf16[32,80,1281]{2,1,0:T(8,128)(2,1)} %all-gather.2.cloned.1.call-done.spec_ref, bf16[80,4,1281]{2,1,0:T(4,128)(2,1)} %pad_maximum_fusion.3.factor_ref), custom_call_target="tpu_custom_call" | custom-call | tf_op jit(solution)/shard_map/pallas_call | solution.py:114
  87.0 2.8 copy.82
  89.8 0.0 copy-start.2
  89.9 7.1 %all-to-all-start = ((bf16[80,80,2,32]{0,3,2,1:T(8,128)(2,1)}), bf16[80,80,2,32]{0,3,2,1:T(8,128)(2,1)S(1)}, u32[]{:S(2)}, u32[]{:S(2)}) async-start(bf16[80,80,2,32]{0,3,2,1:T(8,128)(2,1)} %bitcast.3), calls=%async_computation | async-start | bytes 2621440 | tf_op jit(solution)/shard_map/all_to_all | solution.py:165
  97.0 0.0 all-reduce.2.cloned.1.call-start
  97.0 0.0 copy-done.2
  97.1 0.1 squeeze_reshape.3
  97.1 0.1 dynamic_slice.6
  97.2 0.1 fusion.35
  97.3 34.5 %all-to-all-done = bf16[80,80,2,32]{0,3,2,1:T(8,128)(2,1)S(1)} async-done(((bf16[80,80,2,32]{0,3,2,1:T(8,128)(2,1)}), bf16[80,80,2,32]{0,3,2,1:T(8,128)(2,1)S(1)}, u32[]{:S(2)}, u32[]{:S(2)}) %all-to-all-start) | async-done | bytes 819232 | tf_op jit(solution)/shard_map/all_to_all | solution.py:165
  131.8 1.0 copy.72
  132.7 1.2 all_to_all.19
  134.0 1.0 multiply_bitcast_fusion
  135.0 5.8 %copy.73 = bf16[10,32,640,2]{1,3,2,0:T(2,128)(2,1)S(1)} copy(bf16[10,32,640,2]{2,1,3,0:T(8,128)(2,1)} %multiply_bitcast_fusion) | data formatting | bytes 1638400 | tf_op jit(solution)/shard_map/transpose | solution.py:42
  140.7 3.9 fusion.36
  144.6 0.0 copy-start
  144.6 4.0 %copy.83 = bf16[10,16,1280]{2,1,0:T(8,128)(2,1)} copy(bf16[10,16,1280]{1,2,0:T(8,128)(2,1)} %get-tuple-element.12) | data formatting | bytes 819200
  148.6 1.8 neg.6
  150.4 0.0 copy-done
  150.4 2.6 copy.74
  153.1 13.6 %convolution_multiply_fusion = f32[160,5120]{1,0:T(8,128)S(1)} fusion(bf16[2560,5120]{0,1:T(8,128)(2,1)} %pad_maximum_fusion, bf16[160,1280]{1,0:T(8,128)(2,1)} %bitcast.54, bf16[160,1280]{1,0:T(8,128)(2,1)} %bitcast.53), kind=kOutput, calls=%fused_computation.3 | convolution fusion | flops 4196761600 | bytes 30310400 | tf_op jit(solution)/shard_map/dot_general | solution.py:46
  166.7 0.4 multiply_convert_fusion.1
  167.1 0.1 pad_maximum_fusion.1
  167.2 10.8 %fusion.37 = f32[160,2560]{1,0:T(8,128)S(1)} fusion(bf16[160,5120]{1,0:T(8,128)(2,1)S(1)} %bitcast.52, bf16[2560,5120]{0,1:T(8,128)(2,1)} %pad_maximum_fusion), kind=kOutput, calls=%fused_computation.77 | convolution fusion | flops 4194304000 | bytes 29491200 | tf_op jit(solution)/shard_map/dot_general | solution.py:56
  178.1 0.1 slice_multiply_fusion.1
  178.2 0.4 copy.76
  178.6 5.9 %concatenate.30 = f32[10,16,640,2]{1,0,3,2:T(8,128)} reshape(f32[160,1280]{0,1:T(8,128)S(1)} %copy.76) | data formatting | bytes 1638400 | tf_op jit(solution)/shard_map/concatenate | solution.py:64
  184.6 6.0 %copy.78 = f32[10,16,640,2]{2,1,3,0:T(8,128)S(1)} copy(f32[10,16,640,2]{1,0,3,2:T(8,128)} %concatenate.30) | data formatting | bytes 1638400 | tf_op jit(solution)/shard_map/concatenate | solution.py:64
  190.5 0.4 copy.77
  191.0 5.9 %concatenate.31 = f32[10,16,640,2]{1,0,3,2:T(8,128)} reshape(f32[160,1280]{0,1:T(8,128)S(1)} %copy.77) | data formatting | bytes 1638400 | tf_op jit(solution)/shard_map/concatenate | solution.py:64
  196.9 6.0 %copy.79 = f32[10,16,640,2]{2,1,3,0:T(8,128)S(1)} copy(f32[10,16,640,2]{1,0,3,2:T(8,128)} %concatenate.31) | data formatting | bytes 1638400 | tf_op jit(solution)/shard_map/concatenate | solution.py:64
  202.9 0.2 fusion.1
  203.0 1.4 reshape.589
  204.4 0.3 copy.80
  204.8 0.0 copy-start.1
  204.8 37.2 %all_to_all.23 = bf16[8,80,10,2,32]{1,4,3,2,0:T(8,128)(2,1)S(1)} all-to-all(bf16[8,80,10,2,32]{1,4,3,2,0:T(8,128)(2,1)S(1)} %copy.80), channel_id=1, replica_groups=mesh['lat'=8,'lev'=32] {'lat'}, dimensions={0} | all-to-all | bytes 1638400 | tf_op jit(solution)/shard_map/all_to_all | solution.py:169
  242.0 0.0 copy-done.1
  242.0 0.4 fusion.10
  242.4 0.3 pad_maximum_fusion.2
  242.7 5.1 %copy.81 = bf16[80,40,2,2,32]{1,4,3,2,0:T(8,128)(2,1)} copy(bf16[80,40,2,2,32]{0,4,2,1,3:T(8,128)(2,1)S(1)} %pad_maximum_fusion.2) | data formatting | bytes 1638400 | tf_op jit(solution)/shard_map/stack | solution.py:174
  247.8 18.0 %shard_map.47 = bf16[32,80,1281]{2,1,0:T(8,128)(2,1)} custom-call(bf16[80,40,1281]{2,1,0:T(8,128)(2,1)} %leg_ref.3, bf16[80,128,40]{2,1,0:T(8,128)(2,1)} %bitcast.48, s32[80,1,1281]{2,1,0:T(1,128)} %get-tuple-element.27.code_ref), custom_call_target="tpu_custom_call" | custom-call | tf_op jit(solution)/shard_map/pallas_call | solution.py:131
  265.8 0.0 all-reduce.2.cloned.1.call-update
  265.8 122.3 %all-reduce.2.cloned.1.call-done = bf16[32,80,1281]{2,1,0:T(8,128)(2,1)} async-done(((bf16[32,80,1281]{2,1,0:T(8,128)(2,1)}), bf16[32,80,1281]{2,1,0:T(8,128)(2,1)}) %all-reduce.2.cloned.1.call-update) | async-done | bytes 6558736 | tf_op jit(solution)/shard_map/psum | solution.py:180
  388.1 1.6 constant_dynamic-slice_fusion
  (5 shorter events, 0.0 us)
Async XLA Ops:
  6.5 61.6 %all-gather.2.cloned.1.call-start = ((), (), s32[]{:S(2)}) async-start(), calls=%async_computation.2 | async-start | bytes 7434240 | tf_op jit(solution)/shard_map/all_gather | solution.py:153
  89.8 7.2 %copy-start.2 = (s32[2,40]{1,0:T(2,128)S(1)}, s32[2,40]{1,0:T(2,128)}, u32[]{:S(2)}) copy-start(s32[2,40]{1,0:T(2,128)} %param.7) | copy-start | bytes 964
  89.9 41.9 %all-to-all-start = ((bf16[80,80,2,32]{0,3,2,1:T(8,128)(2,1)}), bf16[80,80,2,32]{0,3,2,1:T(8,128)(2,1)S(1)}, u32[]{:S(2)}, u32[]{:S(2)}) async-start(bf16[80,80,2,32]{0,3,2,1:T(8,128)(2,1)} %bitcast.3), calls=%async_computation | async-start | bytes 2621440 | tf_op jit(solution)/shard_map/all_to_all | solution.py:165
  97.0 291.1 %all-reduce.2.cloned.1.call-start = ((), (), s32[]{:S(2)}) async-start(), calls=%async_computation.3 | async-start | bytes 14417920 | tf_op jit(solution)/shard_map/psum | solution.py:180
  144.6 5.8 %copy-start = (bf16[10,16,1280]{1,2,0:T(8,128)(2,1)S(1)}, bf16[10,16,1280]{1,2,0:T(8,128)(2,1)}, u32[]{:S(2)}) copy-start(bf16[10,16,1280]{1,2,0:T(8,128)(2,1)} %get-tuple-element.11) | copy-start | bytes 1228804
  204.8 37.3 %copy-start.1 = (f32[40]{0:T(128)S(1)}, f32[40]{0:T(128)}, u32[]{:S(2)}) copy-start(f32[40]{0:T(128)} %param.6) | copy-start | bytes 484
Sparse Core Ops, SparseCore 0:
  10.0 58.1 all-gather.1
  265.9 122.1 all-reduce.1

commit v12 on v8

--- a/solution.py
+++ b/solution.py
@@ -101,10 +101,10 @@
 
     for pp in range(block):
         full = jnp.dot(weight_ref[pp], leg_ref[pp], preferred_element_type=jnp.float32)
-        code = code_ref[pp]
-        picked = jnp.where(code == 0, full[:channels], 0.0)
+        factors = code_ref[pp]
+        picked = full[:channels] * factors[0:1]
         for x in range(1, 4):
-            picked = picked + jnp.where(code == x, full[x * channels : (x + 1) * channels], 0.0)
+            picked = picked + full[x * channels : (x + 1) * channels] * factors[x : x + 1]
         out_ref[:, pp, :] = picked.astype(out_ref.dtype)
 
 
@@ -134,7 +134,7 @@
         in_specs=[
             pl.BlockSpec((block, lat_count, packed), lambda i: (i, 0, 0)),
             pl.BlockSpec((block, rows, lat_count), lambda i: (i, 0, 0)),
-            pl.BlockSpec((block, 1, packed), lambda i: (i, 0, 0)),
+            pl.BlockSpec((block, 4, packed), lambda i: (i, 0, 0)),
         ],
         out_specs=pl.BlockSpec((channels, block, packed), lambda i: (0, i, 0)),
         out_shape=jax.ShapeDtypeStruct((channels, pair_count, packed), jnp.bfloat16),
@@ -176,7 +176,8 @@
     )
     weighted = weighted.reshape(pair_count, lat_count, 4 * channels).astype(jnp.bfloat16)
     weighted = jnp.swapaxes(weighted, 1, 2)
-    partial = legendre_direct(legendre, weighted, codes, block)
+    picks = (codes == jnp.arange(4, dtype=jnp.int32)[None, :, None]).astype(jnp.float32)
+    partial = legendre_direct(legendre, weighted, picks, block)
     return lax.psum_scatter(partial, "lev", scatter_dimension=0, tiled=True)
 
 

time: 366 us -> 367 us (level)
  blocking collectives: 37.2 us -> 0 us
  waiting for transfers between devices: 139 us -> 173 us
    all_to_all x1 -> x0, blocking collectives: 37.2 us -> none  [local(): lax.all_to_all(answered, 'lat', split_axis=0, concat_axis=0, tiled=True)]
    all_to_all x0 -> x1, waiting for transfers between devices: none -> 32.7 us  [local(): lax.all_to_all(answered, 'lat', split_axis=0, concat_axis=0, tiled=True)]
    add x1, other arithmetic: 6.98 us -> 0.3 us  [slot_codes(): return (2 * in_second + degree % 2).reshape(pair_count, 1, packed)]
    another operation x2 -> x3, other arithmetic: 5.12 us -> 11.4 us
  transfers between devices with their start and end apart: 3 -> 4, of which waited for: 3 -> 4; matrix products, arithmetic and copies ran while one was open for 14% -> 14% of each run, Pallas kernels for 0% -> 0%
where the time goes in v12:
time: 367 us
  waiting for transfers between devices  173 us (47%)
  other arithmetic  54.6 us (15%)
  local copies, waits for them, and re-layouts  54.4 us (15%)
  Pallas kernels  35.8 us (10%)
  matrix products  24.5 us (7%)
  between operations  13.6 us (4%)
  starting transfers between devices  10.8 us (3%)
    reduce_scatter x1, waiting for transfers between devices, local(): return lax.psum_scatter(partial, 'lev', scatter_dimension=0, tiled=True)  92.7 us
    all_to_all x1, waiting for transfers between devices, local(): lax.all_to_all(fourier, 'lat', split_axis=1, concat_axis=0, tiled=True)  34.5 us
    all_to_all x1, waiting for transfers between devices, local(): lax.all_to_all(answered, 'lat', split_axis=0, concat_axis=0, tiled=True)  32.7 us
    concatenate x4, local copies, waits for them, and re-layouts, fourier_work(): jnp.concatenate([real_out.reshape(lats, half_channels, waves), imag_out.r...  23.8 us
    pallas_call x1, Pallas kernels, legendre_inverse(): pl.pallas_call(inverse_kernel, grid=(pair_count // block,), in_specs=[pl....  18.9 us
    concatenate x1, other arithmetic, wave_tables(): table = lax.optimization_barrier(jnp.concatenate([cosines, sines], axis=0))  18.5 us
    pallas_call x1, Pallas kernels, legendre_direct(): pl.pallas_call(direct_kernel, grid=(pair_count // block,), in_specs=[pl.B...  17 us
    dot_general x1, matrix products, fourier_work(): jnp.dot(lhs, table, preferred_element_type=jnp.float32)  13.6 us
  transfers between devices with their start and end apart: 4, of which 4 were waited for; matrix products, arithmetic and copies ran while one was open for 14% of the time, Pallas kernels for 0%

profile of v12, /device:TPU:2, one launch (start us, length us, event | category | flops | bytes accessed | tf_op | source)
XLA Modules:
  0.0 366.6 jit_solution(12704581484001984508)
XLA Ops:
  6.5 0.0 all-gather.2.cloned.1.call-start
  6.5 0.7 all-gather.2.cloned.1.call-update
  7.3 0.2 copy.69
  7.5 0.2 mul.251
  7.7 1.3 fusion.35
  9.0 1.7 fusion.28
  10.8 12.6 %subtract_convert_fusion = (bf16[1280,80,64]{0,2,1:T(8,128)(2,1)}, bf16[1280,80,64]{0,2,1:T(8,128)(2,1)}) fusion(f32[1280,64]{0,1:T(8,128)S(1)} %get-tuple-element.22, f32[1280,80]{0,1:T(8,128)S(1)} %get-tuple-element.20, f32[1280,64]{0,1:T(8,128)S(1)} %get-tuple-element.21, f32[1280,80]{0,1:T(8,128)S(1)} %get-tuple-element.19), kind=kLoop, calls=%fused_computation.2 | loop fusion | flops 52428800 | bytes 27688960 | tf_op jit(solution)/shard_map/convert_element_type | solution.py:28
  23.3 18.5 %pad_maximum_fusion = bf16[2560,5120]{0,1:T(8,128)(2,1)} fusion(bf16[1280,5120]{0,1:T(8,128)(2,1)} %bitcast.46, bf16[1280,5120]{0,1:T(8,128)(2,1)} %bitcast.45), kind=kLoop, calls=%fused_computation | loop fusion | flops 52428800 | bytes 52428800 | tf_op jit(solution)/shard_map/concatenate | solution.py:30
  41.8 4.8 %fusion.16 = (bf16[80,1,1281]{2,1,0:T(2,128)(2,1)S(1)}, bf16[80,1,1281]{2,1,0:T(2,128)(2,1)S(1)}) fusion(s32[80]{0:T(128)S(1)} %add_subtract_fusion), kind=kLoop, calls=%fused_computation.51 | loop fusion | flops 3791760 | bytes 410240 | tf_op jit(solution)/shard_map/convert.6
  46.6 6.3 %fusion.17 = (bf16[80,1,1281]{2,1,0:T(2,128)(2,1)S(1)}, bf16[80,1,1281]{2,1,0:T(2,128)(2,1)S(1)}) fusion(s32[80]{0:T(128)S(1)} %add_subtract_fusion), kind=kLoop, calls=%fused_computation.52 | loop fusion | flops 4406640 | bytes 410240 | tf_op jit(solution)/shard_map/convert.8
  52.9 3.1 pad_maximum_fusion.3.factor_ref
  56.0 12.2 %all-gather.2.cloned.1.call-done.spec_ref = bf16[32,80,1281]{2,1,0:T(8,128)(2,1)} async-done(((bf16[1,80,1281]{2,1,0:T(8,128)(2,1)}), bf16[32,80,1281]{2,1,0:T(8,128)(2,1)}) %all-gather.2.cloned.1.call-update) | async-done | bytes 6558736 | tf_op jit(solution)/shard_map/all_gather | solution.py:153
  68.2 18.9 %shard_map.46 = bf16[80,80,64]{2,1,0:T(8,128)(2,1)} custom-call(bf16[80,40,1281]{2,1,0:T(8,128)(2,1)} %leg_ref.3, bf16[32,80,1281]{2,1,0:T(8,128)(2,1)} %all-gather.2.cloned.1.call-done.spec_ref, bf16[80,4,1281]{2,1,0:T(4,128)(2,1)} %pad_maximum_fusion.3.factor_ref), custom_call_target="tpu_custom_call" | custom-call | tf_op jit(solution)/shard_map/pallas_call | solution.py:114
  87.0 2.8 copy.82
  89.9 0.0 copy-start.2
  89.9 7.1 %all-to-all-start = ((bf16[80,80,2,32]{0,3,2,1:T(8,128)(2,1)}), bf16[80,80,2,32]{0,3,2,1:T(8,128)(2,1)S(1)}, u32[]{:S(2)}, u32[]{:S(2)}) async-start(bf16[80,80,2,32]{0,3,2,1:T(8,128)(2,1)} %bitcast.3), calls=%async_computation | async-start | bytes 2621440 | tf_op jit(solution)/shard_map/all_to_all | solution.py:165
  97.0 0.0 copy-done.2
  97.0 0.1 squeeze_reshape.3
  97.1 0.1 dynamic_slice.3
  97.2 0.1 fusion.38
  97.3 34.5 %all-to-all-done = bf16[80,80,2,32]{0,3,2,1:T(8,128)(2,1)S(1)} async-done(((bf16[80,80,2,32]{0,3,2,1:T(8,128)(2,1)}), bf16[80,80,2,32]{0,3,2,1:T(8,128)(2,1)S(1)}, u32[]{:S(2)}, u32[]{:S(2)}) %all-to-all-start) | async-done | bytes 819232 | tf_op jit(solution)/shard_map/all_to_all | solution.py:165
  131.8 1.0 copy.72
  132.8 1.0 all_to_all.19
  133.8 1.0 multiply_bitcast_fusion
  134.8 5.8 %copy.73 = bf16[10,32,640,2]{1,3,2,0:T(2,128)(2,1)S(1)} copy(bf16[10,32,640,2]{2,1,3,0:T(8,128)(2,1)} %multiply_bitcast_fusion) | data formatting | bytes 1638400 | tf_op jit(solution)/shard_map/transpose | solution.py:42
  140.5 3.9 %fusion.39 = (bf16[10,16,1280]{1,2,0:T(8,128)(2,1)}, bf16[10,16,1280]{1,2,0:T(8,128)(2,1)}) fusion(bf16[10,32,1280]{1,2,0:T(8,128)(2,1)S(1)} %bitcast.47), kind=kLoop, calls=%fused_computation.83 | loop fusion | bytes 1638400 | tf_op jit(solution)/shard_map/slice | solution.py:43
  144.4 0.0 copy-start
  144.4 4.0 %copy.83 = bf16[10,16,1280]{2,1,0:T(8,128)(2,1)} copy(bf16[10,16,1280]{1,2,0:T(8,128)(2,1)} %get-tuple-element.12) | data formatting | bytes 819200
  148.4 1.8 neg.6
  150.3 0.0 copy-done
  150.3 2.6 copy.74
  152.9 13.6 %convolution_multiply_fusion = f32[160,5120]{1,0:T(8,128)S(1)} fusion(bf16[2560,5120]{0,1:T(8,128)(2,1)} %pad_maximum_fusion, bf16[160,1280]{1,0:T(8,128)(2,1)} %bitcast.54, bf16[160,1280]{1,0:T(8,128)(2,1)} %bitcast.53), kind=kOutput, calls=%fused_computation.3 | convolution fusion | flops 4196761600 | bytes 30310400 | tf_op jit(solution)/shard_map/dot_general | solution.py:46
  166.6 0.4 multiply_convert_fusion.1
  166.9 0.1 pad_maximum_fusion.1
  167.1 10.8 %fusion.40 = f32[160,2560]{1,0:T(8,128)S(1)} fusion(bf16[160,5120]{1,0:T(8,128)(2,1)S(1)} %bitcast.52, bf16[2560,5120]{0,1:T(8,128)(2,1)} %pad_maximum_fusion), kind=kOutput, calls=%fused_computation.84 | convolution fusion | flops 4194304000 | bytes 29491200 | tf_op jit(solution)/shard_map/dot_general | solution.py:56
  177.9 0.1 slice_multiply_fusion.1
  178.0 0.4 copy.76
  178.4 5.9 %concatenate.30 = f32[10,16,640,2]{1,0,3,2:T(8,128)} reshape(f32[160,1280]{0,1:T(8,128)S(1)} %copy.76) | data formatting | bytes 1638400 | tf_op jit(solution)/shard_map/concatenate | solution.py:64
  184.4 6.0 %copy.78 = f32[10,16,640,2]{2,1,3,0:T(8,128)S(1)} copy(f32[10,16,640,2]{1,0,3,2:T(8,128)} %concatenate.30) | data formatting | bytes 1638400 | tf_op jit(solution)/shard_map/concatenate | solution.py:64
  190.4 0.4 copy.77
  190.8 5.9 %concatenate.31 = f32[10,16,640,2]{1,0,3,2:T(8,128)} reshape(f32[160,1280]{0,1:T(8,128)S(1)} %copy.77) | data formatting | bytes 1638400 | tf_op jit(solution)/shard_map/concatenate | solution.py:64
  196.7 6.0 %copy.79 = f32[10,16,640,2]{2,1,3,0:T(8,128)S(1)} copy(f32[10,16,640,2]{1,0,3,2:T(8,128)} %concatenate.31) | data formatting | bytes 1638400 | tf_op jit(solution)/shard_map/concatenate | solution.py:64
  202.7 0.2 fusion.2
  202.8 1.6 reshape.577
  204.5 1.4 copy.80
  205.9 3.6 all-to-all-start.1
  209.5 0.0 copy-start.1
  209.5 0.0 reduce-scatter.2.cloned.1.call-start
  209.5 0.3 fusion.15
  209.9 1.6 fusion.code_ref
  211.5 32.7 %all-to-all-done.1 = bf16[8,80,10,2,32]{1,4,3,2,0:T(8,128)(2,1)S(1)} async-done(((bf16[8,80,10,2,32]{1,4,3,2,0:T(8,128)(2,1)}), bf16[8,80,10,2,32]{1,4,3,2,0:T(8,128)(2,1)S(1)}, u32[]{:S(2)}, u32[]{:S(2)}) %all-to-all-start.1) | async-done | bytes 819232 | tf_op jit(solution)/shard_map/all_to_all | solution.py:169
  244.2 0.0 copy-done.1
  244.2 0.4 fusion.11
  244.6 0.3 pad_maximum_fusion.2
  244.9 5.1 %copy.81 = bf16[80,40,2,2,32]{1,4,3,2,0:T(8,128)(2,1)} copy(bf16[80,40,2,2,32]{0,4,2,1,3:T(8,128)(2,1)S(1)} %pad_maximum_fusion.2) | data formatting | bytes 1638400 | tf_op jit(solution)/shard_map/stack | solution.py:174
  250.0 17.0 %shard_map.47 = bf16[32,80,1281]{2,1,0:T(8,128)(2,1)} custom-call(bf16[80,40,1281]{2,1,0:T(8,128)(2,1)} %leg_ref.3, bf16[80,128,40]{2,1,0:T(8,128)(2,1)} %bitcast.48, f32[80,4,1281]{2,1,0:T(4,128)} %fusion.code_ref), custom_call_target="tpu_custom_call" | custom-call | tf_op jit(solution)/shard_map/pallas_call | solution.py:131
  267.0 0.0 reduce-scatter.2.cloned.1.call-update
  267.0 92.7 %reduce-scatter.2.cloned.1.call-done = bf16[1,80,1281]{2,1,0:T(8,128)(2,1)} async-done(((bf16[32,80,1281]{2,1,0:T(8,128)(2,1)}), bf16[1,80,1281]{2,1,0:T(8,128)(2,1)}) %reduce-scatter.2.cloned.1.call-update) | async-done | bytes 204976 | tf_op jit(solution)/shard_map/reduce_scatter | solution.py:181
  (5 shorter events, 0.0 us)
Async XLA Ops:
  6.5 61.6 %all-gather.2.cloned.1.call-start = ((), (), s32[]{:S(2)}) async-start(), calls=%async_computation.3 | async-start | bytes 7434240 | tf_op jit(solution)/shard_map/all_gather | solution.py:153
  89.9 7.2 %copy-start.2 = (s32[2,40]{1,0:T(2,128)S(1)}, s32[2,40]{1,0:T(2,128)}, u32[]{:S(2)}) copy-start(s32[2,40]{1,0:T(2,128)} %param.7) | copy-start | bytes 964
  89.9 41.9 %all-to-all-start = ((bf16[80,80,2,32]{0,3,2,1:T(8,128)(2,1)}), bf16[80,80,2,32]{0,3,2,1:T(8,128)(2,1)S(1)}, u32[]{:S(2)}, u32[]{:S(2)}) async-start(bf16[80,80,2,32]{0,3,2,1:T(8,128)(2,1)} %bitcast.3), calls=%async_computation | async-start | bytes 2621440 | tf_op jit(solution)/shard_map/all_to_all | solution.py:165
  144.4 5.9 %copy-start = (bf16[10,16,1280]{1,2,0:T(8,128)(2,1)S(1)}, bf16[10,16,1280]{1,2,0:T(8,128)(2,1)}, u32[]{:S(2)}) copy-start(bf16[10,16,1280]{1,2,0:T(8,128)(2,1)} %get-tuple-element.11) | copy-start | bytes 1228804
  205.9 38.3 %all-to-all-start.1 = ((bf16[8,80,10,2,32]{1,4,3,2,0:T(8,128)(2,1)}), bf16[8,80,10,2,32]{1,4,3,2,0:T(8,128)(2,1)S(1)}, u32[]{:S(2)}, u32[]{:S(2)}) async-start(bf16[8,80,10,2,32]{1,4,3,2,0:T(8,128)(2,1)} %copy.80), calls=%async_computation.1 | async-start | bytes 2621440 | tf_op jit(solution)/shard_map/all_to_all | solution.py:169
  209.5 34.7 %copy-start.1 = (f32[40]{0:T(128)S(1)}, f32[40]{0:T(128)}, u32[]{:S(2)}) copy-start(f32[40]{0:T(128)} %param.6) | copy-start | bytes 484
  209.5 150.2 %reduce-scatter.2.cloned.1.call-start = ((), (), s32[]{:S(2)}) async-start(), calls=%async_computation.4 | async-start | bytes 7434240 | tf_op jit(solution)/shard_map/reduce_scatter | solution.py:181
Sparse Core Ops, SparseCore 0:
  10.0 58.1 all-gather.1
  267.1 92.5 reduce-scatter.1
